TPU v7x, 32 devices: a whole 2x2x4 slice. The times are simulated.
32 devices in a mesh: space: 8 (over z, x), batch: 4 (over y, core).
Axes of the slice: x: 2, y: 2, z: 4, core: 2. Of those that a mesh axis runs over, the one named last changes fastest.
Arguments:
- owner: int32 [8, 2048, 1], P('batch', 'space'), may hold values from 0 to 7; in each aligned block of 256 rows (0 to 255, 256 to 511, ..., all dimensions but the last counted through in order) at most 128 rows name the same one
- offset: int32 [8, 2048], P('batch', 'space'), may hold values from 0 to 2047
- profile: float32 [8, 2048, 128], P('batch', 'space'), may hold values from -6 to 6
- diffusion: float32 [32, 512, 128], P('space'), may hold values from 0.04 to 0.16
- velocity: float32 [32, 512, 128], P('space'), may hold values from 0.05 to 0.3
Outputs:
- final_fields: float32 [8, 32, 512, 128], P('batch', 'space')
- gram: float32 [8, 8], replicated
Inputs may be any that keep to these rules, and one draw needn't show every extreme that they name: In each aligned block of 256 rows of owner (one field's rows on one index of space), no value is named by more than 128 rows, a bound that some block reaches.
All inputs are finite; a program needn't handle non-finite values.
Results may differ from a plain program's by a relative error of at most 0.0042.
Values may be sent and summed in bfloat16 or wider, within the bound.
No kernel may reach another device: no remote copies, remote signals or barrier semaphores. Data moves between devices by JAX's collectives and lax.ppermute only.
A program may use at most 320 MiB of HBM per device.

v0:
```python
import math

import jax
import jax.numpy as jnp
from jax import lax
from jax.sharding import PartitionSpec as P

STEPS = 2
ACT = 4
SENS = 4


def padded_2(value, sides, width):
    for axis, dim in sides:
        peers, length = (lax.axis_size(axis), value.shape[dim])
        up = [(i, (i + 1) % peers) for i in range(peers)]
        down = [(j, i) for i, j in up]
        last = lax.slice_in_dim(value, length - width, length, axis=dim)
        initial = lax.slice_in_dim(value, 0, width, axis=dim)
        before = lax.ppermute(last, axis, up)
        after = lax.ppermute(initial, axis, down)
        value = jnp.concatenate([before, value, after], axis=dim)
    return value


def prepare(coef, adjoint):
    diff_c = coef[0]
    vel_c = coef[1]
    pre_lap = jnp.where(adjoint, diff_c, 1.0)
    post_lap = jnp.where(adjoint, 1.0, diff_c)
    pre_dx = jnp.where(adjoint, vel_c, 1.0)
    post_dx = jnp.where(adjoint, 1.0, -vel_c)
    return (pre_lap, post_lap, pre_dx, post_dx)


def advance(extended, weights):
    pre_lap, post_lap, pre_dx, post_dx = weights
    lifted = pre_lap * extended
    moved = pre_dx * extended
    middle = lifted[:, 1:-1]
    padded = jnp.pad(middle, ((0, 0), (0, 0), (0, 0), (1, 1)))
    total = lifted[:, 2:] + lifted[:, :-2]
    total = total + jnp.roll(middle, -1, 2) + jnp.roll(middle, 1, 2)
    total = total + padded[..., 2:] + padded[..., :-2]
    lapl = total - 6.0 * middle
    slope = 0.5 * (moved[:, 2:] - moved[:, :-2])
    return extended[:, 1:-1] + post_lap[1:-1] * lapl + post_dx[1:-1] * slope


def body(owner, offset, profile, diffusion, velocity):
    count = lax.axis_size("space")
    fields_dev, rows_dev = offset.shape
    planes, span, depth = diffusion.shape
    cap = 4 * rows_dev // count
    target = owner[..., 0]
    earlier = jnp.tril(jnp.ones((rows_dev, rows_dev), jnp.bool_), -1)
    same = target[:, :, None] == target[:, None, :]
    rank = jnp.sum(jnp.logical_and(same, earlier[None]), axis=2)
    slot = target * cap + rank

    def place(where_to, columns, values):
        send_cols = jnp.zeros((count * cap,), jnp.int32).at[where_to].set(columns)
        send_vals = jnp.zeros((count * cap, depth), jnp.float32).at[where_to].set(values)
        return (send_cols, send_vals)

    send_cols, send_vals = jax.vmap(place)(slot, offset, profile)
    send_cols = send_cols.reshape(fields_dev, count, cap)
    send_vals = send_vals.reshape(fields_dev, count, cap, depth)
    got_cols, got_vals = (
        lax.all_to_all(send_cols, "space", split_axis=1, concat_axis=1, tiled=True),
        lax.all_to_all(send_vals, "space", split_axis=1, concat_axis=1, tiled=True),
    )

    def deposit(columns, values):
        return (
            jnp.zeros((planes * span, depth), jnp.float32)
            .at[columns.reshape(-1)]
            .add(values.reshape(-1, depth))
        )

    state = jax.vmap(deposit)(got_cols, got_vals).reshape(fields_dev, planes, span, depth)
    adjoint = lax.axis_index("batch") >= lax.axis_size("batch") // 2
    coef = jnp.stack([diffusion, velocity])
    pieces = []

    def record(current):
        snap = current.astype(jnp.bfloat16).reshape(fields_dev, -1)
        pieces.append(lax.all_to_all(snap, "batch", split_axis=1, concat_axis=0, tiled=True))

    rim = padded_2(coef, (("space", 1),), 1)
    weights = prepare(rim, adjoint)
    for step in range(STEPS):
        extended = padded_2(state, (("space", 1),), 1)
        state = advance(extended, weights)
        record(state)
    mixed = jnp.stack(pieces)
    actuated = mixed[:, :ACT].reshape(STEPS * ACT, -1)
    sensed = mixed[:, ACT:].reshape(STEPS * SENS, -1)
    partial_gram = lax.dot_general(
        sensed, actuated, (((1,), (1,)), ((), ())), preferred_element_type=jnp.float32
    )
    scale = 4.0 / math.sqrt(planes * count * span * depth)
    gram = lax.psum(partial_gram, ("space", "batch")) * scale
    return (state, gram)


def solution(mesh):
    in_specs = (
        P("batch", "space", None),
        P("batch", "space"),
        P("batch", "space", None),
        P("space", None, None),
        P("space", None, None),
    )
    out_specs = (P("batch", "space", None, None), P())
    return jax.shard_map(body, mesh=mesh, in_specs=in_specs, out_specs=out_specs, check_vma=False)
```

profile of v0, /device:TPU:0, one launch (start us, length us, event | category | flops | bytes accessed | tf_op | source)
XLA Modules:
  0.0 294.9 jit_solution(17023892134600744317)
XLA Ops:
  3.7 65.0 %scatter_fusion = s32[2,1024]{1,0:T(2,128)} fusion(s32[2,1024]{1,0:T(2,128)} %broadcast.64, s32[512]{0:T(512)S(1)} %bitcast.45, s32[512]{0:T(512)S(1)} %bitcast.59), kind=kCustom, calls=%fused_computation | custom fusion | bytes 10240 | tf_op jit(solution)/shard_map/vmap()/scatter | solution.py:62
  68.7 7.1 %all-to-all-start = ((s32[2,8,128]{2,0,1:T(2,128)}), s32[2,8,128]{2,0,1:T(2,128)S(1)}, u32[]{:S(2)}, u32[]{:S(2)}) async-start(s32[2,8,128]{2,0,1:T(2,128)} %bitcast.1), calls=%async_computation | async-start | bytes 16384 | tf_op jit(solution)/shard_map/all_to_all | solution.py:70
  75.8 24.6 %scatter_fusion.1 = f32[2,1024,128]{2,1,0:T(8,128)S(1)} fusion(f32[2,1024,128]{2,1,0:T(8,128)S(1)} %broadcast_in_dim.15, s32[512]{0:T(512)S(1)} %bitcast.46, f32[512,128]{1,0:T(8,128)S(1)} %bitcast.57), kind=kCustom, calls=%fused_computation.1 | custom fusion | bytes 790528 | tf_op jit(solution)/shard_map/vmap()/scatter | solution.py:63
  101.5 6.0 %all-to-all-start.1 = ((f32[2,8,128,128]{3,2,0,1:T(8,128)}), f32[2,8,128,128]{3,2,0,1:T(8,128)S(1)}, u32[]{:S(2)}, u32[]{:S(2)}) async-start(f32[2,8,128,128]{3,2,0,1:T(8,128)} %copy.19), calls=%async_computation.1 | async-start | bytes 2097152 | tf_op jit(solution)/shard_map/all_to_all | solution.py:71
  110.7 2.7 collective-permute-start.1
  113.6 27.4 %collective-permute-done = f32[2,1,512,128]{3,2,1,0:T(8,128)} collective-permute-done((f32[2,1,512,128]{3,2,1,0:T(8,128)}, f32[2,1,512,128]{3,2,1,0:T(8,128)}, u32[]{:S(2)}, u32[]{:S(2)}) %collective-permute-start) | collective-permute-done | bytes 524320 | tf_op jit(solution)/shard_map/ppermute | solution.py:20
  141.0 2.7 collective-permute-done.1
  143.7 3.1 %pad_maximum_fusion = f32[2,6,512,128]{3,2,1,0:T(8,128)} fusion(f32[2,1,512,128]{3,2,1,0:T(8,128)} %collective-permute-done.1, f32[1,4,512,128]{3,2,1,0:T(8,128)S(1)} %bitcast.52, f32[1,4,512,128]{3,2,1,0:T(8,128)S(1)} %bitcast.54, f32[2,1,512,128]{3,2,1,0:T(8,128)} %collective-permute-done), kind=kLoop, calls=%fused_computation.7 | loop fusion | flops 2359296 | bytes 6291456 | tf_op jit(solution)/shard_map/concatenate | solution.py:22
  147.8 14.8 %scatter_custom_fusion.2 = f32[4096,128]{1,0:T(8,128)S(1)} fusion(s32[2048]{0:T(1024)S(1)} %bitcast.60, f32[2048,128]{1,0:T(8,128)} %bitcast.56, f32[]{:T(128)} %constant.12.clone.1), kind=kCustom, calls=%fused_computation.44 | custom fusion | flops 262144 | bytes 2097664
  162.8 4.7 %collective-permute-start.3 = (f32[2,1,512,128]{3,2,1,0:T(8,128)S(1)}, f32[2,1,512,128]{3,2,1,0:T(8,128)S(1)}, u32[]{:S(2)}, u32[]{:S(2)}) collective-permute-start(f32[2,1,512,128]{3,2,1,0:T(8,128)S(1)} %get-tuple-element.27), channel_id=1, source_target_pairs={{4,0},{8,4},{12,8},{16,12},{20,16},{24,20},{28,24},{0,28},{5,1},{9... | collective-permute-start | bytes 1572872 | tf_op jit(solution)/shard_map/ppermute | solution.py:21
  170.3 14.1 %collective-permute-done.2 = f32[2,1,512,128]{3,2,1,0:T(8,128)S(1)} collective-permute-done((f32[2,1,512,128]{3,2,1,0:T(8,128)S(1)}, f32[2,1,512,128]{3,2,1,0:T(8,128)S(1)}, u32[]{:S(2)}, u32[]{:S(2)}) %collective-permute-start.2) | collective-permute-done | bytes 524320 | tf_op jit(solution)/shard_map/ppermute | solution.py:20
  184.4 3.0 %collective-permute-done.3 = f32[2,1,512,128]{3,2,1,0:T(8,128)S(1)} collective-permute-done((f32[2,1,512,128]{3,2,1,0:T(8,128)S(1)}, f32[2,1,512,128]{3,2,1,0:T(8,128)S(1)}, u32[]{:S(2)}, u32[]{:S(2)}) %collective-permute-start.3) | collective-permute-done | bytes 524320 | tf_op jit(solution)/shard_map/ppermute | solution.py:21
  189.9 2.8 fusion.33
  193.8 4.7 %collective-permute-start.5 = (f32[2,1,512,128]{3,2,1,0:T(8,128)}, f32[2,1,512,128]{3,2,1,0:T(8,128)}, u32[]{:S(2)}, u32[]{:S(2)}) collective-permute-start(f32[2,1,512,128]{3,2,1,0:T(8,128)} %get-tuple-element.25), channel_id=1, source_target_pairs={{4,0},{8,4},{12,8},{16,12},{20,16},{24,20},{28,24},{0,28},{5,1},{9... | collective-permute-start | bytes 1572872 | tf_op jit(solution)/shard_map/ppermute | solution.py:21
  200.7 3.3 %copy.21 = bf16[2,4,65536]{2,0,1:T(2,128)(2,1)} copy(bf16[2,4,65536]{2,1,0:T(4,128)(2,1)} %all_to_all.32) | data formatting | bytes 2097152 | tf_op jit(solution)/shard_map/all_to_all | solution.py:88
  204.0 4.5 %all-to-all-start.2 = ((bf16[2,4,65536]{2,0,1:T(2,128)(2,1)}), bf16[2,4,65536]{2,0,1:T(2,128)(2,1)}, u32[]{:S(2)}, u32[]{:S(2)}) async-start(bf16[2,4,65536]{2,0,1:T(2,128)(2,1)} %copy.21), calls=%async_computation.2 | async-start | bytes 2097152 | tf_op jit(solution)/shard_map/all_to_all | solution.py:88
  208.5 6.6 %collective-permute-done.4 = f32[2,1,512,128]{3,2,1,0:T(8,128)} collective-permute-done((f32[2,1,512,128]{3,2,1,0:T(8,128)}, f32[2,1,512,128]{3,2,1,0:T(8,128)}, u32[]{:S(2)}, u32[]{:S(2)}) %collective-permute-start.4) | collective-permute-done | bytes 524320 | tf_op jit(solution)/shard_map/ppermute | solution.py:20
  215.1 4.9 %collective-permute-done.5 = f32[2,1,512,128]{3,2,1,0:T(8,128)} collective-permute-done((f32[2,1,512,128]{3,2,1,0:T(8,128)}, f32[2,1,512,128]{3,2,1,0:T(8,128)}, u32[]{:S(2)}, u32[]{:S(2)}) %collective-permute-start.5) | collective-permute-done | bytes 524320 | tf_op jit(solution)/shard_map/ppermute | solution.py:21
  220.0 2.9 fusion.1
  224.5 3.2 %fusion.31 = (bf16[2,4,512,128]{3,2,1,0:T(8,128)(2,1)}, f32[2,4,512,128]{3,2,1,0:T(8,128)}) fusion(f32[4,512,128]{2,1,0:T(8,128)S(1)} %get-tuple-element.30, f32[2,6,512,128]{3,2,1,0:T(8,128)S(1)} %get-tuple-element.11, f32[2,4,512,128]{3,2,1,0:T(8,128)S(1)} %get-tuple-element.5, f32[2,4,512,128]{3,2,1,0:T(8,128)S(1)} %slice.182, ...), kind=kLoop, calls=%fused_computation.69 | loop fusion | flops 7864320 | bytes 22020096 | tf_op jit(solution)/shard_map/convert_element_type | solution.py:87
  231.2 3.5 %all-to-all-start.3 = ((bf16[2,4,65536]{2,0,1:T(2,128)(2,1)}), bf16[2,4,65536]{2,0,1:T(2,128)(2,1)S(1)}, u32[]{:S(2)}, u32[]{:S(2)}) async-start(bf16[2,4,65536]{2,0,1:T(2,128)(2,1)} %copy.22), calls=%async_computation.3 | async-start | bytes 2097152 | tf_op jit(solution)/shard_map/all_to_all | solution.py:88
  234.7 2.6 stack.21
  238.6 10.5 %all-to-all-done.3 = bf16[2,4,65536]{2,0,1:T(2,128)(2,1)S(1)} async-done(((bf16[2,4,65536]{2,0,1:T(2,128)(2,1)}), bf16[2,4,65536]{2,0,1:T(2,128)(2,1)S(1)}, u32[]{:S(2)}, u32[]{:S(2)}) %all-to-all-start.3) | async-done | bytes 1048608 | tf_op jit(solution)/shard_map/all_to_all | solution.py:88
  256.0 38.3 %psum.7 = f32[8,8]{1,0:T(8,128)S(1)} all-reduce(f32[8,8]{1,0:T(8,128)S(1)} %fusion.43), channel_id=1, replica_groups=mesh['space'=8,'batch'=4] {'space','batch'}, use_global_device_ids=true, to_apply=%region_4.5 | all-reduce | flops 64 | bytes 512 | tf_op jit(solution)/shard_map/psum | solution.py:103
  (68 shorter events, 31.0 us)
Async XLA Ops:
  3.7 72.1 %copy-start.8 = (f32[2,256,128]{2,1,0:T(8,128)S(1)}, f32[2,256,128]{2,1,0:T(8,128)}, u32[]{:S(2)}) copy-start(f32[2,256,128]{2,1,0:T(8,128)} %param.7) | copy-start | bytes 786436
  68.7 32.9 %all-to-all-start = ((s32[2,8,128]{2,0,1:T(2,128)}), s32[2,8,128]{2,0,1:T(2,128)S(1)}, u32[]{:S(2)}, u32[]{:S(2)}) async-start(s32[2,8,128]{2,0,1:T(2,128)} %bitcast.1), calls=%async_computation | async-start | bytes 16384 | tf_op jit(solution)/shard_map/all_to_all | solution.py:70
  100.5 7.1 %copy-start.6 = (f32[4,512,128]{2,1,0:T(8,128)S(1)}, f32[4,512,128]{2,1,0:T(8,128)}, u32[]{:S(2)}) copy-start(f32[4,512,128]{2,1,0:T(8,128)} %param.9) | copy-start | bytes 3145732
  100.5 7.1 %copy-start.7 = (f32[4,512,128]{2,1,0:T(8,128)S(1)}, f32[4,512,128]{2,1,0:T(8,128)}, u32[]{:S(2)}) copy-start(f32[4,512,128]{2,1,0:T(8,128)} %param.8) | copy-start | bytes 3145732
  101.5 45.2 %all-to-all-start.1 = ((f32[2,8,128,128]{3,2,0,1:T(8,128)}), f32[2,8,128,128]{3,2,0,1:T(8,128)S(1)}, u32[]{:S(2)}, u32[]{:S(2)}) async-start(f32[2,8,128,128]{3,2,0,1:T(8,128)} %copy.19), calls=%async_computation.1 | async-start | bytes 2097152 | tf_op jit(solution)/shard_map/all_to_all | solution.py:71
  107.6 5.8 %copy-start.9 = (s32[2]{0:T(128)S(1)}, s32[2]{0:T(128)}, u32[]{:S(2)}) copy-start(s32[2]{0:T(128)} %constant.43) | copy-start | bytes 28
  107.6 5.9 %copy-start.10 = (s32[2]{0:T(128)S(1)}, s32[2]{0:T(128)}, u32[]{:S(2)}) copy-start(s32[2]{0:T(128)} %constant.46) | copy-start | bytes 28
  108.7 32.4 %collective-permute-start = (f32[2,1,512,128]{3,2,1,0:T(8,128)}, f32[2,1,512,128]{3,2,1,0:T(8,128)}, u32[]{:S(2)}, u32[]{:S(2)}) collective-permute-start(f32[2,1,512,128]{3,2,1,0:T(8,128)} %get-tuple-element.28), channel_id=1, source_target_pairs={{0,4},{4,8},{8,12},{12,16},{16,20},{20,24},{24,28},{28,0},{1,5},{5... | collective-permute-start | bytes 1572872 | tf_op jit(solution)/shard_map/ppermute | solution.py:20
  110.7 33.0 %collective-permute-start.1 = (f32[2,1,512,128]{3,2,1,0:T(8,128)}, f32[2,1,512,128]{3,2,1,0:T(8,128)}, u32[]{:S(2)}, u32[]{:S(2)}) collective-permute-start(f32[2,1,512,128]{3,2,1,0:T(8,128)} %get-tuple-element.29), channel_id=1, source_target_pairs={{4,0},{8,4},{12,8},{16,12},{20,16},{24,20},{28,24},{0,28},{5,1},{9... | collective-permute-start | bytes 1572872 | tf_op jit(solution)/shard_map/ppermute | solution.py:21
  162.6 24.8 %copy-start = (f32[4096,128]{1,0:T(8,128)}, f32[4096,128]{1,0:T(8,128)S(1)}, u32[]{:S(2)}) copy-start(f32[4096,128]{1,0:T(8,128)S(1)} %scatter_custom_fusion.2) | copy-start | bytes 6291460
  162.7 21.7 %collective-permute-start.2 = (f32[2,1,512,128]{3,2,1,0:T(8,128)S(1)}, f32[2,1,512,128]{3,2,1,0:T(8,128)S(1)}, u32[]{:S(2)}, u32[]{:S(2)}) collective-permute-start(f32[2,1,512,128]{3,2,1,0:T(8,128)S(1)} %get-tuple-element.26), channel_id=1, source_target_pairs={{0,4},{4,8},{8,12},{12,16},{16,20},{20,24},{24,28},{28,0},{1,5},{5... | collective-permute-start | bytes 1572872 | tf_op jit(solution)/shard_map/ppermute | solution.py:20
  162.8 24.6 %collective-permute-start.3 = (f32[2,1,512,128]{3,2,1,0:T(8,128)S(1)}, f32[2,1,512,128]{3,2,1,0:T(8,128)S(1)}, u32[]{:S(2)}, u32[]{:S(2)}) collective-permute-start(f32[2,1,512,128]{3,2,1,0:T(8,128)S(1)} %get-tuple-element.27), channel_id=1, source_target_pairs={{4,0},{8,4},{12,8},{16,12},{20,16},{24,20},{28,24},{0,28},{5,1},{9... | collective-permute-start | bytes 1572872 | tf_op jit(solution)/shard_map/ppermute | solution.py:21
  170.1 17.4 %copy-start.2 = (f32[6,512,128]{2,1,0:T(8,128)}, f32[6,512,128]{2,1,0:T(8,128)S(1)}, u32[]{:S(2)}) copy-start(f32[6,512,128]{2,1,0:T(8,128)S(1)} %get-tuple-element.13) | copy-start | bytes 4718596
  170.1 17.3 %copy-start.3 = (f32[6,512,128]{2,1,0:T(8,128)}, f32[6,512,128]{2,1,0:T(8,128)S(1)}, u32[]{:S(2)}) copy-start(f32[6,512,128]{2,1,0:T(8,128)S(1)} %get-tuple-element.14) | copy-start | bytes 4718596
  170.3 18.4 %copy-start.4 = (f32[4,512,128]{2,1,0:T(8,128)}, f32[4,512,128]{2,1,0:T(8,128)S(1)}, u32[]{:S(2)}) copy-start(f32[4,512,128]{2,1,0:T(8,128)S(1)} %get-tuple-element.31) | copy-start | bytes 3145732
  188.3 1.6 copy-start.1
  193.8 21.3 %collective-permute-start.4 = (f32[2,1,512,128]{3,2,1,0:T(8,128)}, f32[2,1,512,128]{3,2,1,0:T(8,128)}, u32[]{:S(2)}, u32[]{:S(2)}) collective-permute-start(f32[2,1,512,128]{3,2,1,0:T(8,128)} %get-tuple-element.24), channel_id=1, source_target_pairs={{0,4},{4,8},{8,12},{12,16},{16,20},{20,24},{24,28},{28,0},{1,5},{5... | collective-permute-start | bytes 1572872 | tf_op jit(solution)/shard_map/ppermute | solution.py:20
  193.8 26.2 %collective-permute-start.5 = (f32[2,1,512,128]{3,2,1,0:T(8,128)}, f32[2,1,512,128]{3,2,1,0:T(8,128)}, u32[]{:S(2)}, u32[]{:S(2)}) collective-permute-start(f32[2,1,512,128]{3,2,1,0:T(8,128)} %get-tuple-element.25), channel_id=1, source_target_pairs={{4,0},{8,4},{12,8},{16,12},{20,16},{24,20},{28,24},{0,28},{5,1},{9... | collective-permute-start | bytes 1572872 | tf_op jit(solution)/shard_map/ppermute | solution.py:21
  204.0 27.1 %all-to-all-start.2 = ((bf16[2,4,65536]{2,0,1:T(2,128)(2,1)}), bf16[2,4,65536]{2,0,1:T(2,128)(2,1)}, u32[]{:S(2)}, u32[]{:S(2)}) async-start(bf16[2,4,65536]{2,0,1:T(2,128)(2,1)} %copy.21), calls=%async_computation.2 | async-start | bytes 2097152 | tf_op jit(solution)/shard_map/all_to_all | solution.py:88
  223.2 1.2 copy-start.5
  231.2 17.9 %all-to-all-start.3 = ((bf16[2,4,65536]{2,0,1:T(2,128)(2,1)}), bf16[2,4,65536]{2,0,1:T(2,128)(2,1)S(1)}, u32[]{:S(2)}, u32[]{:S(2)}) async-start(bf16[2,4,65536]{2,0,1:T(2,128)(2,1)} %copy.22), calls=%async_computation.3 | async-start | bytes 2097152 | tf_op jit(solution)/shard_map/all_to_all | solution.py:88
where the time goes:
time: 298 us; the launch traced here: 295 us
  local copies, waits for them, and re-layouts  117 us (39%)
  waiting for transfers between devices  69.2 us (23%)
  blocking collectives  38.3 us (13%)
  starting transfers between devices  35.3 us (12%)
  other arithmetic  33 us (11%)
    scatter x1, local copies, waits for them, and re-layouts, place(): send_cols = jnp.zeros((count * cap,), jnp.int32).at[where_to].set(columns)  65 us
    ppermute x3, waiting for transfers between devices, padded_2(): before = lax.ppermute(last, axis, up)  48.1 us
    psum x1, blocking collectives, body(): gram = lax.psum(partial_gram, ('space', 'batch')) * scale  38.3 us
    scatter x1, local copies, waits for them, and re-layouts, place(): jnp.zeros((count * cap, depth), jnp.float32).at[where_to].set(values)  24.6 us
    unnamed x5, other arithmetic  15.7 us
    ppermute x3, starting transfers between devices, padded_2(): after = lax.ppermute(initial, axis, down)  12.1 us
    ppermute x3, waiting for transfers between devices, padded_2(): after = lax.ppermute(initial, axis, down)  10.6 us
    all_to_all x2, waiting for transfers between devices, record(): lax.all_to_all(snap, 'batch', split_axis=1, concat_axis=0, tiled=True)  10.5 us
  transfers between devices with their start and end apart: 10, of which 7 were waited for; matrix products, arithmetic and copies ran while one was open for 16% of the time, Pallas kernels for 0%

commit v1 on v0

v1 whole, which is shorter than its diff:
```python
import math

import jax
import jax.numpy as jnp
from jax import lax
from jax.sharding import PartitionSpec as P

STEPS = 2
ACT = 4
SENS = 4


def padded(value, axis, width, dim):
    peers, length = lax.axis_size(axis), value.shape[dim]
    up = [(i, (i + 1) % peers) for i in range(peers)]
    down = [(j, i) for i, j in up]
    last = lax.slice_in_dim(value, length - width, length, axis=dim)
    initial = lax.slice_in_dim(value, 0, width, axis=dim)
    before = lax.ppermute(last, axis, up)
    after = lax.ppermute(initial, axis, down)
    return jnp.concatenate([before, value, after], axis=dim)


def pieces(x):
    out, rest = [], x
    for _ in range(3):
        part = lax.reduce_precision(rest, exponent_bits=8, mantissa_bits=7)
        out.append(part.astype(jnp.bfloat16))
        rest = rest - part
    return out


def select(onehot, values):
    total = None
    for part in pieces(values):
        term = jnp.einsum("fmk,fkd->fmd", onehot, part, preferred_element_type=jnp.float32)
        total = term if total is None else total + term
    return total


def prepare(coef, adjoint):
    diff_c = coef[0]
    vel_c = coef[1]
    pre_lap = jnp.where(adjoint, diff_c, 1.0)
    post_lap = jnp.where(adjoint, 1.0, diff_c)
    pre_dx = jnp.where(adjoint, vel_c, 1.0)
    post_dx = jnp.where(adjoint, 1.0, -vel_c)
    return (pre_lap, post_lap, pre_dx, post_dx)


def advance(extended, weights):
    pre_lap, post_lap, pre_dx, post_dx = weights
    lifted = pre_lap * extended
    moved = pre_dx * extended
    middle = lifted[:, 1:-1]
    padded_z = jnp.pad(middle, ((0, 0), (0, 0), (0, 0), (1, 1)))
    total = lifted[:, 2:] + lifted[:, :-2]
    total = total + jnp.roll(middle, -1, 2) + jnp.roll(middle, 1, 2)
    total = total + padded_z[..., 2:] + padded_z[..., :-2]
    lapl = total - 6.0 * middle
    slope = 0.5 * (moved[:, 2:] - moved[:, :-2])
    return extended[:, 1:-1] + post_lap[1:-1] * lapl + post_dx[1:-1] * slope


def butterfly(value, axes):
    for axis in axes:
        n = lax.axis_size(axis)
        step = 1
        while step < n:
            value = value + lax.ppermute(value, axis, [(i, i ^ step) for i in range(n)])
            step *= 2
    return value


def body(owner, offset, profile, diffusion, velocity):
    count = lax.axis_size("space")
    fields_dev, rows_dev = offset.shape
    planes, span, depth = diffusion.shape
    cap = 4 * rows_dev // count
    slots = count * cap
    col_rows = -(-cap // depth)

    target = owner[..., 0]
    earlier = jnp.tril(jnp.ones((rows_dev, rows_dev), jnp.bool_), -1)
    same = target[:, :, None] == target[:, None, :]
    rank = jnp.sum(jnp.logical_and(same, earlier[None]), axis=2)
    slot = target * cap + rank
    hit = slot[:, None, :] == lax.broadcasted_iota(jnp.int32, (fields_dev, slots, rows_dev), 1)
    send_vals = select(hit.astype(jnp.bfloat16), profile)
    send_cols = jnp.sum(jnp.where(hit, offset[:, None, :], 0), axis=2).astype(jnp.float32)
    send_cols = jnp.pad(send_cols.reshape(fields_dev, count, cap), ((0, 0), (0, 0), (0, col_rows * depth - cap)))
    payload = jnp.concatenate(
        [send_vals.reshape(fields_dev, count, cap, depth), send_cols.reshape(fields_dev, count, col_rows, depth)],
        axis=2,
    )
    got = lax.all_to_all(payload, "space", split_axis=1, concat_axis=1, tiled=True)
    got_vals = got[:, :, :cap].reshape(fields_dev, slots, depth)
    got_cols = got[:, :, cap:].reshape(fields_dev, count, col_rows * depth)[:, :, :cap]
    got_cols = got_cols.reshape(fields_dev, slots).astype(jnp.int32)

    place = got_cols[:, None, :] == lax.broadcasted_iota(jnp.int32, (fields_dev, planes * span, slots), 1)
    state = select(place.astype(jnp.bfloat16), got_vals).reshape(fields_dev, planes, span, depth)

    adjoint = lax.axis_index("batch") >= lax.axis_size("batch") // 2
    coef = jnp.stack([diffusion, velocity])
    rim = padded(coef, "space", STEPS, 1)
    weights = prepare(rim, adjoint)
    extended = padded(state, "space", STEPS, 1)

    pieces_ = []

    def record(current):
        snap = current.astype(jnp.bfloat16).reshape(fields_dev, -1)
        pieces_.append(lax.all_to_all(snap, "batch", split_axis=1, concat_axis=0, tiled=True))

    for step in range(STEPS):
        extended = advance(extended, weights)
        weights = tuple(w[1:-1] for w in weights)
        width = STEPS - 1 - step
        record(extended[:, width:extended.shape[1] - width])
    state = extended
    mixed = jnp.stack(pieces_)
    actuated = mixed[:, :ACT].reshape(STEPS * ACT, -1)
    sensed = mixed[:, ACT:].reshape(STEPS * SENS, -1)
    partial_gram = lax.dot_general(
        sensed, actuated, (((1,), (1,)), ((), ())), preferred_element_type=jnp.float32
    )
    scale = 4.0 / math.sqrt(planes * count * span * depth)
    gram = butterfly(partial_gram, ("batch", "space")) * scale
    return (state, gram)


def solution(mesh):
    in_specs = (
        P("batch", "space", None),
        P("batch", "space"),
        P("batch", "space", None),
        P("space", None, None),
        P("space", None, None),
    )
    out_specs = (P("batch", "space", None, None), P())
    return jax.shard_map(body, mesh=mesh, in_specs=in_specs, out_specs=out_specs, check_vma=False)
```

time: 298 us -> 223 us (0.75)
  local copies, waits for them, and re-layouts: 117 us -> 32.4 us
  waiting for transfers between devices: 69.2 us -> 114 us
  blocking collectives: 38.3 us -> 0 us
  matrix products: 0.77 us -> 12.9 us
  starting transfers between devices: 35.3 us -> 29 us
    scatter x2 -> x0, local copies, waits for them, and re-layouts: 89.6 us -> none  [the longest x1 65 us: place(): send_cols = jnp.zeros((count * cap,), jnp.int32).at[where_to].set(columns)]
    ppermute x6 -> x9, waiting for transfers between devices: 58.7 us -> 99.8 us  [the longest x2 82.5 us: padded(): before = lax.ppermute(last, axis, up)]
    psum x1 -> x0, blocking collectives: 38.3 us -> none  [body(): gram = lax.psum(partial_gram, ('space', 'batch')) * scale]
    unnamed x5 -> x0, other arithmetic: 15.7 us -> none
    dot_general x0 -> x6, matrix products: none -> 12.1 us  [select(): jnp.einsum('fmk,fkd->fmd', onehot, part, preferred_element_type=jnp.float32)]
    mul x1 -> x2, other arithmetic: 0.59 us -> 10.8 us  [the longest x1 10.2 us: advance(): moved = pre_dx * extended]
    all_to_all x2 -> x1, starting transfers between devices: 13.1 us -> 7.28 us  [body(): lax.all_to_all(payload, 'space', split_axis=1, concat_axis=1, tiled=True)]
    concatenate x1 -> x3, other arithmetic: 3.06 us -> 7.18 us  [the longest x2 5.67 us: padded(): return jnp.concatenate([before, value, after], axis=dim)]
  transfers between devices with their start and end apart: 10 -> 12, of which waited for: 7 -> 11; matrix products, arithmetic and copies ran while one was open for 16% -> 11% of each run, Pallas kernels for 0% -> 0%
where the time goes in v1:
time: 223 us; the launch traced here: 222 us
  waiting for transfers between devices  114 us (51%)
  other arithmetic  33.2 us (15%)
  local copies, waits for them, and re-layouts  32.4 us (15%)
  starting transfers between devices  29 us (13%)
  matrix products  12.9 us (6%)
    ppermute x2, waiting for transfers between devices, padded(): before = lax.ppermute(last, axis, up)  82.5 us
    all_to_all x2, waiting for transfers between devices, record(): lax.all_to_all(snap, 'batch', split_axis=1, concat_axis=0, tiled=True)  13.9 us
    dot_general x6, matrix products, select(): jnp.einsum('fmk,fkd->fmd', onehot, part, preferred_element_type=jnp.float32)  12.1 us
    ppermute x5, waiting for transfers between devices, butterfly(): value = value + lax.ppermute(value, axis, [(i, i ^ step) for i in range(n)])  12.1 us
    mul x1, other arithmetic, advance(): moved = pre_dx * extended  10.2 us
    all_to_all x4, local copies, waits for them, and re-layouts, record(): lax.all_to_all(snap, 'batch', split_axis=1, concat_axis=0, tiled=True)  9.02 us
    all_to_all x2, starting transfers between devices, record(): lax.all_to_all(snap, 'batch', split_axis=1, concat_axis=0, tiled=True)  7.77 us
    all_to_all x1, starting transfers between devices, body(): lax.all_to_all(payload, 'space', split_axis=1, concat_axis=1, tiled=True)  7.28 us
  transfers between devices with their start and end apart: 12, of which 11 were waited for; matrix products, arithmetic and copies ran while one was open for 11% of the time, Pallas kernels for 0%

profile of v1, /device:TPU:0, one launch (start us, length us, event | category | flops | bytes accessed | tf_op | source)
XLA Modules:
  0.0 222.1 jit_solution(7220350621608167962)
XLA Ops:
  9.2 7.3 %all-to-all-start = ((f32[2,8,129,128]{3,0,2,1:T(2,128)}), f32[2,8,129,128]{3,0,2,1:T(2,128)S(1)}, u32[]{:S(2)}, u32[]{:S(2)}) async-start(f32[2,8,129,128]{3,0,2,1:T(2,128)} %pad_maximum_fusion.2), calls=%async_computation | async-start | bytes 2113536 | tf_op jit(solution)/shard_map/all_to_all | solution.py:96
  19.9 2.7 %collective-permute-start.3 = (f32[2,2,512,128]{3,2,1,0:T(8,128)}, f32[2,2,512,128]{3,2,1,0:T(8,128)}, u32[]{:S(2)}, u32[]{:S(2)}) collective-permute-start(f32[2,2,512,128]{3,2,1,0:T(8,128)} %get-tuple-element.26), channel_id=1, source_target_pairs={{4,0},{8,4},{12,8},{16,12},{20,16},{24,20},{28,24},{0,28},{5,1},{9... | collective-permute-start | bytes 3145736 | tf_op jit(solution)/shard_map/ppermute | solution.py:20
  22.7 50.3 %collective-permute-done.2 = f32[2,2,512,128]{3,2,1,0:T(8,128)} collective-permute-done((f32[2,2,512,128]{3,2,1,0:T(8,128)}, f32[2,2,512,128]{3,2,1,0:T(8,128)}, u32[]{:S(2)}, u32[]{:S(2)}) %collective-permute-start.2) | collective-permute-done | bytes 1048608 | tf_op jit(solution)/shard_map/ppermute | solution.py:19
  77.0 3.0 %slice_select_fusion.2 = (f32[1,8,512,128]{3,2,1,0:T(8,128)}, f32[1,8,512,128]{3,2,1,0:T(8,128)S(1)}, f32[1,8,512,128]{3,2,1,0:T(8,128)}, f32[1,8,512,128]{3,2,1,0:T(8,128)}) fusion(f32[2,8,512,128]{3,2,1,0:T(8,128)S(1)} %pad_maximum_fusion.1, pred[]{:T(512)S(6)} %ge.12), kind=kLoop, calls=%fused_computation.50 | loop fusion | flops 2621440 | bytes 12582913 | tf_op jit(solution)/shard_map/jit(_where)/select_n | solution.py:45
  80.5 2.8 %fusion.1 = f32[2,2048,128]{2,1,0:T(8,128)S(1)} fusion(bf16[2,1024,128]{2,1,0:T(8,128)(2,1)S(1)} %get-tuple-element.28, s32[2,1024]{1,0:T(2,128)S(1)} %fusion.42), kind=kOutput, calls=%fused_computation.2 | convolution fusion | flops 1077936128 | bytes 2629632 | tf_op jit(solution)/shard_map/fmk,fkd->fmd/dot_general | solution.py:36
  83.4 3.0 %fusion.15 = f32[2,2048,128]{2,1,0:T(8,128)S(1)} fusion(f32[2,2048,128]{2,1,0:T(8,128)S(1)} %fusion.1, bf16[2,1024,128]{2,1,0:T(8,128)(2,1)S(1)} %get-tuple-element.29, s32[2,1024]{1,0:T(2,128)S(1)} %fusion.42), kind=kOutput, calls=%fused_computation.24 | convolution fusion | flops 1078460416 | bytes 4726784 | tf_op jit(solution)/shard_map/fmk,fkd->fmd/dot_general | solution.py:36
  86.4 3.0 %fusion.16 = f32[2,2048,128]{2,1,0:T(8,128)S(1)} fusion(f32[2,2048,128]{2,1,0:T(8,128)S(1)} %fusion.15, bf16[2,1024,128]{2,1,0:T(8,128)(2,1)S(1)} %get-tuple-element.27, s32[2,1024]{1,0:T(2,128)S(1)} %fusion.42), kind=kOutput, calls=%fused_computation.25 | convolution fusion | flops 1078460416 | bytes 4726784 | tf_op jit(solution)/shard_map/fmk,fkd->fmd/dot_general | solution.py:36
  89.9 4.4 %collective-permute-start.1 = (f32[2,2,512,128]{3,2,1,0:T(8,128)S(1)}, f32[2,2,512,128]{3,2,1,0:T(8,128)S(1)}, u32[]{:S(2)}, u32[]{:S(2)}) collective-permute-start(f32[2,2,512,128]{3,2,1,0:T(8,128)S(1)} %get-tuple-element.24), channel_id=1, source_target_pairs={{4,0},{8,4},{12,8},{16,12},{20,16},{24,20},{28,24},{0,28},{5,1},{9... | collective-permute-start | bytes 3145736 | tf_op jit(solution)/shard_map/ppermute | solution.py:20
  102.0 32.2 %collective-permute-done = f32[2,2,512,128]{3,2,1,0:T(8,128)S(1)} collective-permute-done((f32[2,2,512,128]{3,2,1,0:T(8,128)S(1)}, f32[2,2,512,128]{3,2,1,0:T(8,128)S(1)}, u32[]{:S(2)}, u32[]{:S(2)}) %collective-permute-start) | collective-permute-done | bytes 1048608 | tf_op jit(solution)/shard_map/ppermute | solution.py:19
  134.1 3.1 %collective-permute-done.1 = f32[2,2,512,128]{3,2,1,0:T(8,128)S(1)} collective-permute-done((f32[2,2,512,128]{3,2,1,0:T(8,128)S(1)}, f32[2,2,512,128]{3,2,1,0:T(8,128)S(1)}, u32[]{:S(2)}, u32[]{:S(2)}) %collective-permute-start.1) | collective-permute-done | bytes 1048608 | tf_op jit(solution)/shard_map/ppermute | solution.py:20
  137.2 3.8 %pad_maximum_fusion = (f32[2,8,512,128]{3,2,1,0:T(8,128)}, f32[2,8,512,128]{3,2,1,0:T(8,128)S(1)}, f32[2,8,512,128]{3,2,1,0:T(8,128)}) fusion(f32[2,2,512,128]{3,2,1,0:T(8,128)S(1)} %collective-permute-done.1, f32[2,4,512,128]{3,2,1,0:T(8,128)S(1)} %bitcast.48, f32[2,2,512,128]{3,2,1,0:T(8,128)S(1)} %collective-permute-done, f32[8,512,128]{2,1,0:T(8,128)S(1)} %bitcast.45, ...), kind=kLoop, calls=%fused_computation.11 | loop fusion | flops 4194304 | bytes 20971520 | tf_op jit(solution)/shard_map/concatenate | solution.py:21
  141.3 3.3 %fusion.46 = (f32[2,6,511,128]{3,2,1,0:T(8,128)}, f32[2,6,511,128]{3,2,1,0:T(8,128)}) fusion(f32[2,8,512,128]{3,2,1,0:T(8,128)S(1)} %get-tuple-element.7), kind=kLoop, calls=%fused_computation.93 | loop fusion | bytes 12558336 | tf_op jit(solution)/shard_map/jit(_roll_static)/slice | solution.py:58
  144.5 10.2 %broadcast_multiply_fusion.2 = (f32[2,6,512,128]{3,2,1,0:T(8,128)}, f32[2,6,512,128]{3,2,1,0:T(8,128)S(1)}) fusion(f32[6,512,128]{2,1,0:T(8,128)} %get-tuple-element.30, f32[6,512,128]{2,1,0:T(8,128)} %get-tuple-element.31, f32[2,8,512,128]{3,2,1,0:T(8,128)} %get-tuple-element.8, f32[2,6,512,128]{3,2,1,0:T(8,128)S(1)} %slice.214, ...), kind=kLoop, calls=%fused_computation.56 | loop fusion | flops 11796480 | bytes 36175872 | tf_op jit(solution)/shard_map/mul | solution.py:54
  155.9 2.2 %all_to_all.28 = bf16[2,4,65536]{2,1,0:T(4,128)(2,1)} reshape(bf16[2,4,512,128]{3,2,1,0:T(8,128)(2,1)} %slice.321) | data formatting | bytes 2097152 | tf_op jit(solution)/shard_map/all_to_all | solution.py:114
  158.1 3.3 %copy.15 = bf16[2,4,65536]{2,0,1:T(2,128)(2,1)} copy(bf16[2,4,65536]{2,1,0:T(4,128)(2,1)} %all_to_all.28) | data formatting | bytes 2097152 | tf_op jit(solution)/shard_map/all_to_all | solution.py:114
  161.4 4.3 %all-to-all-start.1 = ((bf16[2,4,65536]{2,0,1:T(2,128)(2,1)}), bf16[2,4,65536]{2,0,1:T(2,128)(2,1)}, u32[]{:S(2)}, u32[]{:S(2)}) async-start(bf16[2,4,65536]{2,0,1:T(2,128)(2,1)} %copy.15), calls=%async_computation.1 | async-start | bytes 2097152 | tf_op jit(solution)/shard_map/all_to_all | solution.py:114
  170.0 3.3 %fusion.43 = (bf16[2,4,512,128]{3,2,1,0:T(8,128)(2,1)}, f32[2,4,512,128]{3,2,1,0:T(8,128)}) fusion(f32[4,512,128]{2,1,0:T(8,128)S(1)} %copy-done.4, f32[2,6,512,128]{3,2,1,0:T(8,128)S(1)} %copy-done, f32[2,4,512,128]{3,2,1,0:T(8,128)S(1)} %slice.228, f32[2,4,511,128]{3,2,1,0:T(8,128)S(1)} %get-tuple-element.18, f32[2,4,1,128]{3,2,1,0:T(1,128)S(1)} %get-tuple-element.20, ...), kind=kLoop, calls=%fused_computation.92 | loop fusion | flops 7864320 | bytes 22020096 | tf_op jit(solution)/shard_map/convert_element_type | solution.py:113
  176.7 3.4 %all-to-all-done.1 = bf16[2,4,65536]{2,0,1:T(2,128)(2,1)} async-done(((bf16[2,4,65536]{2,0,1:T(2,128)(2,1)}), bf16[2,4,65536]{2,0,1:T(2,128)(2,1)}, u32[]{:S(2)}, u32[]{:S(2)}) %all-to-all-start.1) | async-done | bytes 1048608 | tf_op jit(solution)/shard_map/all_to_all | solution.py:114
  180.1 3.5 %all-to-all-start.2 = ((bf16[2,4,65536]{2,0,1:T(2,128)(2,1)}), bf16[2,4,65536]{2,0,1:T(2,128)(2,1)S(1)}, u32[]{:S(2)}, u32[]{:S(2)}) async-start(bf16[2,4,65536]{2,0,1:T(2,128)(2,1)} %copy.16), calls=%async_computation.2 | async-start | bytes 2097152 | tf_op jit(solution)/shard_map/all_to_all | solution.py:114
  183.7 2.6 %stack.21 = bf16[1,8,65536]{2,1,0:T(8,128)(2,1)} reshape(bf16[4,2,65536]{2,1,0:T(2,128)(2,1)} %bitcast.15) | data formatting | bytes 2097152 | tf_op jit(solution)/shard_map/stack | solution.py:122
  187.6 10.5 %all-to-all-done.2 = bf16[2,4,65536]{2,0,1:T(2,128)(2,1)S(1)} async-done(((bf16[2,4,65536]{2,0,1:T(2,128)(2,1)}), bf16[2,4,65536]{2,0,1:T(2,128)(2,1)S(1)}, u32[]{:S(2)}, u32[]{:S(2)}) %all-to-all-start.2) | async-done | bytes 1048608 | tf_op jit(solution)/shard_map/all_to_all | solution.py:114
  206.5 3.2 %collective-permute-done.5 = f32[8,8]{1,0:T(8,128)S(1)} collective-permute-done((f32[8,8]{1,0:T(8,128)S(1)}, f32[8,8]{1,0:T(8,128)S(1)}, u32[]{:S(2)}, u32[]{:S(2)}) %collective-permute-start.5) | collective-permute-done | bytes 288 | tf_op jit(solution)/shard_map/ppermute | solution.py:70
  209.7 3.6 %collective-permute-done.6 = f32[8,8]{1,0:T(8,128)S(1)} collective-permute-done((f32[8,8]{1,0:T(8,128)S(1)}, f32[8,8]{1,0:T(8,128)S(1)}, u32[]{:S(2)}, u32[]{:S(2)}) %collective-permute-start.6) | collective-permute-done | bytes 288 | tf_op jit(solution)/shard_map/ppermute | solution.py:70
  217.0 2.6 %collective-permute-start.8 = (f32[8,8]{1,0:T(8,128)S(1)}, f32[8,8]{1,0:T(8,128)S(1)}, u32[]{:S(2)}, u32[]{:S(2)}) collective-permute-start(f32[8,8]{1,0:T(8,128)S(1)} %add.113), channel_id=1, source_target_pairs={{0,16},{4,20},{8,24},{12,28},{16,0},{20,4},{24,8},{28,12},{1,17},{... | collective-permute-start | bytes 776 | tf_op jit(solution)/shard_map/ppermute | solution.py:70
  (73 shorter events, 49.6 us)
Async XLA Ops:
  0.6 5.7 %copy-start.8 = (f32[2,256,128]{2,1,0:T(8,128)S(1)}, f32[2,256,128]{2,1,0:T(8,128)}, u32[]{:S(2)}) copy-start(f32[2,256,128]{2,1,0:T(8,128)} %param.7) | copy-start | bytes 786436
  7.6 8.8 %copy-start.6 = (f32[4,512,128]{2,1,0:T(8,128)S(1)}, f32[4,512,128]{2,1,0:T(8,128)}, u32[]{:S(2)}) copy-start(f32[4,512,128]{2,1,0:T(8,128)} %param.8) | copy-start | bytes 3145732
  7.6 8.8 %copy-start.7 = (f32[4,512,128]{2,1,0:T(8,128)S(1)}, f32[4,512,128]{2,1,0:T(8,128)}, u32[]{:S(2)}) copy-start(f32[4,512,128]{2,1,0:T(8,128)} %param.9) | copy-start | bytes 3145732
  9.2 70.9 %all-to-all-start = ((f32[2,8,129,128]{3,0,2,1:T(2,128)}), f32[2,8,129,128]{3,0,2,1:T(2,128)S(1)}, u32[]{:S(2)}, u32[]{:S(2)}) async-start(f32[2,8,129,128]{3,0,2,1:T(2,128)} %pad_maximum_fusion.2), calls=%async_computation | async-start | bytes 2113536 | tf_op jit(solution)/shard_map/all_to_all | solution.py:96
  17.9 55.0 %collective-permute-start.2 = (f32[2,2,512,128]{3,2,1,0:T(8,128)}, f32[2,2,512,128]{3,2,1,0:T(8,128)}, u32[]{:S(2)}, u32[]{:S(2)}) collective-permute-start(f32[2,2,512,128]{3,2,1,0:T(8,128)} %get-tuple-element.25), channel_id=1, source_target_pairs={{0,4},{4,8},{8,12},{12,16},{16,20},{20,24},{24,28},{28,0},{1,5},{5... | collective-permute-start | bytes 3145736 | tf_op jit(solution)/shard_map/ppermute | solution.py:19
  19.9 55.2 %collective-permute-start.3 = (f32[2,2,512,128]{3,2,1,0:T(8,128)}, f32[2,2,512,128]{3,2,1,0:T(8,128)}, u32[]{:S(2)}, u32[]{:S(2)}) collective-permute-start(f32[2,2,512,128]{3,2,1,0:T(8,128)} %get-tuple-element.26), channel_id=1, source_target_pairs={{4,0},{8,4},{12,8},{16,12},{20,16},{24,20},{28,24},{0,28},{5,1},{9... | collective-permute-start | bytes 3145736 | tf_op jit(solution)/shard_map/ppermute | solution.py:20
  89.4 4.9 %copy-start.3 = (f32[1,8,512,128]{3,2,1,0:T(8,128)S(1)}, f32[1,8,512,128]{3,2,1,0:T(8,128)}, u32[]{:S(2)}) copy-start(f32[1,8,512,128]{3,2,1,0:T(8,128)} %get-tuple-element.9) | copy-start | bytes 6291460
  89.5 44.6 %collective-permute-start = (f32[2,2,512,128]{3,2,1,0:T(8,128)S(1)}, f32[2,2,512,128]{3,2,1,0:T(8,128)S(1)}, u32[]{:S(2)}, u32[]{:S(2)}) collective-permute-start(f32[2,2,512,128]{3,2,1,0:T(8,128)S(1)} %get-tuple-element.23), channel_id=1, source_target_pairs={{0,4},{4,8},{8,12},{12,16},{16,20},{20,24},{24,28},{28,0},{1,5},{5... | collective-permute-start | bytes 3145736 | tf_op jit(solution)/shard_map/ppermute | solution.py:19
  89.9 47.3 %collective-permute-start.1 = (f32[2,2,512,128]{3,2,1,0:T(8,128)S(1)}, f32[2,2,512,128]{3,2,1,0:T(8,128)S(1)}, u32[]{:S(2)}, u32[]{:S(2)}) collective-permute-start(f32[2,2,512,128]{3,2,1,0:T(8,128)S(1)} %get-tuple-element.24), channel_id=1, source_target_pairs={{4,0},{8,4},{12,8},{16,12},{20,16},{24,20},{28,24},{0,28},{5,1},{9... | collective-permute-start | bytes 3145736 | tf_op jit(solution)/shard_map/ppermute | solution.py:20
  95.5 2.2 copy-start.2
  97.7 2.3 %copy-start.1 = (f32[1,8,512,128]{3,2,1,0:T(8,128)S(1)}, f32[1,8,512,128]{3,2,1,0:T(8,128)}, u32[]{:S(2)}) copy-start(f32[1,8,512,128]{3,2,1,0:T(8,128)} %get-tuple-element.12) | copy-start | bytes 6291460
  161.4 18.8 %all-to-all-start.1 = ((bf16[2,4,65536]{2,0,1:T(2,128)(2,1)}), bf16[2,4,65536]{2,0,1:T(2,128)(2,1)}, u32[]{:S(2)}, u32[]{:S(2)}) async-start(bf16[2,4,65536]{2,0,1:T(2,128)(2,1)} %copy.15), calls=%async_computation.1 | async-start | bytes 2097152 | tf_op jit(solution)/shard_map/all_to_all | solution.py:114
  167.3 1.2 copy-start.5
  167.7 2.0 copy-start
  167.7 2.2 %copy-start.4 = (f32[4,512,128]{2,1,0:T(8,128)S(1)}, f32[4,512,128]{2,1,0:T(8,128)}, u32[]{:S(2)}) copy-start(f32[4,512,128]{2,1,0:T(8,128)} %get-tuple-element.32) | copy-start | bytes 3145732
  180.1 17.9 %all-to-all-start.2 = ((bf16[2,4,65536]{2,0,1:T(2,128)(2,1)}), bf16[2,4,65536]{2,0,1:T(2,128)(2,1)S(1)}, u32[]{:S(2)}, u32[]{:S(2)}) async-start(bf16[2,4,65536]{2,0,1:T(2,128)(2,1)} %copy.16), calls=%async_computation.2 | async-start | bytes 2097152 | tf_op jit(solution)/shard_map/all_to_all | solution.py:114
  204.9 1.2 collective-permute-start.4
  206.1 3.6 %collective-permute-start.5 = (f32[8,8]{1,0:T(8,128)S(1)}, f32[8,8]{1,0:T(8,128)S(1)}, u32[]{:S(2)}, u32[]{:S(2)}) collective-permute-start(f32[8,8]{1,0:T(8,128)S(1)} %add.110), channel_id=1, source_target_pairs={{0,2},{1,3},{2,0},{3,1},{4,6},{5,7},{6,4},{7,5},{8,10},{9,11},{10,... | collective-permute-start | bytes 776 | tf_op jit(solution)/shard_map/ppermute | solution.py:70
  209.7 3.6 %collective-permute-start.6 = (f32[8,8]{1,0:T(8,128)S(1)}, f32[8,8]{1,0:T(8,128)S(1)}, u32[]{:S(2)}, u32[]{:S(2)}) collective-permute-start(f32[8,8]{1,0:T(8,128)S(1)} %add.111), channel_id=1, source_target_pairs={{0,4},{4,0},{8,12},{12,8},{16,20},{20,16},{24,28},{28,24},{1,5},{5... | collective-permute-start | bytes 776 | tf_op jit(solution)/shard_map/ppermute | solution.py:70
  213.4 3.6 %collective-permute-start.7 = (f32[8,8]{1,0:T(8,128)S(1)}, f32[8,8]{1,0:T(8,128)S(1)}, u32[]{:S(2)}, u32[]{:S(2)}) collective-permute-start(f32[8,8]{1,0:T(8,128)S(1)} %add.112), channel_id=1, source_target_pairs={{0,8},{4,12},{8,0},{12,4},{16,24},{20,28},{24,16},{28,20},{1,9},{5... | collective-permute-start | bytes 776 | tf_op jit(solution)/shard_map/ppermute | solution.py:70
  217.0 4.5 %collective-permute-start.8 = (f32[8,8]{1,0:T(8,128)S(1)}, f32[8,8]{1,0:T(8,128)S(1)}, u32[]{:S(2)}, u32[]{:S(2)}) collective-permute-start(f32[8,8]{1,0:T(8,128)S(1)} %add.113), channel_id=1, source_target_pairs={{0,16},{4,20},{8,24},{12,28},{16,0},{20,4},{24,8},{28,12},{1,17},{... | collective-permute-start | bytes 776 | tf_op jit(solution)/shard_map/ppermute | solution.py:70

commit v2 on v1

--- a/solution.py
+++ b/solution.py
@@ -18,6 +18,26 @@
     initial = lax.slice_in_dim(value, 0, width, axis=dim)
     before = lax.ppermute(last, axis, up)
     after = lax.ppermute(initial, axis, down)
+    return jnp.concatenate([before, value, after], axis=dim)
+
+
+def padded_shared(value, width, dim):
+    peers, pair = lax.axis_size("space"), lax.axis_size("batch")
+    if pair % 2:
+        return padded(value, "space", width, dim)
+    length = value.shape[dim]
+    odd = lax.axis_index("batch") % 2 == 1
+    last = lax.slice_in_dim(value, length - width, length, axis=dim)
+    initial = lax.slice_in_dim(value, 0, width, axis=dim)
+    routes = []
+    for s in range(peers):
+        for b in range(pair):
+            ahead = (s + 1) % peers if b % 2 == 0 else (s - 1) % peers
+            routes.append((s * pair + b, ahead * pair + b))
+    got = lax.ppermute(jnp.where(odd, initial, last), ("space", "batch"), routes)
+    other = lax.ppermute(got, "batch", [(b, b ^ 1) for b in range(pair)])
+    before = jnp.where(odd, other, got)
+    after = jnp.where(odd, got, other)
     return jnp.concatenate([before, value, after], axis=dim)
 
 
@@ -103,7 +123,7 @@
 
     adjoint = lax.axis_index("batch") >= lax.axis_size("batch") // 2
     coef = jnp.stack([diffusion, velocity])
-    rim = padded(coef, "space", STEPS, 1)
+    rim = padded_shared(coef, STEPS, 1)
     weights = prepare(rim, adjoint)
     extended = padded(state, "space", STEPS, 1)
 

time: 223 us -> 197 us (0.88)
  waiting for transfers between devices: 114 us -> 92.9 us
  other arithmetic: 33.2 us -> 30.7 us
    ppermute x2 -> x1, waiting for transfers between devices: 82.5 us -> 33.2 us  [padded(): before = lax.ppermute(last, axis, up)]
    ppermute x0 -> x2, waiting for transfers between devices: none -> 31 us  [the longest x1 31 us: padded_shared(): lax.ppermute(jnp.where(odd, initial, last), ('space', 'batch'), routes)]
    ppermute x2 -> x1, starting transfers between devices: 7.14 us -> 2.2 us  [padded(): after = lax.ppermute(initial, axis, down)]
    ppermute x0 -> x2, starting transfers between devices: none -> 4.03 us  [the longest x1 2.01 us: padded_shared(): lax.ppermute(jnp.where(odd, initial, last), ('space', 'batch'), routes)]
    ppermute x2 -> x1, waiting for transfers between devices: 5.26 us -> 2.2 us  [padded(): after = lax.ppermute(initial, axis, down)]
    select_n x0 -> x2, other arithmetic: none -> 2.77 us  [the longest x1 1.71 us: padded_shared(): before = jnp.where(odd, other, got)]
    concatenate x2 -> x1, other arithmetic: 5.67 us -> 3.82 us  [padded(): return jnp.concatenate([before, value, after], axis=dim)]
    unnamed x20 -> x14, local copies, waits for them, and re-layouts: 5.9 us -> 4.13 us
  transfers between devices with their start and end apart: 12 -> 12, of which waited for: 11 -> 10; matrix products, arithmetic and copies ran while one was open for 11% -> 16% of each run, Pallas kernels for 0% -> 0%
where the time goes in v2:
time: 197 us; the launch traced here: 196 us
  waiting for transfers between devices  92.9 us (47%)
  other arithmetic  30.7 us (16%)
  local copies, waits for them, and re-layouts  30.6 us (16%)
  starting transfers between devices  27.8 us (14%)
  matrix products  12.9 us (7%)
    ppermute x1, waiting for transfers between devices, padded(): before = lax.ppermute(last, axis, up)  33.2 us
    ppermute x1, waiting for transfers between devices, padded_shared(): lax.ppermute(jnp.where(odd, initial, last), ('space', 'batch'), routes)  31 us
    all_to_all x2, waiting for transfers between devices, record(): lax.all_to_all(snap, 'batch', split_axis=1, concat_axis=0, tiled=True)  13.9 us
    ppermute x5, waiting for transfers between devices, butterfly(): value = value + lax.ppermute(value, axis, [(i, i ^ step) for i in range(n)])  12.6 us
    dot_general x6, matrix products, select(): jnp.einsum('fmk,fkd->fmd', onehot, part, preferred_element_type=jnp.float32)  12.1 us
    mul x1, other arithmetic, advance(): moved = pre_dx * extended  10.2 us
    all_to_all x4, local copies, waits for them, and re-layouts, record(): lax.all_to_all(snap, 'batch', split_axis=1, concat_axis=0, tiled=True)  9.02 us
    all_to_all x2, starting transfers between devices, record(): lax.all_to_all(snap, 'batch', split_axis=1, concat_axis=0, tiled=True)  7.77 us
  transfers between devices with their start and end apart: 12, of which 10 were waited for; matrix products, arithmetic and copies ran while one was open for 16% of the time, Pallas kernels for 0%

profile of v2, /device:TPU:0, one launch (start us, length us, event | category | flops | bytes accessed | tf_op | source)
XLA Modules:
  0.0 195.8 jit_solution(8486411496508409351)
XLA Ops:
  9.1 7.3 %all-to-all-start = ((f32[2,8,129,128]{3,0,2,1:T(2,128)}), f32[2,8,129,128]{3,0,2,1:T(2,128)S(1)}, u32[]{:S(2)}, u32[]{:S(2)}) async-start(f32[2,8,129,128]{3,0,2,1:T(2,128)} %pad_maximum_fusion.2), calls=%async_computation | async-start | bytes 2113536 | tf_op jit(solution)/shard_map/all_to_all | solution.py:116
  19.5 31.0 %collective-permute-done.2 = f32[2,2,512,128]{3,2,1,0:T(8,128)} collective-permute-done((f32[2,2,512,128]{3,2,1,0:T(8,128)}, f32[2,2,512,128]{3,2,1,0:T(8,128)}, u32[]{:S(2)}, u32[]{:S(2)}) %collective-permute-start.2) | collective-permute-done | bytes 1048608 | tf_op jit(solution)/shard_map/ppermute | solution.py:37
  53.0 2.8 %fusion.1 = f32[2,2048,128]{2,1,0:T(8,128)S(1)} fusion(bf16[2,1024,128]{2,1,0:T(8,128)(2,1)S(1)} %get-tuple-element.28, s32[2,1024]{1,0:T(2,128)S(1)} %fusion.43), kind=kOutput, calls=%fused_computation.2 | convolution fusion | flops 1077936128 | bytes 2629632 | tf_op jit(solution)/shard_map/fmk,fkd->fmd/dot_general | solution.py:56
  55.8 3.0 %fusion.15 = f32[2,2048,128]{2,1,0:T(8,128)S(1)} fusion(f32[2,2048,128]{2,1,0:T(8,128)S(1)} %fusion.1, bf16[2,1024,128]{2,1,0:T(8,128)(2,1)S(1)} %get-tuple-element.29, s32[2,1024]{1,0:T(2,128)S(1)} %fusion.43), kind=kOutput, calls=%fused_computation.24 | convolution fusion | flops 1078460416 | bytes 4726784 | tf_op jit(solution)/shard_map/fmk,fkd->fmd/dot_general | solution.py:56
  58.8 3.0 %fusion.16 = f32[2,2048,128]{2,1,0:T(8,128)S(1)} fusion(f32[2,2048,128]{2,1,0:T(8,128)S(1)} %fusion.15, bf16[2,1024,128]{2,1,0:T(8,128)(2,1)S(1)} %get-tuple-element.27, s32[2,1024]{1,0:T(2,128)S(1)} %fusion.43), kind=kOutput, calls=%fused_computation.25 | convolution fusion | flops 1078460416 | bytes 4726784 | tf_op jit(solution)/shard_map/fmk,fkd->fmd/dot_general | solution.py:56
  61.9 2.6 %collective-permute-start = (f32[2,2,512,128]{3,2,1,0:T(8,128)S(1)}, f32[2,2,512,128]{3,2,1,0:T(8,128)S(1)}, u32[]{:S(2)}, u32[]{:S(2)}) collective-permute-start(f32[2,2,512,128]{3,2,1,0:T(8,128)S(1)} %get-tuple-element.23), channel_id=1, source_target_pairs={{0,4},{4,8},{8,12},{12,16},{16,20},{20,24},{24,28},{28,0},{1,5},{5... | collective-permute-start | bytes 3145736 | tf_op jit(solution)/shard_map/ppermute | solution.py:19
  75.5 33.2 %collective-permute-done = f32[2,2,512,128]{3,2,1,0:T(8,128)S(1)} collective-permute-done((f32[2,2,512,128]{3,2,1,0:T(8,128)S(1)}, f32[2,2,512,128]{3,2,1,0:T(8,128)S(1)}, u32[]{:S(2)}, u32[]{:S(2)}) %collective-permute-start) | collective-permute-done | bytes 1048608 | tf_op jit(solution)/shard_map/ppermute | solution.py:19
  108.7 2.2 %collective-permute-done.1 = f32[2,2,512,128]{3,2,1,0:T(8,128)S(1)} collective-permute-done((f32[2,2,512,128]{3,2,1,0:T(8,128)S(1)}, f32[2,2,512,128]{3,2,1,0:T(8,128)S(1)}, u32[]{:S(2)}, u32[]{:S(2)}) %collective-permute-start.1) | collective-permute-done | bytes 1048608 | tf_op jit(solution)/shard_map/ppermute | solution.py:20
  110.9 3.8 %pad_maximum_fusion = (f32[2,8,512,128]{3,2,1,0:T(8,128)}, f32[2,8,512,128]{3,2,1,0:T(8,128)S(1)}, f32[2,8,512,128]{3,2,1,0:T(8,128)}) fusion(f32[2,2,512,128]{3,2,1,0:T(8,128)S(1)} %collective-permute-done.1, f32[2,4,512,128]{3,2,1,0:T(8,128)S(1)} %bitcast.48, f32[2,2,512,128]{3,2,1,0:T(8,128)S(1)} %collective-permute-done, f32[8,512,128]{2,1,0:T(8,128)S(1)} %bitcast.45, ...), kind=kLoop, calls=%fused_computation.11 | loop fusion | flops 4194304 | bytes 20971520 | tf_op jit(solution)/shard_map/concatenate | solution.py:21
  115.0 3.3 %fusion.47 = (f32[2,6,511,128]{3,2,1,0:T(8,128)}, f32[2,6,511,128]{3,2,1,0:T(8,128)}) fusion(f32[2,8,512,128]{3,2,1,0:T(8,128)S(1)} %get-tuple-element.7), kind=kLoop, calls=%fused_computation.96 | loop fusion | bytes 12558336 | tf_op jit(solution)/shard_map/jit(_roll_static)/slice | solution.py:78
  118.3 10.2 %broadcast_multiply_fusion.2 = (f32[2,6,512,128]{3,2,1,0:T(8,128)}, f32[2,6,512,128]{3,2,1,0:T(8,128)S(1)}) fusion(f32[6,512,128]{2,1,0:T(8,128)} %get-tuple-element.30, f32[6,512,128]{2,1,0:T(8,128)} %get-tuple-element.31, f32[2,8,512,128]{3,2,1,0:T(8,128)} %get-tuple-element.8, f32[2,6,512,128]{3,2,1,0:T(8,128)S(1)} %slice.214, ...), kind=kLoop, calls=%fused_computation.56 | loop fusion | flops 11796480 | bytes 36175872 | tf_op jit(solution)/shard_map/mul | solution.py:74
  129.6 2.2 %all_to_all.28 = bf16[2,4,65536]{2,1,0:T(4,128)(2,1)} reshape(bf16[2,4,512,128]{3,2,1,0:T(8,128)(2,1)} %slice.323) | data formatting | bytes 2097152 | tf_op jit(solution)/shard_map/all_to_all | solution.py:134
  131.9 3.3 %copy.15 = bf16[2,4,65536]{2,0,1:T(2,128)(2,1)} copy(bf16[2,4,65536]{2,1,0:T(4,128)(2,1)} %all_to_all.28) | data formatting | bytes 2097152 | tf_op jit(solution)/shard_map/all_to_all | solution.py:134
  135.1 4.3 %all-to-all-start.1 = ((bf16[2,4,65536]{2,0,1:T(2,128)(2,1)}), bf16[2,4,65536]{2,0,1:T(2,128)(2,1)}, u32[]{:S(2)}, u32[]{:S(2)}) async-start(bf16[2,4,65536]{2,0,1:T(2,128)(2,1)} %copy.15), calls=%async_computation.1 | async-start | bytes 2097152 | tf_op jit(solution)/shard_map/all_to_all | solution.py:134
  143.7 3.2 %fusion.44 = (bf16[2,4,512,128]{3,2,1,0:T(8,128)(2,1)}, f32[2,4,512,128]{3,2,1,0:T(8,128)}) fusion(f32[4,512,128]{2,1,0:T(8,128)S(1)} %copy-done.1, f32[2,6,512,128]{3,2,1,0:T(8,128)S(1)} %copy-done, f32[2,4,512,128]{3,2,1,0:T(8,128)S(1)} %slice.228, f32[2,4,511,128]{3,2,1,0:T(8,128)S(1)} %get-tuple-element.18, f32[2,4,1,128]{3,2,1,0:T(1,128)S(1)} %get-tuple-element.20, ...), kind=kLoop, calls=%fused_computation.95 | loop fusion | flops 7864320 | bytes 22020096 | tf_op jit(solution)/shard_map/convert_element_type | solution.py:133
  150.5 3.4 %all-to-all-done.1 = bf16[2,4,65536]{2,0,1:T(2,128)(2,1)} async-done(((bf16[2,4,65536]{2,0,1:T(2,128)(2,1)}), bf16[2,4,65536]{2,0,1:T(2,128)(2,1)}, u32[]{:S(2)}, u32[]{:S(2)}) %all-to-all-start.1) | async-done | bytes 1048608 | tf_op jit(solution)/shard_map/all_to_all | solution.py:134
  153.9 3.5 %all-to-all-start.2 = ((bf16[2,4,65536]{2,0,1:T(2,128)(2,1)}), bf16[2,4,65536]{2,0,1:T(2,128)(2,1)S(1)}, u32[]{:S(2)}, u32[]{:S(2)}) async-start(bf16[2,4,65536]{2,0,1:T(2,128)(2,1)} %copy.16), calls=%async_computation.2 | async-start | bytes 2097152 | tf_op jit(solution)/shard_map/all_to_all | solution.py:134
  157.4 2.6 %stack.21 = bf16[1,8,65536]{2,1,0:T(8,128)(2,1)} reshape(bf16[4,2,65536]{2,1,0:T(2,128)(2,1)} %bitcast.15) | data formatting | bytes 2097152 | tf_op jit(solution)/shard_map/stack | solution.py:142
  161.3 10.5 %all-to-all-done.2 = bf16[2,4,65536]{2,0,1:T(2,128)(2,1)S(1)} async-done(((bf16[2,4,65536]{2,0,1:T(2,128)(2,1)}), bf16[2,4,65536]{2,0,1:T(2,128)(2,1)S(1)}, u32[]{:S(2)}, u32[]{:S(2)}) %all-to-all-start.2) | async-done | bytes 1048608 | tf_op jit(solution)/shard_map/all_to_all | solution.py:134
  180.3 3.2 %collective-permute-done.5 = f32[8,8]{1,0:T(8,128)S(1)} collective-permute-done((f32[8,8]{1,0:T(8,128)S(1)}, f32[8,8]{1,0:T(8,128)S(1)}, u32[]{:S(2)}, u32[]{:S(2)}) %collective-permute-start.5) | collective-permute-done | bytes 288 | tf_op jit(solution)/shard_map/ppermute | solution.py:90
  183.8 3.3 %collective-permute-done.6 = f32[8,8]{1,0:T(8,128)S(1)} collective-permute-done((f32[8,8]{1,0:T(8,128)S(1)}, f32[8,8]{1,0:T(8,128)S(1)}, u32[]{:S(2)}, u32[]{:S(2)}) %collective-permute-start.6) | collective-permute-done | bytes 288 | tf_op jit(solution)/shard_map/ppermute | solution.py:90
  188.1 2.6 %collective-permute-done.7 = f32[8,8]{1,0:T(8,128)S(1)} collective-permute-done((f32[8,8]{1,0:T(8,128)S(1)}, f32[8,8]{1,0:T(8,128)S(1)}, u32[]{:S(2)}, u32[]{:S(2)}) %collective-permute-start.7) | collective-permute-done | bytes 288 | tf_op jit(solution)/shard_map/ppermute | solution.py:90
  190.7 2.2 %collective-permute-start.8 = (f32[8,8]{1,0:T(8,128)S(1)}, f32[8,8]{1,0:T(8,128)S(1)}, u32[]{:S(2)}, u32[]{:S(2)}) collective-permute-start(f32[8,8]{1,0:T(8,128)S(1)} %add.118), channel_id=1, source_target_pairs={{0,16},{4,20},{8,24},{12,28},{16,0},{20,4},{24,8},{28,12},{1,17},{... | collective-permute-start | bytes 776 | tf_op jit(solution)/shard_map/ppermute | solution.py:90
  193.0 2.3 %collective-permute-done.8 = f32[8,8]{1,0:T(8,128)S(1)} collective-permute-done((f32[8,8]{1,0:T(8,128)S(1)}, f32[8,8]{1,0:T(8,128)S(1)}, u32[]{:S(2)}, u32[]{:S(2)}) %collective-permute-start.8) | collective-permute-done | bytes 288 | tf_op jit(solution)/shard_map/ppermute | solution.py:90
  (68 shorter events, 45.9 us)
Async XLA Ops:
  0.6 5.7 %copy-start.5 = (f32[2,256,128]{2,1,0:T(8,128)S(1)}, f32[2,256,128]{2,1,0:T(8,128)}, u32[]{:S(2)}) copy-start(f32[2,256,128]{2,1,0:T(8,128)} %param.7) | copy-start | bytes 786436
  7.6 8.8 %copy-start.3 = (f32[4,512,128]{2,1,0:T(8,128)S(1)}, f32[4,512,128]{2,1,0:T(8,128)}, u32[]{:S(2)}) copy-start(f32[4,512,128]{2,1,0:T(8,128)} %param.8) | copy-start | bytes 3145732
  7.6 8.8 %copy-start.4 = (f32[4,512,128]{2,1,0:T(8,128)S(1)}, f32[4,512,128]{2,1,0:T(8,128)}, u32[]{:S(2)}) copy-start(f32[4,512,128]{2,1,0:T(8,128)} %param.9) | copy-start | bytes 3145732
  9.1 43.4 %all-to-all-start = ((f32[2,8,129,128]{3,0,2,1:T(2,128)}), f32[2,8,129,128]{3,0,2,1:T(2,128)S(1)}, u32[]{:S(2)}, u32[]{:S(2)}) async-start(f32[2,8,129,128]{3,0,2,1:T(2,128)} %pad_maximum_fusion.2), calls=%async_computation | async-start | bytes 2113536 | tf_op jit(solution)/shard_map/all_to_all | solution.py:116
  17.5 33.0 %collective-permute-start.2 = (f32[2,2,512,128]{3,2,1,0:T(8,128)}, f32[2,2,512,128]{3,2,1,0:T(8,128)}, u32[]{:S(2)}, u32[]{:S(2)}) collective-permute-start(f32[2,2,512,128]{3,2,1,0:T(8,128)} %fusion.35), channel_id=1, source_target_pairs={{0,4},{1,29},{2,6},{3,31},{4,8},{5,1},{6,10},{7,3},{8,12},{9,5},{1... | collective-permute-start | bytes 3145736 | tf_op jit(solution)/shard_map/ppermute | solution.py:37
  50.5 16.3 %collective-permute-start.3 = (f32[2,2,512,128]{3,2,1,0:T(8,128)}, f32[2,2,512,128]{3,2,1,0:T(8,128)}, u32[]{:S(2)}, u32[]{:S(2)}) collective-permute-start(f32[2,2,512,128]{3,2,1,0:T(8,128)} %collective-permute-done.2), channel_id=1, source_target_pairs={{0,1},{1,0},{2,3},{3,2},{4,5},{5,4},{6,7},{7,6},{8,9},{9,8},{10,11... | collective-permute-start | bytes 3145736 | tf_op jit(solution)/shard_map/ppermute | solution.py:38
  61.9 46.8 %collective-permute-start = (f32[2,2,512,128]{3,2,1,0:T(8,128)S(1)}, f32[2,2,512,128]{3,2,1,0:T(8,128)S(1)}, u32[]{:S(2)}, u32[]{:S(2)}) collective-permute-start(f32[2,2,512,128]{3,2,1,0:T(8,128)S(1)} %get-tuple-element.23), channel_id=1, source_target_pairs={{0,4},{4,8},{8,12},{12,16},{16,20},{20,24},{24,28},{28,0},{1,5},{5... | collective-permute-start | bytes 3145736 | tf_op jit(solution)/shard_map/ppermute | solution.py:19
  64.5 46.4 %collective-permute-start.1 = (f32[2,2,512,128]{3,2,1,0:T(8,128)S(1)}, f32[2,2,512,128]{3,2,1,0:T(8,128)S(1)}, u32[]{:S(2)}, u32[]{:S(2)}) collective-permute-start(f32[2,2,512,128]{3,2,1,0:T(8,128)S(1)} %get-tuple-element.24), channel_id=1, source_target_pairs={{4,0},{8,4},{12,8},{16,12},{20,16},{24,20},{28,24},{0,28},{5,1},{9... | collective-permute-start | bytes 3145736 | tf_op jit(solution)/shard_map/ppermute | solution.py:20
  135.1 18.8 %all-to-all-start.1 = ((bf16[2,4,65536]{2,0,1:T(2,128)(2,1)}), bf16[2,4,65536]{2,0,1:T(2,128)(2,1)}, u32[]{:S(2)}, u32[]{:S(2)}) async-start(bf16[2,4,65536]{2,0,1:T(2,128)(2,1)} %copy.15), calls=%async_computation.1 | async-start | bytes 2097152 | tf_op jit(solution)/shard_map/all_to_all | solution.py:134
  141.1 1.2 copy-start.2
  141.4 2.0 %copy-start = (f32[2,6,512,128]{3,2,1,0:T(8,128)S(1)}, f32[2,6,512,128]{3,2,1,0:T(8,128)}, u32[]{:S(2)}) copy-start(f32[2,6,512,128]{3,2,1,0:T(8,128)} %get-tuple-element.4) | copy-start | bytes 9437188
  141.4 2.2 %copy-start.1 = (f32[4,512,128]{2,1,0:T(8,128)S(1)}, f32[4,512,128]{2,1,0:T(8,128)}, u32[]{:S(2)}) copy-start(f32[4,512,128]{2,1,0:T(8,128)} %get-tuple-element.32) | copy-start | bytes 3145732
  153.9 17.9 %all-to-all-start.2 = ((bf16[2,4,65536]{2,0,1:T(2,128)(2,1)}), bf16[2,4,65536]{2,0,1:T(2,128)(2,1)S(1)}, u32[]{:S(2)}, u32[]{:S(2)}) async-start(bf16[2,4,65536]{2,0,1:T(2,128)(2,1)} %copy.16), calls=%async_computation.2 | async-start | bytes 2097152 | tf_op jit(solution)/shard_map/all_to_all | solution.py:134
  178.7 1.2 collective-permute-start.4
  179.9 3.6 %collective-permute-start.5 = (f32[8,8]{1,0:T(8,128)S(1)}, f32[8,8]{1,0:T(8,128)S(1)}, u32[]{:S(2)}, u32[]{:S(2)}) collective-permute-start(f32[8,8]{1,0:T(8,128)S(1)} %add.115), channel_id=1, source_target_pairs={{0,2},{1,3},{2,0},{3,1},{4,6},{5,7},{6,4},{7,5},{8,10},{9,11},{10,... | collective-permute-start | bytes 776 | tf_op jit(solution)/shard_map/ppermute | solution.py:90
  183.5 3.6 %collective-permute-start.6 = (f32[8,8]{1,0:T(8,128)S(1)}, f32[8,8]{1,0:T(8,128)S(1)}, u32[]{:S(2)}, u32[]{:S(2)}) collective-permute-start(f32[8,8]{1,0:T(8,128)S(1)} %add.116), channel_id=1, source_target_pairs={{0,4},{4,0},{8,12},{12,8},{16,20},{20,16},{24,28},{28,24},{1,5},{5... | collective-permute-start | bytes 776 | tf_op jit(solution)/shard_map/ppermute | solution.py:90
  187.1 3.6 %collective-permute-start.7 = (f32[8,8]{1,0:T(8,128)S(1)}, f32[8,8]{1,0:T(8,128)S(1)}, u32[]{:S(2)}, u32[]{:S(2)}) collective-permute-start(f32[8,8]{1,0:T(8,128)S(1)} %add.117), channel_id=1, source_target_pairs={{0,8},{4,12},{8,0},{12,4},{16,24},{20,28},{24,16},{28,20},{1,9},{5... | collective-permute-start | bytes 776 | tf_op jit(solution)/shard_map/ppermute | solution.py:90
  190.7 4.5 %collective-permute-start.8 = (f32[8,8]{1,0:T(8,128)S(1)}, f32[8,8]{1,0:T(8,128)S(1)}, u32[]{:S(2)}, u32[]{:S(2)}) collective-permute-start(f32[8,8]{1,0:T(8,128)S(1)} %add.118), channel_id=1, source_target_pairs={{0,16},{4,20},{8,24},{12,28},{16,0},{20,4},{24,8},{28,12},{1,17},{... | collective-permute-start | bytes 776 | tf_op jit(solution)/shard_map/ppermute | solution.py:90

commit v3 on v2

--- a/solution.py
+++ b/solution.py
@@ -10,14 +10,17 @@
 SENS = 4
 
 
+LINK = jnp.bfloat16
+
+
 def padded(value, axis, width, dim):
     peers, length = lax.axis_size(axis), value.shape[dim]
     up = [(i, (i + 1) % peers) for i in range(peers)]
     down = [(j, i) for i, j in up]
-    last = lax.slice_in_dim(value, length - width, length, axis=dim)
-    initial = lax.slice_in_dim(value, 0, width, axis=dim)
-    before = lax.ppermute(last, axis, up)
-    after = lax.ppermute(initial, axis, down)
+    last = lax.slice_in_dim(value, length - width, length, axis=dim).astype(LINK)
+    initial = lax.slice_in_dim(value, 0, width, axis=dim).astype(LINK)
+    before = lax.ppermute(last, axis, up).astype(value.dtype)
+    after = lax.ppermute(initial, axis, down).astype(value.dtype)
     return jnp.concatenate([before, value, after], axis=dim)
 
 
@@ -34,8 +37,9 @@
         for b in range(pair):
             ahead = (s + 1) % peers if b % 2 == 0 else (s - 1) % peers
             routes.append((s * pair + b, ahead * pair + b))
-    got = lax.ppermute(jnp.where(odd, initial, last), ("space", "batch"), routes)
-    other = lax.ppermute(got, "batch", [(b, b ^ 1) for b in range(pair)])
+    got = lax.ppermute(jnp.where(odd, initial, last).astype(LINK), ("space", "batch"), routes)
+    other = lax.ppermute(got, "batch", [(b, b ^ 1) for b in range(pair)]).astype(value.dtype)
+    got = got.astype(value.dtype)
     before = jnp.where(odd, other, got)
     after = jnp.where(odd, got, other)
     return jnp.concatenate([before, value, after], axis=dim)

time: 197 us -> 174 us (0.88)
  waiting for transfers between devices: 92.9 us -> 74 us
  starting transfers between devices: 27.8 us -> 24.2 us
    ppermute x4, waiting for transfers between devices: 66.3 us -> 26.5 us  [the longest x1 15.3 us: padded(): before = lax.ppermute(last, axis, up).astype(value.dtype)]
    all_to_all x1, waiting for transfers between devices: 0.01 us -> 18.6 us  [body(): lax.all_to_all(payload, 'space', split_axis=1, concat_axis=1, tiled=True)]
    ppermute x5, starting transfers between devices: 3.94 us -> 1.48 us  [butterfly(): value = value + lax.ppermute(value, axis, [(i, i ^ step) for i in range(n)])]
    ppermute x5, waiting for transfers between devices: 12.6 us -> 15 us  [butterfly(): value = value + lax.ppermute(value, axis, [(i, i ^ step) for i in range(n)])]
    mul x1 -> x2, other arithmetic: 1.46 us -> 3.43 us  [advance(): return extended[:, 1:-1] + post_lap[1:-1] * lapl + post_dx[1:-1] * slope]
    unnamed x14 -> x28, local copies, waits for them, and re-layouts: 4.13 us -> 5.77 us
  transfers between devices with their start and end apart: 12 -> 12, of which waited for: 10 -> 11; matrix products, arithmetic and copies ran while one was open for 16% -> 14% of each run, Pallas kernels for 0% -> 0%
where the time goes in v3:
time: 174 us; the launch traced here: 173 us
  waiting for transfers between devices  74 us (43%)
  local copies, waits for them, and re-layouts  31.5 us (18%)
  other arithmetic  31.2 us (18%)
  starting transfers between devices  24.2 us (14%)
  matrix products  11 us (6%)
    all_to_all x1, waiting for transfers between devices, body(): lax.all_to_all(payload, 'space', split_axis=1, concat_axis=1, tiled=True)  18.6 us
    ppermute x1, waiting for transfers between devices, padded(): before = lax.ppermute(last, axis, up).astype(value.dtype)  15.3 us
    ppermute x5, waiting for transfers between devices, butterfly(): value = value + lax.ppermute(value, axis, [(i, i ^ step) for i in range(n)])  15 us
    all_to_all x2, waiting for transfers between devices, record(): lax.all_to_all(snap, 'batch', split_axis=1, concat_axis=0, tiled=True)  14 us
    dot_general x6, matrix products, select(): jnp.einsum('fmk,fkd->fmd', onehot, part, preferred_element_type=jnp.float32)  10.2 us
    mul x1, other arithmetic, advance(): moved = pre_dx * extended  10.2 us
    ppermute x1, waiting for transfers between devices, padded_shared(): lax.ppermute(jnp.where(odd, initial, last).astype(LINK), ('space', 'batch...  9.06 us
    all_to_all x4, local copies, waits for them, and re-layouts, record(): lax.all_to_all(snap, 'batch', split_axis=1, concat_axis=0, tiled=True)  9 us
  transfers between devices with their start and end apart: 12, of which 11 were waited for; matrix products, arithmetic and copies ran while one was open for 14% of the time, Pallas kernels for 0%

profile of v3, /device:TPU:0, one launch (start us, length us, event | category | flops | bytes accessed | tf_op | source)
XLA Modules:
  0.0 172.9 jit_solution(1217854613100608203)
XLA Ops:
  2.4 3.0 %collective-permute-start.2 = (bf16[2,2,512,128]{3,2,1,0:T(8,128)(2,1)S(1)}, bf16[2,2,512,128]{3,2,1,0:T(8,128)(2,1)}, u32[]{:S(2)}, u32[]{:S(2)}) collective-permute-start(bf16[2,2,512,128]{3,2,1,0:T(8,128)(2,1)S(1)} %fusion.36), channel_id=1, source_target_pairs={{0,4},{1,29},{2,6},{3,31},{4,8},{5,1},{6,10},{7,3},{8,12},{9,5},{1... | collective-permute-start | bytes 1572872 | tf_op jit(solution)/shard_map/ppermute | solution.py:40
  8.4 9.1 %collective-permute-done.2 = bf16[2,2,512,128]{3,2,1,0:T(8,128)(2,1)} collective-permute-done((bf16[2,2,512,128]{3,2,1,0:T(8,128)(2,1)S(1)}, bf16[2,2,512,128]{3,2,1,0:T(8,128)(2,1)}, u32[]{:S(2)}, u32[]{:S(2)}) %collective-permute-start.2) | collective-permute-done | bytes 524320 | tf_op jit(solution)/shard_map/ppermute | solution.py:40
  19.0 7.1 %all-to-all-start = ((f32[2,8,129,128]{3,0,2,1:T(2,128)}), f32[2,8,129,128]{3,0,2,1:T(2,128)S(1)}, u32[]{:S(2)}, u32[]{:S(2)}) async-start(f32[2,8,129,128]{3,0,2,1:T(2,128)} %pad_maximum_fusion.2), calls=%async_computation | async-start | bytes 2113536 | tf_op jit(solution)/shard_map/all_to_all | solution.py:120
  34.2 18.6 %all-to-all-done = f32[2,8,129,128]{3,0,2,1:T(2,128)S(1)} async-done(((f32[2,8,129,128]{3,0,2,1:T(2,128)}), f32[2,8,129,128]{3,0,2,1:T(2,128)S(1)}, u32[]{:S(2)}, u32[]{:S(2)}) %all-to-all-start) | async-done | bytes 1056800 | tf_op jit(solution)/shard_map/all_to_all | solution.py:120
  53.2 2.8 %fusion.1 = f32[2,2048,128]{2,1,0:T(8,128)S(1)} fusion(bf16[2,1024,128]{2,1,0:T(8,128)(2,1)S(1)} %get-tuple-element.26, s32[2,1024]{1,0:T(2,128)S(1)} %fusion.44), kind=kOutput, calls=%fused_computation.2 | convolution fusion | flops 1077936128 | bytes 2629632 | tf_op jit(solution)/shard_map/fmk,fkd->fmd/dot_general | solution.py:60
  56.1 3.0 %fusion.15 = f32[2,2048,128]{2,1,0:T(8,128)S(1)} fusion(f32[2,2048,128]{2,1,0:T(8,128)S(1)} %fusion.1, bf16[2,1024,128]{2,1,0:T(8,128)(2,1)S(1)} %get-tuple-element.27, s32[2,1024]{1,0:T(2,128)S(1)} %fusion.44), kind=kOutput, calls=%fused_computation.24 | convolution fusion | flops 1078460416 | bytes 4726784 | tf_op jit(solution)/shard_map/fmk,fkd->fmd/dot_general | solution.py:60
  59.1 3.0 %fusion.16 = f32[2,2048,128]{2,1,0:T(8,128)S(1)} fusion(f32[2,2048,128]{2,1,0:T(8,128)S(1)} %fusion.15, bf16[2,1024,128]{2,1,0:T(8,128)(2,1)S(1)} %get-tuple-element.25, s32[2,1024]{1,0:T(2,128)S(1)} %fusion.44), kind=kOutput, calls=%fused_computation.25 | convolution fusion | flops 1078460416 | bytes 4726784 | tf_op jit(solution)/shard_map/fmk,fkd->fmd/dot_general | solution.py:60
  63.8 3.3 %collective-permute-start.1 = (bf16[2,2,512,128]{3,2,1,0:T(8,128)(2,1)S(1)}, bf16[2,2,512,128]{3,2,1,0:T(8,128)(2,1)S(1)}, u32[]{:S(2)}, u32[]{:S(2)}) collective-permute-start(bf16[2,2,512,128]{3,2,1,0:T(8,128)(2,1)S(1)} %get-tuple-element.24), channel_id=1, source_target_pairs={{4,0},{8,4},{12,8},{16,12},{20,16},{24,20},{28,24},{0,28},{5,1},{9... | collective-permute-start | bytes 1572872 | tf_op jit(solution)/shard_map/ppermute | solution.py:23
  70.5 15.3 %collective-permute-done = bf16[2,2,512,128]{3,2,1,0:T(8,128)(2,1)S(1)} collective-permute-done((bf16[2,2,512,128]{3,2,1,0:T(8,128)(2,1)S(1)}, bf16[2,2,512,128]{3,2,1,0:T(8,128)(2,1)S(1)}, u32[]{:S(2)}, u32[]{:S(2)}) %collective-permute-start) | collective-permute-done | bytes 524320 | tf_op jit(solution)/shard_map/ppermute | solution.py:22
  88.0 3.9 %pad_maximum_fusion = (f32[2,8,512,128]{3,2,1,0:T(8,128)}, f32[2,8,512,128]{3,2,1,0:T(8,128)S(1)}, f32[2,8,512,128]{3,2,1,0:T(8,128)}) fusion(f32[2,2,512,128]{3,2,1,0:T(8,128)S(1)} %convert_element_type.85, f32[2,4,512,128]{3,2,1,0:T(8,128)S(1)} %bitcast.48, f32[2,2,512,128]{3,2,1,0:T(8,128)S(1)} %convert_element_type.84, f32[8,512,128]{2,1,0:T(8,128)S(1)} %bitcast.45, ...), kind=kLoop, calls=%fused_computation.11 | loop fusion | flops 4194304 | bytes 20971520 | tf_op jit(solution)/shard_map/concatenate | solution.py:24
  92.1 3.3 %fusion.48 = (f32[2,6,511,128]{3,2,1,0:T(8,128)}, f32[2,6,511,128]{3,2,1,0:T(8,128)}) fusion(f32[2,8,512,128]{3,2,1,0:T(8,128)S(1)} %get-tuple-element.7), kind=kLoop, calls=%fused_computation.97 | loop fusion | bytes 12558336 | tf_op jit(solution)/shard_map/jit(_roll_static)/slice | solution.py:82
  95.4 10.2 %broadcast_multiply_fusion.2 = (f32[2,6,512,128]{3,2,1,0:T(8,128)}, f32[2,6,512,128]{3,2,1,0:T(8,128)S(1)}) fusion(f32[6,512,128]{2,1,0:T(8,128)} %get-tuple-element.30, f32[6,512,128]{2,1,0:T(8,128)} %get-tuple-element.32, f32[2,8,512,128]{3,2,1,0:T(8,128)} %get-tuple-element.8, f32[2,6,512,128]{3,2,1,0:T(8,128)S(1)} %slice.216, ...), kind=kLoop, calls=%fused_computation.56 | loop fusion | flops 11796480 | bytes 36175872 | tf_op jit(solution)/shard_map/mul | solution.py:78
  106.7 2.2 %all_to_all.28 = bf16[2,4,65536]{2,1,0:T(4,128)(2,1)} reshape(bf16[2,4,512,128]{3,2,1,0:T(8,128)(2,1)} %slice.327) | data formatting | bytes 2097152 | tf_op jit(solution)/shard_map/all_to_all | solution.py:138
  109.0 3.3 %copy.15 = bf16[2,4,65536]{2,0,1:T(2,128)(2,1)} copy(bf16[2,4,65536]{2,1,0:T(4,128)(2,1)} %all_to_all.28) | data formatting | bytes 2097152 | tf_op jit(solution)/shard_map/all_to_all | solution.py:138
  112.2 4.2 %all-to-all-start.1 = ((bf16[2,4,65536]{2,0,1:T(2,128)(2,1)}), bf16[2,4,65536]{2,0,1:T(2,128)(2,1)}, u32[]{:S(2)}, u32[]{:S(2)}) async-start(bf16[2,4,65536]{2,0,1:T(2,128)(2,1)} %copy.15), calls=%async_computation.1 | async-start | bytes 2097152 | tf_op jit(solution)/shard_map/all_to_all | solution.py:138
  120.8 3.2 %fusion.45 = (bf16[2,4,512,128]{3,2,1,0:T(8,128)(2,1)}, f32[2,4,512,128]{3,2,1,0:T(8,128)}) fusion(f32[4,512,128]{2,1,0:T(8,128)S(1)} %copy-done.6, f32[2,6,512,128]{3,2,1,0:T(8,128)S(1)} %copy-done, f32[2,4,512,128]{3,2,1,0:T(8,128)S(1)} %slice.230, f32[2,4,511,128]{3,2,1,0:T(8,128)S(1)} %get-tuple-element.18, f32[2,4,1,128]{3,2,1,0:T(1,128)S(1)} %get-tuple-element.20, ...), kind=kLoop, calls=%fused_computation.96 | loop fusion | flops 7864320 | bytes 22020096 | tf_op jit(solution)/shard_map/convert_element_type | solution.py:137
  127.5 3.5 %all-to-all-done.1 = bf16[2,4,65536]{2,0,1:T(2,128)(2,1)} async-done(((bf16[2,4,65536]{2,0,1:T(2,128)(2,1)}), bf16[2,4,65536]{2,0,1:T(2,128)(2,1)}, u32[]{:S(2)}, u32[]{:S(2)}) %all-to-all-start.1) | async-done | bytes 1048608 | tf_op jit(solution)/shard_map/all_to_all | solution.py:138
  131.0 3.5 %all-to-all-start.2 = ((bf16[2,4,65536]{2,0,1:T(2,128)(2,1)}), bf16[2,4,65536]{2,0,1:T(2,128)(2,1)S(1)}, u32[]{:S(2)}, u32[]{:S(2)}) async-start(bf16[2,4,65536]{2,0,1:T(2,128)(2,1)} %copy.16), calls=%async_computation.2 | async-start | bytes 2097152 | tf_op jit(solution)/shard_map/all_to_all | solution.py:138
  134.5 2.6 %stack.21 = bf16[1,8,65536]{2,1,0:T(8,128)(2,1)} reshape(bf16[4,2,65536]{2,1,0:T(2,128)(2,1)} %bitcast.15) | data formatting | bytes 2097152 | tf_op jit(solution)/shard_map/stack | solution.py:146
  138.4 10.5 %all-to-all-done.2 = bf16[2,4,65536]{2,0,1:T(2,128)(2,1)S(1)} async-done(((bf16[2,4,65536]{2,0,1:T(2,128)(2,1)}), bf16[2,4,65536]{2,0,1:T(2,128)(2,1)S(1)}, u32[]{:S(2)}, u32[]{:S(2)}) %all-to-all-start.2) | async-done | bytes 1048608 | tf_op jit(solution)/shard_map/all_to_all | solution.py:138
  157.3 3.2 %collective-permute-done.5 = f32[8,8]{1,0:T(8,128)S(1)} collective-permute-done((f32[8,8]{1,0:T(8,128)S(1)}, f32[8,8]{1,0:T(8,128)S(1)}, u32[]{:S(2)}, u32[]{:S(2)}) %collective-permute-start.5) | collective-permute-done | bytes 288 | tf_op jit(solution)/shard_map/ppermute | solution.py:94
  160.9 3.2 %collective-permute-done.6 = f32[8,8]{1,0:T(8,128)S(1)} collective-permute-done((f32[8,8]{1,0:T(8,128)S(1)}, f32[8,8]{1,0:T(8,128)S(1)}, u32[]{:S(2)}, u32[]{:S(2)}) %collective-permute-start.6) | collective-permute-done | bytes 288 | tf_op jit(solution)/shard_map/ppermute | solution.py:94
  164.2 3.6 %collective-permute-done.7 = f32[8,8]{1,0:T(8,128)S(1)} collective-permute-done((f32[8,8]{1,0:T(8,128)S(1)}, f32[8,8]{1,0:T(8,128)S(1)}, u32[]{:S(2)}, u32[]{:S(2)}) %collective-permute-start.7) | collective-permute-done | bytes 288 | tf_op jit(solution)/shard_map/ppermute | solution.py:94
  168.5 3.8 %collective-permute-done.8 = f32[8,8]{1,0:T(8,128)S(1)} collective-permute-done((f32[8,8]{1,0:T(8,128)S(1)}, f32[8,8]{1,0:T(8,128)S(1)}, u32[]{:S(2)}, u32[]{:S(2)}) %collective-permute-start.8) | collective-permute-done | bytes 288 | tf_op jit(solution)/shard_map/ppermute | solution.py:94
  (84 shorter events, 42.5 us)
Async XLA Ops:
  0.6 4.8 %copy-start.11 = (s32[2,256,1]{1,2,0:T(1,128)S(1)}, s32[2,256,1]{1,2,0:T(1,128)}, u32[]{:S(2)}) copy-start(s32[2,256,1]{1,2,0:T(1,128)} %param.5) | copy-start | bytes 6148
  0.6 5.1 %copy-start.10 = (f32[2,256,128]{2,1,0:T(8,128)S(1)}, f32[2,256,128]{2,1,0:T(8,128)}, u32[]{:S(2)}) copy-start(f32[2,256,128]{2,1,0:T(8,128)} %param.7) | copy-start | bytes 786436
  2.4 15.1 %collective-permute-start.2 = (bf16[2,2,512,128]{3,2,1,0:T(8,128)(2,1)S(1)}, bf16[2,2,512,128]{3,2,1,0:T(8,128)(2,1)}, u32[]{:S(2)}, u32[]{:S(2)}) collective-permute-start(bf16[2,2,512,128]{3,2,1,0:T(8,128)(2,1)S(1)} %fusion.36), channel_id=1, source_target_pairs={{0,4},{1,29},{2,6},{3,31},{4,8},{5,1},{6,10},{7,3},{8,12},{9,5},{1... | collective-permute-start | bytes 1572872 | tf_op jit(solution)/shard_map/ppermute | solution.py:40
  6.7 1.3 copy-start.12
  17.5 8.7 %collective-permute-start.3 = (bf16[2,2,512,128]{3,2,1,0:T(8,128)(2,1)}, bf16[2,2,512,128]{3,2,1,0:T(8,128)(2,1)}, u32[]{:S(2)}, u32[]{:S(2)}) collective-permute-start(bf16[2,2,512,128]{3,2,1,0:T(8,128)(2,1)} %collective-permute-done.2), channel_id=1, source_target_pairs={{0,1},{1,0},{2,3},{3,2},{4,5},{5,4},{6,7},{7,6},{8,9},{9,8},{10,11... | collective-permute-start | bytes 1572872 | tf_op jit(solution)/shard_map/ppermute | solution.py:41
  19.0 33.8 %all-to-all-start = ((f32[2,8,129,128]{3,0,2,1:T(2,128)}), f32[2,8,129,128]{3,0,2,1:T(2,128)S(1)}, u32[]{:S(2)}, u32[]{:S(2)}) async-start(f32[2,8,129,128]{3,0,2,1:T(2,128)} %pad_maximum_fusion.2), calls=%async_computation | async-start | bytes 2113536 | tf_op jit(solution)/shard_map/all_to_all | solution.py:120
  26.1 1.5 copy-start.8
  26.1 1.9 %copy-start.9 = (f32[4,512,128]{2,1,0:T(8,128)S(1)}, f32[4,512,128]{2,1,0:T(8,128)}, u32[]{:S(2)}) copy-start(f32[4,512,128]{2,1,0:T(8,128)} %param.9) | copy-start | bytes 3145732
  30.2 1.3 copy-start.2
  30.2 2.0 %copy-start.4 = (f32[1,8,512,128]{3,2,1,0:T(8,128)}, f32[1,8,512,128]{3,2,1,0:T(8,128)S(1)}, u32[]{:S(2)}) copy-start(f32[1,8,512,128]{3,2,1,0:T(8,128)S(1)} %get-tuple-element.11) | copy-start | bytes 6291460
  62.1 5.1 %copy-start.3 = (f32[1,8,512,128]{3,2,1,0:T(8,128)S(1)}, f32[1,8,512,128]{3,2,1,0:T(8,128)}, u32[]{:S(2)}) copy-start(f32[1,8,512,128]{3,2,1,0:T(8,128)} %copy-done.2) | copy-start | bytes 6291460
  62.1 5.0 %copy-start.5 = (f32[1,8,512,128]{3,2,1,0:T(8,128)S(1)}, f32[1,8,512,128]{3,2,1,0:T(8,128)}, u32[]{:S(2)}) copy-start(f32[1,8,512,128]{3,2,1,0:T(8,128)} %copy-done.4) | copy-start | bytes 6291460
  62.3 23.4 %collective-permute-start = (bf16[2,2,512,128]{3,2,1,0:T(8,128)(2,1)S(1)}, bf16[2,2,512,128]{3,2,1,0:T(8,128)(2,1)S(1)}, u32[]{:S(2)}, u32[]{:S(2)}) collective-permute-start(bf16[2,2,512,128]{3,2,1,0:T(8,128)(2,1)S(1)} %get-tuple-element.23), channel_id=1, source_target_pairs={{0,4},{4,8},{8,12},{12,16},{16,20},{20,24},{24,28},{28,0},{1,5},{5... | collective-permute-start | bytes 1572872 | tf_op jit(solution)/shard_map/ppermute | solution.py:22
  63.8 4.8 %copy-start.1 = (f32[1,8,512,128]{3,2,1,0:T(8,128)S(1)}, f32[1,8,512,128]{3,2,1,0:T(8,128)}, u32[]{:S(2)}) copy-start(f32[1,8,512,128]{3,2,1,0:T(8,128)} %get-tuple-element.12) | copy-start | bytes 6291460
  63.8 24.1 %collective-permute-start.1 = (bf16[2,2,512,128]{3,2,1,0:T(8,128)(2,1)S(1)}, bf16[2,2,512,128]{3,2,1,0:T(8,128)(2,1)S(1)}, u32[]{:S(2)}, u32[]{:S(2)}) collective-permute-start(bf16[2,2,512,128]{3,2,1,0:T(8,128)(2,1)S(1)} %get-tuple-element.24), channel_id=1, source_target_pairs={{4,0},{8,4},{12,8},{16,12},{20,16},{24,20},{28,24},{0,28},{5,1},{9... | collective-permute-start | bytes 1572872 | tf_op jit(solution)/shard_map/ppermute | solution.py:23
  112.2 18.7 %all-to-all-start.1 = ((bf16[2,4,65536]{2,0,1:T(2,128)(2,1)}), bf16[2,4,65536]{2,0,1:T(2,128)(2,1)}, u32[]{:S(2)}, u32[]{:S(2)}) async-start(bf16[2,4,65536]{2,0,1:T(2,128)(2,1)} %copy.15), calls=%async_computation.1 | async-start | bytes 2097152 | tf_op jit(solution)/shard_map/all_to_all | solution.py:138
  118.5 2.0 %copy-start = (f32[2,6,512,128]{3,2,1,0:T(8,128)S(1)}, f32[2,6,512,128]{3,2,1,0:T(8,128)}, u32[]{:S(2)}) copy-start(f32[2,6,512,128]{3,2,1,0:T(8,128)} %get-tuple-element.4) | copy-start | bytes 9437188
  118.5 2.2 %copy-start.6 = (f32[4,512,128]{2,1,0:T(8,128)S(1)}, f32[4,512,128]{2,1,0:T(8,128)}, u32[]{:S(2)}) copy-start(f32[4,512,128]{2,1,0:T(8,128)} %get-tuple-element.34) | copy-start | bytes 3145732
  131.0 17.9 %all-to-all-start.2 = ((bf16[2,4,65536]{2,0,1:T(2,128)(2,1)}), bf16[2,4,65536]{2,0,1:T(2,128)(2,1)S(1)}, u32[]{:S(2)}, u32[]{:S(2)}) async-start(bf16[2,4,65536]{2,0,1:T(2,128)(2,1)} %copy.16), calls=%async_computation.2 | async-start | bytes 2097152 | tf_op jit(solution)/shard_map/all_to_all | solution.py:138
  155.8 1.2 collective-permute-start.4
  157.0 3.6 %collective-permute-start.5 = (f32[8,8]{1,0:T(8,128)S(1)}, f32[8,8]{1,0:T(8,128)S(1)}, u32[]{:S(2)}, u32[]{:S(2)}) collective-permute-start(f32[8,8]{1,0:T(8,128)S(1)} %add.115), channel_id=1, source_target_pairs={{0,2},{1,3},{2,0},{3,1},{4,6},{5,7},{6,4},{7,5},{8,10},{9,11},{10,... | collective-permute-start | bytes 776 | tf_op jit(solution)/shard_map/ppermute | solution.py:94
  160.6 3.6 %collective-permute-start.6 = (f32[8,8]{1,0:T(8,128)S(1)}, f32[8,8]{1,0:T(8,128)S(1)}, u32[]{:S(2)}, u32[]{:S(2)}) collective-permute-start(f32[8,8]{1,0:T(8,128)S(1)} %add.116), channel_id=1, source_target_pairs={{0,4},{4,0},{8,12},{12,8},{16,20},{20,16},{24,28},{28,24},{1,5},{5... | collective-permute-start | bytes 776 | tf_op jit(solution)/shard_map/ppermute | solution.py:94
  164.2 3.6 %collective-permute-start.7 = (f32[8,8]{1,0:T(8,128)S(1)}, f32[8,8]{1,0:T(8,128)S(1)}, u32[]{:S(2)}, u32[]{:S(2)}) collective-permute-start(f32[8,8]{1,0:T(8,128)S(1)} %add.117), channel_id=1, source_target_pairs={{0,8},{4,12},{8,0},{12,4},{16,24},{20,28},{24,16},{28,20},{1,9},{5... | collective-permute-start | bytes 776 | tf_op jit(solution)/shard_map/ppermute | solution.py:94
  167.8 4.5 %collective-permute-start.8 = (f32[8,8]{1,0:T(8,128)S(1)}, f32[8,8]{1,0:T(8,128)S(1)}, u32[]{:S(2)}, u32[]{:S(2)}) collective-permute-start(f32[8,8]{1,0:T(8,128)S(1)} %add.118), channel_id=1, source_target_pairs={{0,16},{4,20},{8,24},{12,28},{16,0},{20,4},{24,8},{28,12},{1,17},{... | collective-permute-start | bytes 776 | tf_op jit(solution)/shard_map/ppermute | solution.py:94
  (1 other events, 1.2 us)

commit v4 on v3

--- a/solution.py
+++ b/solution.py
@@ -55,10 +55,12 @@
 
 
 def select(onehot, values):
-    total = None
-    for part in pieces(values):
-        term = jnp.einsum("fmk,fkd->fmd", onehot, part, preferred_element_type=jnp.float32)
-        total = term if total is None else total + term
+    depth = values.shape[-1]
+    parts = pieces(values)
+    terms = jnp.einsum("fmk,fkd->fmd", onehot, jnp.concatenate(parts, axis=-1), preferred_element_type=jnp.float32)
+    total = terms[..., :depth]
+    for i in range(1, len(parts)):
+        total = total + terms[..., i * depth:(i + 1) * depth]
     return total
 
 
@@ -131,24 +133,26 @@
     weights = prepare(rim, adjoint)
     extended = padded(state, "space", STEPS, 1)
 
-    pieces_ = []
-
-    def record(current):
-        snap = current.astype(jnp.bfloat16).reshape(fields_dev, -1)
-        pieces_.append(lax.all_to_all(snap, "batch", split_axis=1, concat_axis=0, tiled=True))
-
+    share = lax.axis_size("batch")
+    cut = 1 if planes % share == 0 else 2
+    snaps = []
     for step in range(STEPS):
         extended = advance(extended, weights)
         weights = tuple(w[1:-1] for w in weights)
         width = STEPS - 1 - step
-        record(extended[:, width:extended.shape[1] - width])
+        snap = extended[:, width:extended.shape[1] - width].astype(jnp.bfloat16)
+        mixed = lax.all_to_all(snap, "batch", split_axis=cut, concat_axis=0, tiled=True)
+        snaps.append(mixed.reshape(mixed.shape[0], -1))
     state = extended
-    mixed = jnp.stack(pieces_)
-    actuated = mixed[:, :ACT].reshape(STEPS * ACT, -1)
-    sensed = mixed[:, ACT:].reshape(STEPS * SENS, -1)
-    partial_gram = lax.dot_general(
-        sensed, actuated, (((1,), (1,)), ((), ())), preferred_element_type=jnp.float32
-    )
+    rows = []
+    for sensed in snaps:
+        row = []
+        for actuated in snaps:
+            row.append(lax.dot_general(
+                sensed[ACT:ACT + SENS], actuated[:ACT], (((1,), (1,)), ((), ())), preferred_element_type=jnp.float32
+            ))
+        rows.append(jnp.concatenate(row, axis=1))
+    partial_gram = jnp.concatenate(rows, axis=0)
     scale = 4.0 / math.sqrt(planes * count * span * depth)
     gram = butterfly(partial_gram, ("batch", "space")) * scale
     return (state, gram)

time: 174 us -> 161 us (0.925)
  local copies, waits for them, and re-layouts: 31.5 us -> 15.3 us
  waiting for transfers between devices: 74 us -> 79.1 us
  matrix products: 11 us -> 9.17 us
    all_to_all x4 -> x0, local copies, waits for them, and re-layouts: 9 us -> none  [record(): lax.all_to_all(snap, 'batch', split_axis=1, concat_axis=0, tiled=True)]
    all_to_all x2, waiting for transfers between devices: 14 us -> 20.1 us  [body(): lax.all_to_all(snap, 'batch', split_axis=cut, concat_axis=0, tiled=True)]
    another operation x3 -> x0, local copies, waits for them, and re-layouts: 5.27 us -> none  [body(): mixed = jnp.stack(pieces_)]
    dot_general x7 -> x6, matrix products: 11 us -> 9.17 us  [the longest x2 5.22 us: select(): jnp.einsum('fmk,fkd->fmd', onehot, jnp.concatenate(parts, axis=-1), prefe...]
    reshape x2 -> x0, local copies, waits for them, and re-layouts: 1.76 us -> none  [the longest x1 1.49 us: body(): actuated = mixed[:, :ACT].reshape(STEPS * ACT, -1)]
    unnamed x28 -> x30, local copies, waits for them, and re-layouts: 5.77 us -> 5.89 us
  transfers between devices with their start and end apart: 12 -> 12, of which waited for: 11 -> 11; matrix products, arithmetic and copies ran while one was open for 14% -> 13% of each run, Pallas kernels for 0% -> 0%
where the time goes in v4:
time: 161 us; the launch traced here: 160 us
  waiting for transfers between devices  79.1 us (49%)
  other arithmetic  31.7 us (20%)
  starting transfers between devices  24.2 us (15%)
  local copies, waits for them, and re-layouts  15.3 us (10%)
  matrix products  9.17 us (6%)
    all_to_all x2, waiting for transfers between devices, body(): lax.all_to_all(snap, 'batch', split_axis=cut, concat_axis=0, tiled=True)  20.1 us
    all_to_all x1, waiting for transfers between devices, body(): lax.all_to_all(payload, 'space', split_axis=1, concat_axis=1, tiled=True)  18.6 us
    ppermute x1, waiting for transfers between devices, padded(): before = lax.ppermute(last, axis, up).astype(value.dtype)  15.2 us
    ppermute x5, waiting for transfers between devices, butterfly(): value = value + lax.ppermute(value, axis, [(i, i ^ step) for i in range(n)])  13.5 us
    mul x1, other arithmetic, advance(): moved = pre_dx * extended  10.2 us
    ppermute x1, waiting for transfers between devices, padded_shared(): lax.ppermute(jnp.where(odd, initial, last).astype(LINK), ('space', 'batch...  9.53 us
    all_to_all x2, starting transfers between devices, body(): lax.all_to_all(snap, 'batch', split_axis=cut, concat_axis=0, tiled=True)  7.76 us
    all_to_all x1, starting transfers between devices, body(): lax.all_to_all(payload, 'space', split_axis=1, concat_axis=1, tiled=True)  7.14 us
  transfers between devices with their start and end apart: 12, of which 11 were waited for; matrix products, arithmetic and copies ran while one was open for 13% of the time, Pallas kernels for 0%

profile of v4, /device:TPU:0, one launch (start us, length us, event | category | flops | bytes accessed | tf_op | source)
XLA Modules:
  0.0 160.5 jit_solution(1599343013788772842)
XLA Ops:
  0.7 1.7 %fusion.31 = bf16[2,2,512,128]{3,2,1,0:T(8,128)(2,1)S(1)} fusion(f32[1,4,512,128]{3,2,1,0:T(8,128)} %bitcast.78, f32[1,4,512,128]{3,2,1,0:T(8,128)} %bitcast.80, pred[]{:T(512)S(6)} %eq.41), kind=kLoop, calls=%fused_computation.68 | loop fusion | flops 786432 | bytes 2621441 | tf_op jit(solution)/shard_map/convert_element_type | solution.py:40
  2.4 3.0 %collective-permute-start.2 = (bf16[2,2,512,128]{3,2,1,0:T(8,128)(2,1)S(1)}, bf16[2,2,512,128]{3,2,1,0:T(8,128)(2,1)}, u32[]{:S(2)}, u32[]{:S(2)}) collective-permute-start(bf16[2,2,512,128]{3,2,1,0:T(8,128)(2,1)S(1)} %fusion.31), channel_id=1, source_target_pairs={{0,4},{1,29},{2,6},{3,31},{4,8},{5,1},{6,10},{7,3},{8,12},{9,5},{1... | collective-permute-start | bytes 1572872 | tf_op jit(solution)/shard_map/ppermute | solution.py:40
  7.9 9.5 %collective-permute-done.2 = bf16[2,2,512,128]{3,2,1,0:T(8,128)(2,1)} collective-permute-done((bf16[2,2,512,128]{3,2,1,0:T(8,128)(2,1)S(1)}, bf16[2,2,512,128]{3,2,1,0:T(8,128)(2,1)}, u32[]{:S(2)}, u32[]{:S(2)}) %collective-permute-start.2) | collective-permute-done | bytes 524320 | tf_op jit(solution)/shard_map/ppermute | solution.py:40
  19.0 7.1 %all-to-all-start = ((f32[2,8,129,128]{3,0,2,1:T(2,128)}), f32[2,8,129,128]{3,0,2,1:T(2,128)S(1)}, u32[]{:S(2)}, u32[]{:S(2)}) async-start(f32[2,8,129,128]{3,0,2,1:T(2,128)} %pad_maximum_fusion.2), calls=%async_computation | async-start | bytes 2113536 | tf_op jit(solution)/shard_map/all_to_all | solution.py:122
  28.3 1.9 %slice_select_fusion.2 = (f32[1,8,512,128]{3,2,1,0:T(8,128)S(1)}, f32[1,8,512,128]{3,2,1,0:T(8,128)S(1)}, f32[1,8,512,128]{3,2,1,0:T(8,128)S(1)}, f32[1,8,512,128]{3,2,1,0:T(8,128)}) fusion(f32[2,8,512,128]{3,2,1,0:T(8,128)S(1)} %pad_maximum_fusion.1, pred[]{:T(512)S(6)} %ge.12), kind=kLoop, calls=%fused_computation.44 | loop fusion | flops 2621440 | bytes 12582913 | tf_op jit(solution)/shard_map/jit(_where)/select_n | solution.py:71
  32.2 1.9 %fusion.21 = (f32[6,512,128]{2,1,0:T(8,128)}, f32[6,512,128]{2,1,0:T(8,128)}) fusion(f32[1,8,512,128]{3,2,1,0:T(8,128)S(1)} %get-tuple-element.15, f32[1,8,512,128]{3,2,1,0:T(8,128)S(1)} %get-tuple-element.13), kind=kLoop, calls=%fused_computation.48 | loop fusion | flops 393216 | bytes 6291456 | tf_op jit(solution)/shard_map/mul | solution.py:88
  34.1 18.6 %all-to-all-done = f32[2,8,129,128]{3,0,2,1:T(2,128)S(1)} async-done(((f32[2,8,129,128]{3,0,2,1:T(2,128)}), f32[2,8,129,128]{3,0,2,1:T(2,128)S(1)}, u32[]{:S(2)}, u32[]{:S(2)}) %all-to-all-start) | async-done | bytes 1056800 | tf_op jit(solution)/shard_map/all_to_all | solution.py:122
  53.2 4.5 %fusion = f32[2,2048,384]{2,1,0:T(8,128)S(1)} fusion(s32[2,1024]{1,0:T(2,128)S(1)} %fusion.61, bf16[2,1024,128]{2,1,0:T(8,128)(2,1)S(1)} %get-tuple-element.32, bf16[2,1024,128]{2,1,0:T(8,128)(2,1)S(1)} %get-tuple-element.33, bf16[2,1024,128]{2,1,0:T(8,128)(2,1)S(1)} %get-tuple-element.31), kind=kOutput, calls=%fused_computation.1 | convolution fusion | flops 3230138368 | bytes 7872512 | tf_op jit(solution)/shard_map/fmk,fkd->fmd/dot_general | solution.py:60
  59.6 3.3 %collective-permute-start.1 = (bf16[2,2,512,128]{3,2,0,1:T(8,128)(2,1)S(1)}, bf16[2,2,512,128]{3,2,0,1:T(8,128)(2,1)S(1)}, u32[]{:S(2)}, u32[]{:S(2)}) collective-permute-start(bf16[2,2,512,128]{3,2,0,1:T(8,128)(2,1)S(1)} %get-tuple-element.30), channel_id=1, source_target_pairs={{4,0},{8,4},{12,8},{16,12},{20,16},{24,20},{28,24},{0,28},{5,1},{9... | collective-permute-start | bytes 1572872 | tf_op jit(solution)/shard_map/ppermute | solution.py:23
  64.5 1.9 %slice_bitcast_fusion = (f32[6,512,128]{2,1,0:T(8,128)}, f32[6,512,128]{2,1,0:T(8,128)}) fusion(f32[1,8,512,128]{3,2,1,0:T(8,128)S(1)} %copy-done.1, f32[1,8,512,128]{3,2,1,0:T(8,128)S(1)} %get-tuple-element.14), kind=kLoop, calls=%fused_computation.45 | loop fusion | bytes 6291456 | tf_op jit(solution)/shard_map/slice | solution.py:141
  66.3 15.2 %collective-permute-done = bf16[2,2,512,128]{3,2,0,1:T(8,128)(2,1)S(1)} collective-permute-done((bf16[2,2,512,128]{3,2,0,1:T(8,128)(2,1)S(1)}, bf16[2,2,512,128]{3,2,0,1:T(8,128)(2,1)S(1)}, u32[]{:S(2)}, u32[]{:S(2)}) %collective-permute-start) | collective-permute-done | bytes 524320 | tf_op jit(solution)/shard_map/ppermute | solution.py:22
  81.7 2.1 %collective-permute-done.1 = bf16[2,2,512,128]{3,2,0,1:T(8,128)(2,1)S(1)} collective-permute-done((bf16[2,2,512,128]{3,2,0,1:T(8,128)(2,1)S(1)}, bf16[2,2,512,128]{3,2,0,1:T(8,128)(2,1)S(1)}, u32[]{:S(2)}, u32[]{:S(2)}) %collective-permute-start.1) | collective-permute-done | bytes 524320 | tf_op jit(solution)/shard_map/ppermute | solution.py:23
  83.9 3.8 %pad_maximum_fusion = (f32[2,8,512,128]{3,2,0,1:T(8,128)}, f32[2,8,512,128]{3,2,0,1:T(8,128)S(1)}, f32[2,8,512,128]{3,2,0,1:T(8,128)}) fusion(f32[2,2,512,128]{3,2,0,1:T(8,128)S(1)} %convert_element_type.85, f32[2,2,512,128]{3,2,0,1:T(8,128)S(1)} %convert_element_type.84, f32[8,512,128]{2,1,0:T(8,128)S(1)} %bitcast.72, f32[8,512,128]{2,1,0:T(8,128)S(1)} %bitcast.73, ...), kind=kLoop, calls=%fused_computation.7 | loop fusion | flops 4194304 | bytes 20971520 | tf_op jit(solution)/shard_map/concatenate | solution.py:24
  87.9 3.3 %fusion.67 = (f32[2,6,511,128]{3,2,0,1:T(8,128)}, f32[2,6,511,128]{3,2,0,1:T(8,128)}) fusion(f32[2,8,512,128]{3,2,0,1:T(8,128)S(1)} %get-tuple-element.11), kind=kLoop, calls=%fused_computation.121 | loop fusion | bytes 12558336 | tf_op jit(solution)/shard_map/jit(_roll_static)/slice | solution.py:84
  91.2 10.2 %broadcast_multiply_fusion.2 = (f32[2,6,512,128]{3,2,0,1:T(8,128)}, f32[2,6,512,128]{3,2,0,1:T(8,128)S(1)}) fusion(f32[6,512,128]{2,1,0:T(8,128)} %get-tuple-element.39, f32[6,512,128]{2,1,0:T(8,128)} %get-tuple-element.41, f32[2,8,512,128]{3,2,0,1:T(8,128)} %get-tuple-element.12, f32[2,6,512,128]{3,2,0,1:T(8,128)S(1)} %slice.274, ...), kind=kLoop, calls=%fused_computation.55 | loop fusion | flops 11796480 | bytes 36175872 | tf_op jit(solution)/shard_map/mul | solution.py:80
  102.6 4.2 %all-to-all-start.1 = ((bf16[2,4,512,128]{3,2,0,1:T(8,128)(2,1)}), bf16[2,4,512,128]{3,2,0,1:T(8,128)(2,1)}, u32[]{:S(2)}, u32[]{:S(2)}) async-start(bf16[2,4,512,128]{3,2,0,1:T(8,128)(2,1)} %slice.397), calls=%async_computation.1 | async-start | bytes 2097152 | tf_op jit(solution)/shard_map/all_to_all | solution.py:144
  111.1 3.2 %fusion.64 = (bf16[2,4,512,128]{3,2,0,1:T(8,128)(2,1)}, f32[2,4,512,128]{3,2,0,1:T(8,128)}) fusion(f32[4,512,128]{2,1,0:T(8,128)S(1)} %copy-done.7, f32[2,6,512,128]{3,2,0,1:T(8,128)S(1)} %copy-done, f32[2,4,512,128]{3,2,0,1:T(8,128)S(1)} %slice.288, f32[2,4,511,128]{3,2,0,1:T(8,128)S(1)} %get-tuple-element.22, f32[2,4,1,128]{3,2,0,1:T(1,128)S(1)} %get-tuple-element.24, ...), kind=kLoop, calls=%fused_computation.120 | loop fusion | flops 7864320 | bytes 22020096 | tf_op jit(solution)/shard_map/convert_element_type | solution.py:143
  114.4 7.0 %all-to-all-done.1 = bf16[2,4,512,128]{3,2,0,1:T(8,128)(2,1)} async-done(((bf16[2,4,512,128]{3,2,0,1:T(8,128)(2,1)}), bf16[2,4,512,128]{3,2,0,1:T(8,128)(2,1)}, u32[]{:S(2)}, u32[]{:S(2)}) %all-to-all-start.1) | async-done | bytes 1048608 | tf_op jit(solution)/shard_map/all_to_all | solution.py:144
  121.3 3.5 %all-to-all-start.2 = ((bf16[2,4,512,128]{3,2,0,1:T(8,128)(2,1)}), bf16[2,4,512,128]{3,2,0,1:T(8,128)(2,1)S(1)}, u32[]{:S(2)}, u32[]{:S(2)}) async-start(bf16[2,4,512,128]{3,2,0,1:T(8,128)(2,1)} %get-tuple-element.6), calls=%async_computation.2 | async-start | bytes 2097152 | tf_op jit(solution)/shard_map/all_to_all | solution.py:144
  126.1 13.1 %all-to-all-done.2 = bf16[2,4,512,128]{3,2,0,1:T(8,128)(2,1)S(1)} async-done(((bf16[2,4,512,128]{3,2,0,1:T(8,128)(2,1)}), bf16[2,4,512,128]{3,2,0,1:T(8,128)(2,1)S(1)}, u32[]{:S(2)}, u32[]{:S(2)}) %all-to-all-start.2) | async-done | bytes 1048608 | tf_op jit(solution)/shard_map/all_to_all | solution.py:144
  144.9 3.2 %collective-permute-done.5 = f32[8,8]{1,0:T(8,128)S(1)} collective-permute-done((f32[8,8]{1,0:T(8,128)S(1)}, f32[8,8]{1,0:T(8,128)S(1)}, u32[]{:S(2)}, u32[]{:S(2)}) %collective-permute-start.5) | collective-permute-done | bytes 288 | tf_op jit(solution)/shard_map/ppermute | solution.py:96
  148.5 3.2 %collective-permute-done.6 = f32[8,8]{1,0:T(8,128)S(1)} collective-permute-done((f32[8,8]{1,0:T(8,128)S(1)}, f32[8,8]{1,0:T(8,128)S(1)}, u32[]{:S(2)}, u32[]{:S(2)}) %collective-permute-start.6) | collective-permute-done | bytes 288 | tf_op jit(solution)/shard_map/ppermute | solution.py:96
  151.8 3.6 %collective-permute-done.7 = f32[8,8]{1,0:T(8,128)S(1)} collective-permute-done((f32[8,8]{1,0:T(8,128)S(1)}, f32[8,8]{1,0:T(8,128)S(1)}, u32[]{:S(2)}, u32[]{:S(2)}) %collective-permute-start.7) | collective-permute-done | bytes 288 | tf_op jit(solution)/shard_map/ppermute | solution.py:96
  157.6 2.3 %collective-permute-done.8 = f32[8,8]{1,0:T(8,128)S(1)} collective-permute-done((f32[8,8]{1,0:T(8,128)S(1)}, f32[8,8]{1,0:T(8,128)S(1)}, u32[]{:S(2)}, u32[]{:S(2)}) %collective-permute-start.8) | collective-permute-done | bytes 288 | tf_op jit(solution)/shard_map/ppermute | solution.py:96
  (80 shorter events, 27.8 us)
Async XLA Ops:
  0.6 4.8 %copy-start.12 = (s32[2,256,1]{1,2,0:T(1,128)S(1)}, s32[2,256,1]{1,2,0:T(1,128)}, u32[]{:S(2)}) copy-start(s32[2,256,1]{1,2,0:T(1,128)} %param.5) | copy-start | bytes 6148
  0.6 5.1 %copy-start.11 = (f32[2,256,128]{2,1,0:T(8,128)S(1)}, f32[2,256,128]{2,1,0:T(8,128)}, u32[]{:S(2)}) copy-start(f32[2,256,128]{2,1,0:T(8,128)} %param.7) | copy-start | bytes 786436
  2.4 15.1 %collective-permute-start.2 = (bf16[2,2,512,128]{3,2,1,0:T(8,128)(2,1)S(1)}, bf16[2,2,512,128]{3,2,1,0:T(8,128)(2,1)}, u32[]{:S(2)}, u32[]{:S(2)}) collective-permute-start(bf16[2,2,512,128]{3,2,1,0:T(8,128)(2,1)S(1)} %fusion.31), channel_id=1, source_target_pairs={{0,4},{1,29},{2,6},{3,31},{4,8},{5,1},{6,10},{7,3},{8,12},{9,5},{1... | collective-permute-start | bytes 1572872 | tf_op jit(solution)/shard_map/ppermute | solution.py:40
  17.5 8.7 %collective-permute-start.3 = (bf16[2,2,512,128]{3,2,1,0:T(8,128)(2,1)}, bf16[2,2,512,128]{3,2,1,0:T(8,128)(2,1)}, u32[]{:S(2)}, u32[]{:S(2)}) collective-permute-start(bf16[2,2,512,128]{3,2,1,0:T(8,128)(2,1)} %collective-permute-done.2), channel_id=1, source_target_pairs={{0,1},{1,0},{2,3},{3,2},{4,5},{5,4},{6,7},{7,6},{8,9},{9,8},{10,11... | collective-permute-start | bytes 1572872 | tf_op jit(solution)/shard_map/ppermute | solution.py:41
  19.0 33.8 %all-to-all-start = ((f32[2,8,129,128]{3,0,2,1:T(2,128)}), f32[2,8,129,128]{3,0,2,1:T(2,128)S(1)}, u32[]{:S(2)}, u32[]{:S(2)}) async-start(f32[2,8,129,128]{3,0,2,1:T(2,128)} %pad_maximum_fusion.2), calls=%async_computation | async-start | bytes 2113536 | tf_op jit(solution)/shard_map/all_to_all | solution.py:122
  26.1 1.5 copy-start.9
  26.1 1.9 %copy-start.10 = (f32[4,512,128]{2,1,0:T(8,128)S(1)}, f32[4,512,128]{2,1,0:T(8,128)}, u32[]{:S(2)}) copy-start(f32[4,512,128]{2,1,0:T(8,128)} %param.9) | copy-start | bytes 3145732
  30.2 1.4 copy-start.2
  30.2 2.0 %copy-start.4 = (f32[1,8,512,128]{3,2,1,0:T(8,128)}, f32[1,8,512,128]{3,2,1,0:T(8,128)S(1)}, u32[]{:S(2)}) copy-start(f32[1,8,512,128]{3,2,1,0:T(8,128)S(1)} %get-tuple-element.15) | copy-start | bytes 6291460
  57.7 5.2 %copy-start.5 = (f32[1,8,512,128]{3,2,1,0:T(8,128)S(1)}, f32[1,8,512,128]{3,2,1,0:T(8,128)}, u32[]{:S(2)}) copy-start(f32[1,8,512,128]{3,2,1,0:T(8,128)} %copy-done.4) | copy-start | bytes 6291460
  58.0 4.9 %copy-start.3 = (f32[1,8,512,128]{3,2,1,0:T(8,128)S(1)}, f32[1,8,512,128]{3,2,1,0:T(8,128)}, u32[]{:S(2)}) copy-start(f32[1,8,512,128]{3,2,1,0:T(8,128)} %copy-done.2) | copy-start | bytes 6291460
  58.2 23.4 %collective-permute-start = (bf16[2,2,512,128]{3,2,0,1:T(8,128)(2,1)S(1)}, bf16[2,2,512,128]{3,2,0,1:T(8,128)(2,1)S(1)}, u32[]{:S(2)}, u32[]{:S(2)}) collective-permute-start(bf16[2,2,512,128]{3,2,0,1:T(8,128)(2,1)S(1)} %get-tuple-element.29), channel_id=1, source_target_pairs={{0,4},{4,8},{8,12},{12,16},{16,20},{20,24},{24,28},{28,0},{1,5},{5... | collective-permute-start | bytes 1572872 | tf_op jit(solution)/shard_map/ppermute | solution.py:22
  59.6 4.8 %copy-start.1 = (f32[1,8,512,128]{3,2,1,0:T(8,128)S(1)}, f32[1,8,512,128]{3,2,1,0:T(8,128)}, u32[]{:S(2)}) copy-start(f32[1,8,512,128]{3,2,1,0:T(8,128)} %get-tuple-element.16) | copy-start | bytes 6291460
  59.6 24.2 %collective-permute-start.1 = (bf16[2,2,512,128]{3,2,0,1:T(8,128)(2,1)S(1)}, bf16[2,2,512,128]{3,2,0,1:T(8,128)(2,1)S(1)}, u32[]{:S(2)}, u32[]{:S(2)}) collective-permute-start(bf16[2,2,512,128]{3,2,0,1:T(8,128)(2,1)S(1)} %get-tuple-element.30), channel_id=1, source_target_pairs={{4,0},{8,4},{12,8},{16,12},{20,16},{24,20},{28,24},{0,28},{5,1},{9... | collective-permute-start | bytes 1572872 | tf_op jit(solution)/shard_map/ppermute | solution.py:23
  102.6 18.7 %all-to-all-start.1 = ((bf16[2,4,512,128]{3,2,0,1:T(8,128)(2,1)}), bf16[2,4,512,128]{3,2,0,1:T(8,128)(2,1)}, u32[]{:S(2)}, u32[]{:S(2)}) async-start(bf16[2,4,512,128]{3,2,0,1:T(8,128)(2,1)} %slice.397), calls=%async_computation.1 | async-start | bytes 2097152 | tf_op jit(solution)/shard_map/all_to_all | solution.py:144
  108.9 2.0 %copy-start = (f32[2,6,512,128]{3,2,0,1:T(8,128)S(1)}, f32[2,6,512,128]{3,2,0,1:T(8,128)}, u32[]{:S(2)}) copy-start(f32[2,6,512,128]{3,2,0,1:T(8,128)} %get-tuple-element.8) | copy-start | bytes 9437188
  108.9 2.2 %copy-start.7 = (f32[4,512,128]{2,1,0:T(8,128)S(1)}, f32[4,512,128]{2,1,0:T(8,128)}, u32[]{:S(2)}) copy-start(f32[4,512,128]{2,1,0:T(8,128)} %get-tuple-element.43) | copy-start | bytes 3145732
  121.3 17.9 %all-to-all-start.2 = ((bf16[2,4,512,128]{3,2,0,1:T(8,128)(2,1)}), bf16[2,4,512,128]{3,2,0,1:T(8,128)(2,1)S(1)}, u32[]{:S(2)}, u32[]{:S(2)}) async-start(bf16[2,4,512,128]{3,2,0,1:T(8,128)(2,1)} %get-tuple-element.6), calls=%async_computation.2 | async-start | bytes 2097152 | tf_op jit(solution)/shard_map/all_to_all | solution.py:144
  141.3 14.8 %copy-start.6 = (f32[2,4,512,128]{3,2,0,1:T(8,128)S(1)}, f32[2,4,512,128]{3,2,0,1:T(8,128)}, u32[]{:S(2)}) copy-start(f32[2,4,512,128]{3,2,0,1:T(8,128)} %get-tuple-element.7) | copy-start | bytes 6291460
  143.4 1.2 collective-permute-start.4
  144.5 3.6 %collective-permute-start.5 = (f32[8,8]{1,0:T(8,128)S(1)}, f32[8,8]{1,0:T(8,128)S(1)}, u32[]{:S(2)}, u32[]{:S(2)}) collective-permute-start(f32[8,8]{1,0:T(8,128)S(1)} %add.115), channel_id=1, source_target_pairs={{0,2},{1,3},{2,0},{3,1},{4,6},{5,7},{6,4},{7,5},{8,10},{9,11},{10,... | collective-permute-start | bytes 776 | tf_op jit(solution)/shard_map/ppermute | solution.py:96
  148.2 3.6 %collective-permute-start.6 = (f32[8,8]{1,0:T(8,128)S(1)}, f32[8,8]{1,0:T(8,128)S(1)}, u32[]{:S(2)}, u32[]{:S(2)}) collective-permute-start(f32[8,8]{1,0:T(8,128)S(1)} %add.116), channel_id=1, source_target_pairs={{0,4},{4,0},{8,12},{12,8},{16,20},{20,16},{24,28},{28,24},{1,5},{5... | collective-permute-start | bytes 776 | tf_op jit(solution)/shard_map/ppermute | solution.py:96
  151.8 3.6 %collective-permute-start.7 = (f32[8,8]{1,0:T(8,128)S(1)}, f32[8,8]{1,0:T(8,128)S(1)}, u32[]{:S(2)}, u32[]{:S(2)}) collective-permute-start(f32[8,8]{1,0:T(8,128)S(1)} %add.117), channel_id=1, source_target_pairs={{0,8},{4,12},{8,0},{12,4},{16,24},{20,28},{24,16},{28,20},{1,9},{5... | collective-permute-start | bytes 776 | tf_op jit(solution)/shard_map/ppermute | solution.py:96
  155.4 4.5 %collective-permute-start.8 = (f32[8,8]{1,0:T(8,128)S(1)}, f32[8,8]{1,0:T(8,128)S(1)}, u32[]{:S(2)}, u32[]{:S(2)}) collective-permute-start(f32[8,8]{1,0:T(8,128)S(1)} %add.118), channel_id=1, source_target_pairs={{0,16},{4,20},{8,24},{12,28},{16,0},{20,4},{24,8},{28,12},{1,17},{... | collective-permute-start | bytes 776 | tf_op jit(solution)/shard_map/ppermute | solution.py:96
  (2 other events, 2.1 us)

commit v5 on v4

--- a/solution.py
+++ b/solution.py
@@ -3,6 +3,8 @@
 import jax
 import jax.numpy as jnp
 from jax import lax
+from jax.experimental import pallas as pl
+from jax.experimental.pallas import tpu as pltpu
 from jax.sharding import PartitionSpec as P
 
 STEPS = 2
@@ -13,21 +15,19 @@
 LINK = jnp.bfloat16
 
 
-def padded(value, axis, width, dim):
+def halos(value, axis, width, dim):
     peers, length = lax.axis_size(axis), value.shape[dim]
     up = [(i, (i + 1) % peers) for i in range(peers)]
     down = [(j, i) for i, j in up]
     last = lax.slice_in_dim(value, length - width, length, axis=dim).astype(LINK)
     initial = lax.slice_in_dim(value, 0, width, axis=dim).astype(LINK)
-    before = lax.ppermute(last, axis, up).astype(value.dtype)
-    after = lax.ppermute(initial, axis, down).astype(value.dtype)
-    return jnp.concatenate([before, value, after], axis=dim)
-
-
-def padded_shared(value, width, dim):
+    return lax.ppermute(last, axis, up), lax.ppermute(initial, axis, down)
+
+
+def halos_shared(value, width, dim):
     peers, pair = lax.axis_size("space"), lax.axis_size("batch")
     if pair % 2:
-        return padded(value, "space", width, dim)
+        return halos(value, "space", width, dim)
     length = value.shape[dim]
     odd = lax.axis_index("batch") % 2 == 1
     last = lax.slice_in_dim(value, length - width, length, axis=dim)
@@ -38,11 +38,117 @@
             ahead = (s + 1) % peers if b % 2 == 0 else (s - 1) % peers
             routes.append((s * pair + b, ahead * pair + b))
     got = lax.ppermute(jnp.where(odd, initial, last).astype(LINK), ("space", "batch"), routes)
-    other = lax.ppermute(got, "batch", [(b, b ^ 1) for b in range(pair)]).astype(value.dtype)
-    got = got.astype(value.dtype)
-    before = jnp.where(odd, other, got)
-    after = jnp.where(odd, got, other)
-    return jnp.concatenate([before, value, after], axis=dim)
+    other = lax.ppermute(got, "batch", [(b, b ^ 1) for b in range(pair)])
+    return jnp.where(odd, other, got), jnp.where(odd, got, other)
+
+
+ROWS = 8
+
+
+def stencil_kernel(flag_ref, x_ref, xb_ref, xa_ref, d_ref, v_ref, cb_ref, ca_ref, out_ref, s1_ref, s2_ref, mid_ref):
+    planes, span, depth = x_ref.shape[1], x_ref.shape[2], x_ref.shape[3]
+    halo = xb_ref.shape[1]
+    ext = planes + 2 * halo
+    tiles = span // ROWS
+    sub = lax.broadcasted_iota(jnp.int32, (ROWS, depth), 0)
+    lane = lax.broadcasted_iota(jnp.int32, (ROWS, depth), 1)
+
+    def rows(c):
+        return pl.ds(pl.multiple_of(c * ROWS, ROWS), ROWS)
+
+    def level0(k, c):
+        if k < halo:
+            return xb_ref[0, k, rows(c), :].astype(jnp.float32)
+        if k < halo + planes:
+            return x_ref[0, k - halo, rows(c), :]
+        return xa_ref[0, k - halo - planes, rows(c), :].astype(jnp.float32)
+
+    def level1(k, c):
+        return mid_ref[k - 1, rows(c), :]
+
+    def coef(which, k, c):
+        if k < halo:
+            return cb_ref[which, k, rows(c), :].astype(jnp.float32)
+        if k < halo + planes:
+            return (d_ref if which == 0 else v_ref)[k - halo, rows(c), :]
+        return ca_ref[which, k - halo - planes, rows(c), :].astype(jnp.float32)
+
+    def lap(m, zero, p, before, after):
+        total = p + m
+        up = jnp.where(sub == ROWS - 1, pltpu.roll(after, ROWS - 1, 0), pltpu.roll(zero, ROWS - 1, 0))
+        down = jnp.where(sub == 0, pltpu.roll(before, 1, 0), pltpu.roll(zero, 1, 0))
+        total = total + up + down
+        zu = jnp.where(lane == depth - 1, 0.0, pltpu.roll(zero, depth - 1, 1))
+        zd = jnp.where(lane == 0, 0.0, pltpu.roll(zero, 1, 1))
+        total = total + zu + zd
+        return total - 6.0 * zero
+
+    def update(load, k, c, adjoint):
+        prev, nxt = (c + tiles - 1) % tiles, (c + 1) % tiles
+        xm, x0, xp = load(k - 1, c), load(k, c), load(k + 1, c)
+        xbefore, xafter = load(k, prev), load(k, nxt)
+        if adjoint:
+            lifted = lap(coef(0, k - 1, c) * xm, coef(0, k, c) * x0, coef(0, k + 1, c) * xp,
+                         coef(0, k, prev) * xbefore, coef(0, k, nxt) * xafter)
+            slope = 0.5 * (coef(1, k + 1, c) * xp - coef(1, k - 1, c) * xm)
+            return x0 + lifted + slope
+        lifted = lap(xm, x0, xp, xbefore, xafter)
+        slope = 0.5 * (xp - xm)
+        return x0 + coef(0, k, c) * lifted - coef(1, k, c) * slope
+
+    def run(adjoint):
+        for k in range(1, ext - 1):
+            def first(c, carry, k=k):
+                value = update(level0, k, c, adjoint)
+                mid_ref[k - 1, rows(c), :] = value
+                if halo <= k < halo + planes:
+                    s1_ref[0, k - halo, rows(c), :] = value.astype(s1_ref.dtype)
+                return carry
+            lax.fori_loop(0, tiles, first, 0, unroll=2)
+        for k in range(halo, halo + planes):
+            def second(c, carry, k=k):
+                value = update(level1, k, c, adjoint)
+                out_ref[0, k - halo, rows(c), :] = value
+                s2_ref[0, k - halo, rows(c), :] = value.astype(s2_ref.dtype)
+                return carry
+            lax.fori_loop(0, tiles, second, 0, unroll=2)
+
+    @pl.when(flag_ref[0] == 0)
+    def _():
+        run(False)
+
+    @pl.when(flag_ref[0] != 0)
+    def _():
+        run(True)
+
+
+def two_steps(flag, state, before, after, diffusion, velocity, coef_before, coef_after):
+    fields, planes, span, depth = state.shape
+    halo = before.shape[1]
+    field_block = lambda n: pl.BlockSpec((1, n, span, depth), lambda f: (f, 0, 0, 0))
+    whole = lambda shape: pl.BlockSpec(shape, lambda f: (0,) * len(shape))
+    return pl.pallas_call(
+        stencil_kernel,
+        grid=(fields,),
+        in_specs=[
+            pl.BlockSpec(memory_space=pltpu.SMEM),
+            field_block(planes),
+            field_block(halo),
+            field_block(halo),
+            whole((planes, span, depth)),
+            whole((planes, span, depth)),
+            whole((2, halo, span, depth)),
+            whole((2, halo, span, depth)),
+        ],
+        out_specs=[field_block(planes), field_block(planes), field_block(planes)],
+        out_shape=[
+            jax.ShapeDtypeStruct(state.shape, jnp.float32),
+            jax.ShapeDtypeStruct(state.shape, jnp.bfloat16),
+            jax.ShapeDtypeStruct(state.shape, jnp.bfloat16),
+        ],
+        scratch_shapes=[pltpu.VMEM((planes + 2 * halo - 2, span, depth), jnp.float32)],
+        compiler_params=pltpu.CompilerParams(dimension_semantics=("arbitrary",)),
+    )(flag, state, before, after, diffusion, velocity, coef_before, coef_after)
 
 
 def pieces(x):
@@ -62,30 +168,6 @@
     for i in range(1, len(parts)):
         total = total + terms[..., i * depth:(i + 1) * depth]
     return total
-
-
-def prepare(coef, adjoint):
-    diff_c = coef[0]
-    vel_c = coef[1]
-    pre_lap = jnp.where(adjoint, diff_c, 1.0)
-    post_lap = jnp.where(adjoint, 1.0, diff_c)
-    pre_dx = jnp.where(adjoint, vel_c, 1.0)
-    post_dx = jnp.where(adjoint, 1.0, -vel_c)
-    return (pre_lap, post_lap, pre_dx, post_dx)
-
-
-def advance(extended, weights):
-    pre_lap, post_lap, pre_dx, post_dx = weights
-    lifted = pre_lap * extended
-    moved = pre_dx * extended
-    middle = lifted[:, 1:-1]
-    padded_z = jnp.pad(middle, ((0, 0), (0, 0), (0, 0), (1, 1)))
-    total = lifted[:, 2:] + lifted[:, :-2]
-    total = total + jnp.roll(middle, -1, 2) + jnp.roll(middle, 1, 2)
-    total = total + padded_z[..., 2:] + padded_z[..., :-2]
-    lapl = total - 6.0 * middle
-    slope = 0.5 * (moved[:, 2:] - moved[:, :-2])
-    return extended[:, 1:-1] + post_lap[1:-1] * lapl + post_dx[1:-1] * slope
 
 
 def butterfly(value, axes):
@@ -128,22 +210,17 @@
     state = select(place.astype(jnp.bfloat16), got_vals).reshape(fields_dev, planes, span, depth)
 
     adjoint = lax.axis_index("batch") >= lax.axis_size("batch") // 2
-    coef = jnp.stack([diffusion, velocity])
-    rim = padded_shared(coef, STEPS, 1)
-    weights = prepare(rim, adjoint)
-    extended = padded(state, "space", STEPS, 1)
+    flag = adjoint.astype(jnp.int32).reshape(1)
+    coef_before, coef_after = halos_shared(jnp.stack([diffusion, velocity]), STEPS, 1)
+    before, after = halos(state, "space", STEPS, 1)
+    state, snap1, snap2 = two_steps(flag, state, before, after, diffusion, velocity, coef_before, coef_after)
 
     share = lax.axis_size("batch")
     cut = 1 if planes % share == 0 else 2
     snaps = []
-    for step in range(STEPS):
-        extended = advance(extended, weights)
-        weights = tuple(w[1:-1] for w in weights)
-        width = STEPS - 1 - step
-        snap = extended[:, width:extended.shape[1] - width].astype(jnp.bfloat16)
+    for snap in (snap1, snap2):
         mixed = lax.all_to_all(snap, "batch", split_axis=cut, concat_axis=0, tiled=True)
         snaps.append(mixed.reshape(mixed.shape[0], -1))
-    state = extended
     rows = []
     for sensed in snaps:
         row = []

time: 161 us -> 193 us (1.20)
  Pallas kernels: 0 us -> 54.4 us
  other arithmetic: 31.7 us -> 7.36 us
  local copies, waits for them, and re-layouts: 15.3 us -> 7.19 us
  waiting for transfers between devices: 79.1 us -> 86 us
  starting transfers between devices: 24.2 us -> 27.2 us
    pallas_call x0 -> x1, Pallas kernels: none -> 54.4 us  [two_steps(): pl.pallas_call(stencil_kernel, grid=(fields,), in_specs=[pl.BlockSpec(mem...]
    ppermute x4, waiting for transfers between devices: 26.9 us -> 47.4 us  [the longest x1 25.5 us: halos_shared(): lax.ppermute(jnp.where(odd, initial, last).astype(LINK), ('space', 'batch...]
    all_to_all x1, waiting for transfers between devices: 18.6 us -> 0.01 us  [body(): lax.all_to_all(payload, 'space', split_axis=1, concat_axis=1, tiled=True)]
    mul x4 -> x0, other arithmetic: 15.3 us -> none  [the longest x1 10.2 us: advance(): moved = pre_dx * extended]
    all_to_all x2, waiting for transfers between devices: 20.1 us -> 27.5 us  [body(): lax.all_to_all(snap, 'batch', split_axis=cut, concat_axis=0, tiled=True)]
    slice x9 -> x1, local copies, waits for them, and re-layouts: 7.13 us -> 0.07 us  [halos(): initial = lax.slice_in_dim(value, 0, width, axis=dim).astype(LINK)]
    convert_element_type x4 -> x1, other arithmetic: 5.08 us -> 0.14 us  [halos_shared(): jnp.where(odd, initial, last).astype(LINK)]
    concatenate x2 -> x0, other arithmetic: 4.13 us -> none  [the longest x1 3.84 us: padded(): return jnp.concatenate([before, value, after], axis=dim)]
  transfers between devices with their start and end apart: 12 -> 12, of which waited for: 11 -> 10; matrix products, arithmetic and copies ran while one was open for 13% -> 4% of each run, Pallas kernels for 0% -> 0%
where the time goes in v5:
time: 193 us; the launch traced here: 192 us
  waiting for transfers between devices  86 us (45%)
  Pallas kernels  54.4 us (28%)
  starting transfers between devices  27.2 us (14%)
  matrix products  9.16 us (5%)
  other arithmetic  7.36 us (4%)
  local copies, waits for them, and re-layouts  7.19 us (4%)
    pallas_call x1, Pallas kernels, two_steps(): pl.pallas_call(stencil_kernel, grid=(fields,), in_specs=[pl.BlockSpec(mem...  54.4 us
    all_to_all x2, waiting for transfers between devices, body(): lax.all_to_all(snap, 'batch', split_axis=cut, concat_axis=0, tiled=True)  27.5 us
    ppermute x1, waiting for transfers between devices, halos_shared(): lax.ppermute(jnp.where(odd, initial, last).astype(LINK), ('space', 'batch...  25.5 us
    ppermute x2, waiting for transfers between devices, halos(): return (lax.ppermute(last, axis, up), lax.ppermute(initial, axis, down))  21.9 us
    ppermute x5, waiting for transfers between devices, butterfly(): value = value + lax.ppermute(value, axis, [(i, i ^ step) for i in range(n)])  11.1 us
    all_to_all x1, starting transfers between devices, body(): lax.all_to_all(payload, 'space', split_axis=1, concat_axis=1, tiled=True)  7.28 us
    all_to_all x2, starting transfers between devices, body(): lax.all_to_all(snap, 'batch', split_axis=cut, concat_axis=0, tiled=True)  7.21 us
    ppermute x5, starting transfers between devices, butterfly(): value = value + lax.ppermute(value, axis, [(i, i ^ step) for i in range(n)])  5.35 us
  transfers between devices with their start and end apart: 12, of which 10 were waited for; matrix products, arithmetic and copies ran while one was open for 4% of the time, Pallas kernels for 0%

profile of v5, /device:TPU:0, one launch (start us, length us, event | category | flops | bytes accessed | tf_op | source)
XLA Modules:
  0.0 192.2 jit_solution(366234257132637773)
XLA Ops:
  6.2 1.5 pad_maximum_fusion
  7.6 7.3 %all-to-all-start = ((f32[2,8,129,128]{3,0,2,1:T(2,128)}), f32[2,8,129,128]{3,0,2,1:T(2,128)S(1)}, u32[]{:S(2)}, u32[]{:S(2)}) async-start(f32[2,8,129,128]{3,0,2,1:T(2,128)} %pad_maximum_fusion), calls=%async_computation | async-start | bytes 2113536 | tf_op jit(solution)/shard_map/all_to_all | solution.py:204
  15.1 2.1 %collective-permute-start.2 = (bf16[2,2,512,128]{3,2,1,0:T(8,128)(2,1)S(1)}, bf16[2,2,512,128]{3,2,1,0:T(8,128)(2,1)S(1)}, u32[]{:S(2)}, u32[]{:S(2)}) collective-permute-start(bf16[2,2,512,128]{3,2,1,0:T(8,128)(2,1)S(1)} %fusion.12), channel_id=1, source_target_pairs={{0,4},{1,29},{2,6},{3,31},{4,8},{5,1},{6,10},{7,3},{8,12},{9,5},{1... | collective-permute-start | bytes 1572872 | tf_op jit(solution)/shard_map/ppermute | solution.py:40
  17.2 25.5 %collective-permute-done.2 = bf16[2,2,512,128]{3,2,1,0:T(8,128)(2,1)S(1)} collective-permute-done((bf16[2,2,512,128]{3,2,1,0:T(8,128)(2,1)S(1)}, bf16[2,2,512,128]{3,2,1,0:T(8,128)(2,1)S(1)}, u32[]{:S(2)}, u32[]{:S(2)}) %collective-permute-start.2) | collective-permute-done | bytes 524320 | tf_op jit(solution)/shard_map/ppermute | solution.py:40
  43.1 4.5 %fusion = f32[2,2048,384]{2,1,0:T(8,128)S(1)} fusion(s32[2,1024]{1,0:T(2,128)S(1)} %fusion.41, bf16[2,1024,128]{2,1,0:T(8,128)(2,1)S(1)} %get-tuple-element.17, bf16[2,1024,128]{2,1,0:T(8,128)(2,1)S(1)} %get-tuple-element.18, bf16[2,1024,128]{2,1,0:T(8,128)(2,1)S(1)} %get-tuple-element.16), kind=kOutput, calls=%fused_computation.1 | convolution fusion | flops 3230138368 | bytes 7872512 | tf_op jit(solution)/shard_map/fmk,fkd->fmd/dot_general | solution.py:166
  48.2 1.1 copy-done
  49.2 5.3 %collective-permute-start = (bf16[2,2,512,128]{3,2,1,0:T(8,128)(2,1)S(1)}, bf16[2,2,512,128]{3,2,1,0:T(8,128)(2,1)S(1)}, u32[]{:S(2)}, u32[]{:S(2)}) collective-permute-start(bf16[2,2,512,128]{3,2,1,0:T(8,128)(2,1)S(1)} %get-tuple-element.15), channel_id=1, source_target_pairs={{0,4},{4,8},{8,12},{12,16},{16,20},{20,24},{24,28},{28,0},{1,5},{5... | collective-permute-start | bytes 1572872 | tf_op jit(solution)/shard_map/ppermute | solution.py:24
  54.5 1.1 broadcast_select_fusion
  55.6 20.6 %collective-permute-done.xb_ref = bf16[2,2,512,128]{3,2,1,0:T(8,128)(2,1)S(1)} collective-permute-done((bf16[2,2,512,128]{3,2,1,0:T(8,128)(2,1)S(1)}, bf16[2,2,512,128]{3,2,1,0:T(8,128)(2,1)S(1)}, u32[]{:S(2)}, u32[]{:S(2)}) %collective-permute-start) | collective-permute-done | bytes 524320 | tf_op jit(solution)/shard_map/ppermute | solution.py:24
  76.2 1.3 collective-permute-done.1.xa_ref
  78.3 54.4 %shard_map.68 = (f32[2,4,512,128]{3,2,1,0:T(8,128)}, bf16[2,4,512,128]{3,2,1,0:T(8,128)(2,1)}, bf16[2,4,512,128]{3,2,1,0:T(8,128)(2,1)}) custom-call(s32[1]{0:T(128)} %bitcast.flag_ref, f32[2,4,512,128]{3,2,1,0:T(8,128)} %bitcast.60, bf16[2,2,512,128]{3,2,1,0:T(8,128)(2,1)} %copy-done.4, bf16[2,2,512,128]{3,2,1,0:T(8,128)(2,1)} %copy-done.5, ...), custom_call_target="tpu_custom_call" | custom-call | tf_op jit(solution)/shard_map/pallas_call | solution.py:130
  132.7 2.4 %copy.18 = bf16[2,4,512,128]{3,2,0,1:T(8,128)(2,1)} copy(bf16[2,4,512,128]{3,2,1,0:T(8,128)(2,1)} %get-tuple-element.7) | data formatting | bytes 2097152 | tf_op jit(solution)/shard_map/pallas_call | solution.py:130
  135.1 3.5 %all-to-all-start.2 = ((bf16[2,4,512,128]{3,2,0,1:T(8,128)(2,1)}), bf16[2,4,512,128]{3,2,0,1:T(8,128)(2,1)S(1)}, u32[]{:S(2)}, u32[]{:S(2)}) async-start(bf16[2,4,512,128]{3,2,0,1:T(8,128)(2,1)} %copy.18), calls=%async_computation.2 | async-start | bytes 2097152 | tf_op jit(solution)/shard_map/all_to_all | solution.py:222
  138.6 1.0 copy.17
  139.7 13.3 %all-to-all-done.2 = bf16[2,4,512,128]{3,2,0,1:T(8,128)(2,1)S(1)} async-done(((bf16[2,4,512,128]{3,2,0,1:T(8,128)(2,1)}), bf16[2,4,512,128]{3,2,0,1:T(8,128)(2,1)S(1)}, u32[]{:S(2)}, u32[]{:S(2)}) %all-to-all-start.2) | async-done | bytes 1048608 | tf_op jit(solution)/shard_map/all_to_all | solution.py:222
  153.0 3.7 %all-to-all-start.1 = ((bf16[2,4,512,128]{3,2,0,1:T(8,128)(2,1)}), bf16[2,4,512,128]{3,2,0,1:T(8,128)(2,1)S(1)}, u32[]{:S(2)}, u32[]{:S(2)}) async-start(bf16[2,4,512,128]{3,2,0,1:T(8,128)(2,1)} %copy.17), calls=%async_computation.1 | async-start | bytes 2097152 | tf_op jit(solution)/shard_map/all_to_all | solution.py:222
  156.8 14.1 %all-to-all-done.1 = bf16[2,4,512,128]{3,2,0,1:T(8,128)(2,1)S(1)} async-done(((bf16[2,4,512,128]{3,2,0,1:T(8,128)(2,1)}), bf16[2,4,512,128]{3,2,0,1:T(8,128)(2,1)S(1)}, u32[]{:S(2)}, u32[]{:S(2)}) %all-to-all-start.1) | async-done | bytes 1048608 | tf_op jit(solution)/shard_map/all_to_all | solution.py:222
  175.1 1.2 collective-permute-done.4
  176.6 3.2 %collective-permute-done.5 = f32[8,8]{1,0:T(8,128)S(1)} collective-permute-done((f32[8,8]{1,0:T(8,128)S(1)}, f32[8,8]{1,0:T(8,128)S(1)}, u32[]{:S(2)}, u32[]{:S(2)}) %collective-permute-start.5) | collective-permute-done | bytes 288 | tf_op jit(solution)/shard_map/ppermute | solution.py:178
  179.8 1.4 collective-permute-start.6
  181.2 2.2 %collective-permute-done.6 = f32[8,8]{1,0:T(8,128)S(1)} collective-permute-done((f32[8,8]{1,0:T(8,128)S(1)}, f32[8,8]{1,0:T(8,128)S(1)}, u32[]{:S(2)}, u32[]{:S(2)}) %collective-permute-start.6) | collective-permute-done | bytes 288 | tf_op jit(solution)/shard_map/ppermute | solution.py:178
  184.4 2.7 %collective-permute-done.7 = f32[8,8]{1,0:T(8,128)S(1)} collective-permute-done((f32[8,8]{1,0:T(8,128)S(1)}, f32[8,8]{1,0:T(8,128)S(1)}, u32[]{:S(2)}, u32[]{:S(2)}) %collective-permute-start.7) | collective-permute-done | bytes 288 | tf_op jit(solution)/shard_map/ppermute | solution.py:178
  187.1 2.7 %collective-permute-start.8 = (f32[8,8]{1,0:T(8,128)S(1)}, f32[8,8]{1,0:T(8,128)S(1)}, u32[]{:S(2)}, u32[]{:S(2)}) collective-permute-start(f32[8,8]{1,0:T(8,128)S(1)} %add.58), channel_id=1, source_target_pairs={{0,16},{4,20},{8,24},{12,28},{16,0},{20,4},{24,8},{28,12},{1,17},{... | collective-permute-start | bytes 776 | tf_op jit(solution)/shard_map/ppermute | solution.py:178
  189.7 1.8 collective-permute-done.8
  (49 shorter events, 13.5 us)
Async XLA Ops:
  6.1 8.8 %copy-start.1 = (f32[4,512,128]{2,1,0:T(8,128)S(1)}, f32[4,512,128]{2,1,0:T(8,128)}, u32[]{:S(2)}) copy-start(f32[4,512,128]{2,1,0:T(8,128)} %d_ref.1) | copy-start | bytes 3145732
  6.2 8.8 %copy-start.2 = (f32[4,512,128]{2,1,0:T(8,128)S(1)}, f32[4,512,128]{2,1,0:T(8,128)}, u32[]{:S(2)}) copy-start(f32[4,512,128]{2,1,0:T(8,128)} %v_ref.1) | copy-start | bytes 3145732
  7.6 35.0 %all-to-all-start = ((f32[2,8,129,128]{3,0,2,1:T(2,128)}), f32[2,8,129,128]{3,0,2,1:T(2,128)S(1)}, u32[]{:S(2)}, u32[]{:S(2)}) async-start(f32[2,8,129,128]{3,0,2,1:T(2,128)} %pad_maximum_fusion), calls=%async_computation | async-start | bytes 2113536 | tf_op jit(solution)/shard_map/all_to_all | solution.py:204
  15.1 27.5 %collective-permute-start.2 = (bf16[2,2,512,128]{3,2,1,0:T(8,128)(2,1)S(1)}, bf16[2,2,512,128]{3,2,1,0:T(8,128)(2,1)S(1)}, u32[]{:S(2)}, u32[]{:S(2)}) collective-permute-start(bf16[2,2,512,128]{3,2,1,0:T(8,128)(2,1)S(1)} %fusion.12), channel_id=1, source_target_pairs={{0,4},{1,29},{2,6},{3,31},{4,8},{5,1},{6,10},{7,3},{8,12},{9,5},{1... | collective-permute-start | bytes 1572872 | tf_op jit(solution)/shard_map/ppermute | solution.py:40
  42.6 11.9 %collective-permute-start.3 = (bf16[2,2,512,128]{3,2,1,0:T(8,128)(2,1)S(1)}, bf16[2,2,512,128]{3,2,1,0:T(8,128)(2,1)S(1)}, u32[]{:S(2)}, u32[]{:S(2)}) collective-permute-start(bf16[2,2,512,128]{3,2,1,0:T(8,128)(2,1)S(1)} %collective-permute-done.2), channel_id=1, source_target_pairs={{0,1},{1,0},{2,3},{3,2},{4,5},{5,4},{6,7},{7,6},{8,9},{9,8},{10,11... | collective-permute-start | bytes 1572872 | tf_op jit(solution)/shard_map/ppermute | solution.py:41
  47.9 1.3 copy-start
  49.2 27.0 %collective-permute-start = (bf16[2,2,512,128]{3,2,1,0:T(8,128)(2,1)S(1)}, bf16[2,2,512,128]{3,2,1,0:T(8,128)(2,1)S(1)}, u32[]{:S(2)}, u32[]{:S(2)}) collective-permute-start(bf16[2,2,512,128]{3,2,1,0:T(8,128)(2,1)S(1)} %get-tuple-element.15), channel_id=1, source_target_pairs={{0,4},{4,8},{8,12},{12,16},{16,20},{20,24},{24,28},{28,0},{1,5},{5... | collective-permute-start | bytes 1572872 | tf_op jit(solution)/shard_map/ppermute | solution.py:24
  54.5 23.0 %collective-permute-start.1 = (bf16[2,2,512,128]{3,2,1,0:T(8,128)(2,1)S(1)}, bf16[2,2,512,128]{3,2,1,0:T(8,128)(2,1)S(1)}, u32[]{:S(2)}, u32[]{:S(2)}) collective-permute-start(bf16[2,2,512,128]{3,2,1,0:T(8,128)(2,1)S(1)} %get-tuple-element.14), channel_id=1, source_target_pairs={{4,0},{8,4},{12,8},{16,12},{20,16},{24,20},{28,24},{0,28},{5,1},{9... | collective-permute-start | bytes 1572872 | tf_op jit(solution)/shard_map/ppermute | solution.py:24
  76.2 1.3 copy-start.4
  77.5 0.8 copy-start.5
  132.7 5.9 %copy-start.3 = (bf16[2,4,512,128]{3,2,1,0:T(8,128)(2,1)S(1)}, bf16[2,4,512,128]{3,2,1,0:T(8,128)(2,1)}, u32[]{:S(2)}) copy-start(bf16[2,4,512,128]{3,2,1,0:T(8,128)(2,1)} %get-tuple-element.6) | copy-start | bytes 3145732
  135.1 17.9 %all-to-all-start.2 = ((bf16[2,4,512,128]{3,2,0,1:T(8,128)(2,1)}), bf16[2,4,512,128]{3,2,0,1:T(8,128)(2,1)S(1)}, u32[]{:S(2)}, u32[]{:S(2)}) async-start(bf16[2,4,512,128]{3,2,0,1:T(8,128)(2,1)} %copy.18), calls=%async_computation.2 | async-start | bytes 2097152 | tf_op jit(solution)/shard_map/all_to_all | solution.py:222
  153.0 17.9 %all-to-all-start.1 = ((bf16[2,4,512,128]{3,2,0,1:T(8,128)(2,1)}), bf16[2,4,512,128]{3,2,0,1:T(8,128)(2,1)S(1)}, u32[]{:S(2)}, u32[]{:S(2)}) async-start(bf16[2,4,512,128]{3,2,0,1:T(8,128)(2,1)} %copy.17), calls=%async_computation.1 | async-start | bytes 2097152 | tf_op jit(solution)/shard_map/all_to_all | solution.py:222
  175.1 1.2 collective-permute-start.4
  176.2 3.6 %collective-permute-start.5 = (f32[8,8]{1,0:T(8,128)S(1)}, f32[8,8]{1,0:T(8,128)S(1)}, u32[]{:S(2)}, u32[]{:S(2)}) collective-permute-start(f32[8,8]{1,0:T(8,128)S(1)} %add.55), channel_id=1, source_target_pairs={{0,2},{1,3},{2,0},{3,1},{4,6},{5,7},{6,4},{7,5},{8,10},{9,11},{10,... | collective-permute-start | bytes 776 | tf_op jit(solution)/shard_map/ppermute | solution.py:178
  179.8 3.6 %collective-permute-start.6 = (f32[8,8]{1,0:T(8,128)S(1)}, f32[8,8]{1,0:T(8,128)S(1)}, u32[]{:S(2)}, u32[]{:S(2)}) collective-permute-start(f32[8,8]{1,0:T(8,128)S(1)} %add.56), channel_id=1, source_target_pairs={{0,4},{4,0},{8,12},{12,8},{16,20},{20,16},{24,28},{28,24},{1,5},{5... | collective-permute-start | bytes 776 | tf_op jit(solution)/shard_map/ppermute | solution.py:178
  183.5 3.6 %collective-permute-start.7 = (f32[8,8]{1,0:T(8,128)S(1)}, f32[8,8]{1,0:T(8,128)S(1)}, u32[]{:S(2)}, u32[]{:S(2)}) collective-permute-start(f32[8,8]{1,0:T(8,128)S(1)} %add.57), channel_id=1, source_target_pairs={{0,8},{4,12},{8,0},{12,4},{16,24},{20,28},{24,16},{28,20},{1,9},{5... | collective-permute-start | bytes 776 | tf_op jit(solution)/shard_map/ppermute | solution.py:178
  187.1 4.5 %collective-permute-start.8 = (f32[8,8]{1,0:T(8,128)S(1)}, f32[8,8]{1,0:T(8,128)S(1)}, u32[]{:S(2)}, u32[]{:S(2)}) collective-permute-start(f32[8,8]{1,0:T(8,128)S(1)} %add.58), channel_id=1, source_target_pairs={{0,16},{4,20},{8,24},{12,28},{16,0},{20,4},{24,8},{28,12},{1,17},{... | collective-permute-start | bytes 776 | tf_op jit(solution)/shard_map/ppermute | solution.py:178

commit v6 on v5

--- a/solution.py
+++ b/solution.py
@@ -42,19 +42,20 @@
     return jnp.where(odd, other, got), jnp.where(odd, got, other)
 
 
-ROWS = 8
+ROWS = 256
 
 
 def stencil_kernel(flag_ref, x_ref, xb_ref, xa_ref, d_ref, v_ref, cb_ref, ca_ref, out_ref, s1_ref, s2_ref, mid_ref):
     planes, span, depth = x_ref.shape[1], x_ref.shape[2], x_ref.shape[3]
     halo = xb_ref.shape[1]
     ext = planes + 2 * halo
-    tiles = span // ROWS
-    sub = lax.broadcasted_iota(jnp.int32, (ROWS, depth), 0)
-    lane = lax.broadcasted_iota(jnp.int32, (ROWS, depth), 1)
+    block = math.gcd(span, ROWS)
+    tiles = span // block
+    sub = lax.broadcasted_iota(jnp.int32, (block, depth), 0)
+    lane = lax.broadcasted_iota(jnp.int32, (block, depth), 1)
 
     def rows(c):
-        return pl.ds(pl.multiple_of(c * ROWS, ROWS), ROWS)
+        return pl.ds(pl.multiple_of(c * block, block), block)
 
     def level0(k, c):
         if k < halo:
@@ -75,7 +76,7 @@
 
     def lap(m, zero, p, before, after):
         total = p + m
-        up = jnp.where(sub == ROWS - 1, pltpu.roll(after, ROWS - 1, 0), pltpu.roll(zero, ROWS - 1, 0))
+        up = jnp.where(sub == block - 1, pltpu.roll(after, block - 1, 0), pltpu.roll(zero, block - 1, 0))
         down = jnp.where(sub == 0, pltpu.roll(before, 1, 0), pltpu.roll(zero, 1, 0))
         total = total + up + down
         zu = jnp.where(lane == depth - 1, 0.0, pltpu.roll(zero, depth - 1, 1))

time: 193 us -> 146 us (0.76)
  Pallas kernels: 54.4 us -> 7.52 us
    pallas_call x1, Pallas kernels: 54.4 us -> 7.52 us  [two_steps(): pl.pallas_call(stencil_kernel, grid=(fields,), in_specs=[pl.BlockSpec(mem...]
  transfers between devices with their start and end apart: 12 -> 12, of which waited for: 10 -> 10; matrix products, arithmetic and copies ran while one was open for 4% -> 5% of each run, Pallas kernels for 0% -> 0%
where the time goes in v6:
time: 146 us; the launch traced here: 145 us
  waiting for transfers between devices  86.5 us (59%)
  starting transfers between devices  26.9 us (18%)
  matrix products  9.16 us (6%)
  Pallas kernels  7.52 us (5%)
  other arithmetic  7.36 us (5%)
  local copies, waits for them, and re-layouts  7.19 us (5%)
    all_to_all x2, waiting for transfers between devices, body(): lax.all_to_all(snap, 'batch', split_axis=cut, concat_axis=0, tiled=True)  27.8 us
    ppermute x1, waiting for transfers between devices, halos_shared(): lax.ppermute(jnp.where(odd, initial, last).astype(LINK), ('space', 'batch...  25.5 us
    ppermute x2, waiting for transfers between devices, halos(): return (lax.ppermute(last, axis, up), lax.ppermute(initial, axis, down))  21.9 us
    ppermute x5, waiting for transfers between devices, butterfly(): value = value + lax.ppermute(value, axis, [(i, i ^ step) for i in range(n)])  11.3 us
    pallas_call x1, Pallas kernels, two_steps(): pl.pallas_call(stencil_kernel, grid=(fields,), in_specs=[pl.BlockSpec(mem...  7.52 us
    all_to_all x1, starting transfers between devices, body(): lax.all_to_all(payload, 'space', split_axis=1, concat_axis=1, tiled=True)  7.28 us
    all_to_all x2, starting transfers between devices, body(): lax.all_to_all(snap, 'batch', split_axis=cut, concat_axis=0, tiled=True)  7.09 us
    ppermute x2, starting transfers between devices, halos(): return (lax.ppermute(last, axis, up), lax.ppermute(initial, axis, down))  5.27 us
  transfers between devices with their start and end apart: 12, of which 10 were waited for; matrix products, arithmetic and copies ran while one was open for 5% of the time, Pallas kernels for 0%

profile of v6, /device:TPU:0, one launch (start us, length us, event | category | flops | bytes accessed | tf_op | source)
XLA Modules:
  0.0 145.5 jit_solution(13163677984340826425)
XLA Ops:
  6.2 1.5 %pad_maximum_fusion = f32[2,8,129,128]{3,0,2,1:T(2,128)} fusion(f32[2,8,1,128]{3,0,2,1:T(2,128)S(1)} %convert_bitcast_fusion, f32[2,8,128,128]{3,0,2,1:T(2,128)S(1)} %copy.15), kind=kLoop, calls=%fused_computation.19 | loop fusion | flops 264192 | bytes 2113536 | tf_op jit(solution)/shard_map/concatenate | solution.py:201
  7.6 7.3 %all-to-all-start = ((f32[2,8,129,128]{3,0,2,1:T(2,128)}), f32[2,8,129,128]{3,0,2,1:T(2,128)S(1)}, u32[]{:S(2)}, u32[]{:S(2)}) async-start(f32[2,8,129,128]{3,0,2,1:T(2,128)} %pad_maximum_fusion), calls=%async_computation | async-start | bytes 2113536 | tf_op jit(solution)/shard_map/all_to_all | solution.py:205
  15.1 2.1 %collective-permute-start.2 = (bf16[2,2,512,128]{3,2,1,0:T(8,128)(2,1)S(1)}, bf16[2,2,512,128]{3,2,1,0:T(8,128)(2,1)S(1)}, u32[]{:S(2)}, u32[]{:S(2)}) collective-permute-start(bf16[2,2,512,128]{3,2,1,0:T(8,128)(2,1)S(1)} %fusion.12), channel_id=1, source_target_pairs={{0,4},{1,29},{2,6},{3,31},{4,8},{5,1},{6,10},{7,3},{8,12},{9,5},{1... | collective-permute-start | bytes 1572872 | tf_op jit(solution)/shard_map/ppermute | solution.py:40
  17.2 25.5 %collective-permute-done.2 = bf16[2,2,512,128]{3,2,1,0:T(8,128)(2,1)S(1)} collective-permute-done((bf16[2,2,512,128]{3,2,1,0:T(8,128)(2,1)S(1)}, bf16[2,2,512,128]{3,2,1,0:T(8,128)(2,1)S(1)}, u32[]{:S(2)}, u32[]{:S(2)}) %collective-permute-start.2) | collective-permute-done | bytes 524320 | tf_op jit(solution)/shard_map/ppermute | solution.py:40
  43.1 4.5 %fusion = f32[2,2048,384]{2,1,0:T(8,128)S(1)} fusion(s32[2,1024]{1,0:T(2,128)S(1)} %fusion.41, bf16[2,1024,128]{2,1,0:T(8,128)(2,1)S(1)} %get-tuple-element.17, bf16[2,1024,128]{2,1,0:T(8,128)(2,1)S(1)} %get-tuple-element.18, bf16[2,1024,128]{2,1,0:T(8,128)(2,1)S(1)} %get-tuple-element.16), kind=kOutput, calls=%fused_computation.1 | convolution fusion | flops 3230138368 | bytes 7872512 | tf_op jit(solution)/shard_map/fmk,fkd->fmd/dot_general | solution.py:167
  48.2 1.1 copy-done
  49.2 5.3 %collective-permute-start = (bf16[2,2,512,128]{3,2,1,0:T(8,128)(2,1)S(1)}, bf16[2,2,512,128]{3,2,1,0:T(8,128)(2,1)S(1)}, u32[]{:S(2)}, u32[]{:S(2)}) collective-permute-start(bf16[2,2,512,128]{3,2,1,0:T(8,128)(2,1)S(1)} %get-tuple-element.15), channel_id=1, source_target_pairs={{0,4},{4,8},{8,12},{12,16},{16,20},{20,24},{24,28},{28,0},{1,5},{5... | collective-permute-start | bytes 1572872 | tf_op jit(solution)/shard_map/ppermute | solution.py:24
  54.5 1.1 broadcast_select_fusion
  55.6 20.6 %collective-permute-done.xb_ref = bf16[2,2,512,128]{3,2,1,0:T(8,128)(2,1)S(1)} collective-permute-done((bf16[2,2,512,128]{3,2,1,0:T(8,128)(2,1)S(1)}, bf16[2,2,512,128]{3,2,1,0:T(8,128)(2,1)S(1)}, u32[]{:S(2)}, u32[]{:S(2)}) %collective-permute-start) | collective-permute-done | bytes 524320 | tf_op jit(solution)/shard_map/ppermute | solution.py:24
  76.2 1.3 collective-permute-done.1.xa_ref
  78.3 7.5 %shard_map.68 = (f32[2,4,512,128]{3,2,1,0:T(8,128)}, bf16[2,4,512,128]{3,2,1,0:T(8,128)(2,1)}, bf16[2,4,512,128]{3,2,1,0:T(8,128)(2,1)}) custom-call(s32[1]{0:T(128)} %bitcast.flag_ref, f32[2,4,512,128]{3,2,1,0:T(8,128)} %bitcast.60, bf16[2,2,512,128]{3,2,1,0:T(8,128)(2,1)} %copy-done.4, bf16[2,2,512,128]{3,2,1,0:T(8,128)(2,1)} %copy-done.5, ...), custom_call_target="tpu_custom_call" | custom-call | tf_op jit(solution)/shard_map/pallas_call | solution.py:131
  85.8 2.4 %copy.18 = bf16[2,4,512,128]{3,2,0,1:T(8,128)(2,1)} copy(bf16[2,4,512,128]{3,2,1,0:T(8,128)(2,1)} %get-tuple-element.7) | data formatting | bytes 2097152 | tf_op jit(solution)/shard_map/pallas_call | solution.py:131
  88.2 3.6 %all-to-all-start.2 = ((bf16[2,4,512,128]{3,2,0,1:T(8,128)(2,1)}), bf16[2,4,512,128]{3,2,0,1:T(8,128)(2,1)S(1)}, u32[]{:S(2)}, u32[]{:S(2)}) async-start(bf16[2,4,512,128]{3,2,0,1:T(8,128)(2,1)} %copy.18), calls=%async_computation.2 | async-start | bytes 2097152 | tf_op jit(solution)/shard_map/all_to_all | solution.py:223
  91.8 1.0 copy.17
  92.8 13.5 %all-to-all-done.2 = bf16[2,4,512,128]{3,2,0,1:T(8,128)(2,1)S(1)} async-done(((bf16[2,4,512,128]{3,2,0,1:T(8,128)(2,1)}), bf16[2,4,512,128]{3,2,0,1:T(8,128)(2,1)S(1)}, u32[]{:S(2)}, u32[]{:S(2)}) %all-to-all-start.2) | async-done | bytes 1048608 | tf_op jit(solution)/shard_map/all_to_all | solution.py:223
  106.3 3.5 %all-to-all-start.1 = ((bf16[2,4,512,128]{3,2,0,1:T(8,128)(2,1)}), bf16[2,4,512,128]{3,2,0,1:T(8,128)(2,1)S(1)}, u32[]{:S(2)}, u32[]{:S(2)}) async-start(bf16[2,4,512,128]{3,2,0,1:T(8,128)(2,1)} %copy.17), calls=%async_computation.1 | async-start | bytes 2097152 | tf_op jit(solution)/shard_map/all_to_all | solution.py:223
  109.9 14.3 %all-to-all-done.1 = bf16[2,4,512,128]{3,2,0,1:T(8,128)(2,1)S(1)} async-done(((bf16[2,4,512,128]{3,2,0,1:T(8,128)(2,1)}), bf16[2,4,512,128]{3,2,0,1:T(8,128)(2,1)S(1)}, u32[]{:S(2)}, u32[]{:S(2)}) %all-to-all-start.1) | async-done | bytes 1048608 | tf_op jit(solution)/shard_map/all_to_all | solution.py:223
  128.4 1.2 collective-permute-done.4
  129.9 3.2 %collective-permute-done.5 = f32[8,8]{1,0:T(8,128)S(1)} collective-permute-done((f32[8,8]{1,0:T(8,128)S(1)}, f32[8,8]{1,0:T(8,128)S(1)}, u32[]{:S(2)}, u32[]{:S(2)}) %collective-permute-start.5) | collective-permute-done | bytes 288 | tf_op jit(solution)/shard_map/ppermute | solution.py:179
  133.1 1.3 collective-permute-start.6
  134.4 2.3 %collective-permute-done.6 = f32[8,8]{1,0:T(8,128)S(1)} collective-permute-done((f32[8,8]{1,0:T(8,128)S(1)}, f32[8,8]{1,0:T(8,128)S(1)}, u32[]{:S(2)}, u32[]{:S(2)}) %collective-permute-start.6) | collective-permute-done | bytes 288 | tf_op jit(solution)/shard_map/ppermute | solution.py:179
  137.7 2.7 %collective-permute-done.7 = f32[8,8]{1,0:T(8,128)S(1)} collective-permute-done((f32[8,8]{1,0:T(8,128)S(1)}, f32[8,8]{1,0:T(8,128)S(1)}, u32[]{:S(2)}, u32[]{:S(2)}) %collective-permute-start.7) | collective-permute-done | bytes 288 | tf_op jit(solution)/shard_map/ppermute | solution.py:179
  140.3 2.6 %collective-permute-start.8 = (f32[8,8]{1,0:T(8,128)S(1)}, f32[8,8]{1,0:T(8,128)S(1)}, u32[]{:S(2)}, u32[]{:S(2)}) collective-permute-start(f32[8,8]{1,0:T(8,128)S(1)} %add.58), channel_id=1, source_target_pairs={{0,16},{4,20},{8,24},{12,28},{16,0},{20,4},{24,8},{28,12},{1,17},{... | collective-permute-start | bytes 776 | tf_op jit(solution)/shard_map/ppermute | solution.py:179
  142.9 1.9 %collective-permute-done.8 = f32[8,8]{1,0:T(8,128)S(1)} collective-permute-done((f32[8,8]{1,0:T(8,128)S(1)}, f32[8,8]{1,0:T(8,128)S(1)}, u32[]{:S(2)}, u32[]{:S(2)}) %collective-permute-start.8) | collective-permute-done | bytes 288 | tf_op jit(solution)/shard_map/ppermute | solution.py:179
  (49 shorter events, 13.5 us)
Async XLA Ops:
  6.1 8.8 %copy-start.1 = (f32[4,512,128]{2,1,0:T(8,128)S(1)}, f32[4,512,128]{2,1,0:T(8,128)}, u32[]{:S(2)}) copy-start(f32[4,512,128]{2,1,0:T(8,128)} %d_ref.1) | copy-start | bytes 3145732
  6.2 8.8 %copy-start.2 = (f32[4,512,128]{2,1,0:T(8,128)S(1)}, f32[4,512,128]{2,1,0:T(8,128)}, u32[]{:S(2)}) copy-start(f32[4,512,128]{2,1,0:T(8,128)} %v_ref.1) | copy-start | bytes 3145732
  7.6 35.0 %all-to-all-start = ((f32[2,8,129,128]{3,0,2,1:T(2,128)}), f32[2,8,129,128]{3,0,2,1:T(2,128)S(1)}, u32[]{:S(2)}, u32[]{:S(2)}) async-start(f32[2,8,129,128]{3,0,2,1:T(2,128)} %pad_maximum_fusion), calls=%async_computation | async-start | bytes 2113536 | tf_op jit(solution)/shard_map/all_to_all | solution.py:205
  15.1 27.5 %collective-permute-start.2 = (bf16[2,2,512,128]{3,2,1,0:T(8,128)(2,1)S(1)}, bf16[2,2,512,128]{3,2,1,0:T(8,128)(2,1)S(1)}, u32[]{:S(2)}, u32[]{:S(2)}) collective-permute-start(bf16[2,2,512,128]{3,2,1,0:T(8,128)(2,1)S(1)} %fusion.12), channel_id=1, source_target_pairs={{0,4},{1,29},{2,6},{3,31},{4,8},{5,1},{6,10},{7,3},{8,12},{9,5},{1... | collective-permute-start | bytes 1572872 | tf_op jit(solution)/shard_map/ppermute | solution.py:40
  42.6 11.9 %collective-permute-start.3 = (bf16[2,2,512,128]{3,2,1,0:T(8,128)(2,1)S(1)}, bf16[2,2,512,128]{3,2,1,0:T(8,128)(2,1)S(1)}, u32[]{:S(2)}, u32[]{:S(2)}) collective-permute-start(bf16[2,2,512,128]{3,2,1,0:T(8,128)(2,1)S(1)} %collective-permute-done.2), channel_id=1, source_target_pairs={{0,1},{1,0},{2,3},{3,2},{4,5},{5,4},{6,7},{7,6},{8,9},{9,8},{10,11... | collective-permute-start | bytes 1572872 | tf_op jit(solution)/shard_map/ppermute | solution.py:41
  47.9 1.3 copy-start
  49.2 27.0 %collective-permute-start = (bf16[2,2,512,128]{3,2,1,0:T(8,128)(2,1)S(1)}, bf16[2,2,512,128]{3,2,1,0:T(8,128)(2,1)S(1)}, u32[]{:S(2)}, u32[]{:S(2)}) collective-permute-start(bf16[2,2,512,128]{3,2,1,0:T(8,128)(2,1)S(1)} %get-tuple-element.15), channel_id=1, source_target_pairs={{0,4},{4,8},{8,12},{12,16},{16,20},{20,24},{24,28},{28,0},{1,5},{5... | collective-permute-start | bytes 1572872 | tf_op jit(solution)/shard_map/ppermute | solution.py:24
  54.5 23.0 %collective-permute-start.1 = (bf16[2,2,512,128]{3,2,1,0:T(8,128)(2,1)S(1)}, bf16[2,2,512,128]{3,2,1,0:T(8,128)(2,1)S(1)}, u32[]{:S(2)}, u32[]{:S(2)}) collective-permute-start(bf16[2,2,512,128]{3,2,1,0:T(8,128)(2,1)S(1)} %get-tuple-element.14), channel_id=1, source_target_pairs={{4,0},{8,4},{12,8},{16,12},{20,16},{24,20},{28,24},{0,28},{5,1},{9... | collective-permute-start | bytes 1572872 | tf_op jit(solution)/shard_map/ppermute | solution.py:24
  76.2 1.3 copy-start.4
  77.5 0.8 copy-start.5
  85.8 6.0 %copy-start.3 = (bf16[2,4,512,128]{3,2,1,0:T(8,128)(2,1)S(1)}, bf16[2,4,512,128]{3,2,1,0:T(8,128)(2,1)}, u32[]{:S(2)}) copy-start(bf16[2,4,512,128]{3,2,1,0:T(8,128)(2,1)} %get-tuple-element.6) | copy-start | bytes 3145732
  88.2 18.1 %all-to-all-start.2 = ((bf16[2,4,512,128]{3,2,0,1:T(8,128)(2,1)}), bf16[2,4,512,128]{3,2,0,1:T(8,128)(2,1)S(1)}, u32[]{:S(2)}, u32[]{:S(2)}) async-start(bf16[2,4,512,128]{3,2,0,1:T(8,128)(2,1)} %copy.18), calls=%async_computation.2 | async-start | bytes 2097152 | tf_op jit(solution)/shard_map/all_to_all | solution.py:223
  106.3 17.9 %all-to-all-start.1 = ((bf16[2,4,512,128]{3,2,0,1:T(8,128)(2,1)}), bf16[2,4,512,128]{3,2,0,1:T(8,128)(2,1)S(1)}, u32[]{:S(2)}, u32[]{:S(2)}) async-start(bf16[2,4,512,128]{3,2,0,1:T(8,128)(2,1)} %copy.17), calls=%async_computation.1 | async-start | bytes 2097152 | tf_op jit(solution)/shard_map/all_to_all | solution.py:223
  128.3 1.2 collective-permute-start.4
  129.5 3.6 %collective-permute-start.5 = (f32[8,8]{1,0:T(8,128)S(1)}, f32[8,8]{1,0:T(8,128)S(1)}, u32[]{:S(2)}, u32[]{:S(2)}) collective-permute-start(f32[8,8]{1,0:T(8,128)S(1)} %add.55), channel_id=1, source_target_pairs={{0,2},{1,3},{2,0},{3,1},{4,6},{5,7},{6,4},{7,5},{8,10},{9,11},{10,... | collective-permute-start | bytes 776 | tf_op jit(solution)/shard_map/ppermute | solution.py:179
  133.1 3.6 %collective-permute-start.6 = (f32[8,8]{1,0:T(8,128)S(1)}, f32[8,8]{1,0:T(8,128)S(1)}, u32[]{:S(2)}, u32[]{:S(2)}) collective-permute-start(f32[8,8]{1,0:T(8,128)S(1)} %add.56), channel_id=1, source_target_pairs={{0,4},{4,0},{8,12},{12,8},{16,20},{20,16},{24,28},{28,24},{1,5},{5... | collective-permute-start | bytes 776 | tf_op jit(solution)/shard_map/ppermute | solution.py:179
  136.7 3.6 %collective-permute-start.7 = (f32[8,8]{1,0:T(8,128)S(1)}, f32[8,8]{1,0:T(8,128)S(1)}, u32[]{:S(2)}, u32[]{:S(2)}) collective-permute-start(f32[8,8]{1,0:T(8,128)S(1)} %add.57), channel_id=1, source_target_pairs={{0,8},{4,12},{8,0},{12,4},{16,24},{20,28},{24,16},{28,20},{1,9},{5... | collective-permute-start | bytes 776 | tf_op jit(solution)/shard_map/ppermute | solution.py:179
  140.3 4.5 %collective-permute-start.8 = (f32[8,8]{1,0:T(8,128)S(1)}, f32[8,8]{1,0:T(8,128)S(1)}, u32[]{:S(2)}, u32[]{:S(2)}) collective-permute-start(f32[8,8]{1,0:T(8,128)S(1)} %add.58), channel_id=1, source_target_pairs={{0,16},{4,20},{8,24},{12,28},{16,0},{20,4},{24,8},{28,12},{1,17},{... | collective-permute-start | bytes 776 | tf_op jit(solution)/shard_map/ppermute | solution.py:179

commit v7 on v6

--- a/solution.py
+++ b/solution.py
@@ -45,10 +45,8 @@
 ROWS = 256
 
 
-def stencil_kernel(flag_ref, x_ref, xb_ref, xa_ref, d_ref, v_ref, cb_ref, ca_ref, out_ref, s1_ref, s2_ref, mid_ref):
+def stencil_parts(flag_ref, x_ref, xb_ref, xa_ref, d_ref, v_ref, cb_ref, ca_ref, halo):
     planes, span, depth = x_ref.shape[1], x_ref.shape[2], x_ref.shape[3]
-    halo = xb_ref.shape[1]
-    ext = planes + 2 * halo
     block = math.gcd(span, ROWS)
     tiles = span // block
     sub = lax.broadcasted_iota(jnp.int32, (block, depth), 0)
@@ -63,9 +61,6 @@
         if k < halo + planes:
             return x_ref[0, k - halo, rows(c), :]
         return xa_ref[0, k - halo - planes, rows(c), :].astype(jnp.float32)
-
-    def level1(k, c):
-        return mid_ref[k - 1, rows(c), :]
 
     def coef(which, k, c):
         if k < halo:
@@ -97,14 +92,52 @@
         slope = 0.5 * (xp - xm)
         return x0 + coef(0, k, c) * lifted - coef(1, k, c) * slope
 
+    def both(run):
+        @pl.when(flag_ref[0] == 0)
+        def _():
+            run(False)
+
+        @pl.when(flag_ref[0] != 0)
+        def _():
+            run(True)
+
+    return planes, tiles, rows, level0, update, both
+
+
+def interior_kernel(flag_ref, x_ref, d_ref, v_ref, s_ref):
+    halo = STEPS
+    planes, tiles, rows, level0, update, both = stencil_parts(
+        flag_ref, x_ref, None, None, d_ref, v_ref, None, None, halo)
+
+    def run(adjoint):
+        for k in range(halo + 1, halo + planes - 1):
+            def first(c, carry, k=k):
+                s_ref[0, k - halo - 1, rows(c), :] = update(level0, k, c, adjoint).astype(s_ref.dtype)
+                return carry
+
+            lax.fori_loop(0, tiles, first, 0, unroll=2)
+
+    both(run)
+
+
+def stencil_kernel(flag_ref, x_ref, xb_ref, xa_ref, d_ref, v_ref, cb_ref, ca_ref, out_ref, s1_ref, s2_ref, mid_ref):
+    halo = xb_ref.shape[1]
+    planes, tiles, rows, level0, update, both = stencil_parts(
+        flag_ref, x_ref, xb_ref, xa_ref, d_ref, v_ref, cb_ref, ca_ref, halo)
+    ext = planes + 2 * halo
+
+    def level1(k, c):
+        return mid_ref[k - 1, rows(c), :]
+
     def run(adjoint):
         for k in range(1, ext - 1):
             def first(c, carry, k=k):
                 value = update(level0, k, c, adjoint)
                 mid_ref[k - 1, rows(c), :] = value
-                if halo <= k < halo + planes:
-                    s1_ref[0, k - halo, rows(c), :] = value.astype(s1_ref.dtype)
+                if k == halo or k == halo + planes - 1:
+                    s1_ref[0, 0 if k == halo else 1, rows(c), :] = value.astype(s1_ref.dtype)
                 return carry
+
             lax.fori_loop(0, tiles, first, 0, unroll=2)
         for k in range(halo, halo + planes):
             def second(c, carry, k=k):
@@ -112,15 +145,27 @@
                 out_ref[0, k - halo, rows(c), :] = value
                 s2_ref[0, k - halo, rows(c), :] = value.astype(s2_ref.dtype)
                 return carry
+
             lax.fori_loop(0, tiles, second, 0, unroll=2)
 
-    @pl.when(flag_ref[0] == 0)
-    def _():
-        run(False)
-
-    @pl.when(flag_ref[0] != 0)
-    def _():
-        run(True)
+    both(run)
+
+
+def interior_step(flag, state, diffusion, velocity):
+    fields, planes, span, depth = state.shape
+    return pl.pallas_call(
+        interior_kernel,
+        grid=(fields,),
+        in_specs=[
+            pl.BlockSpec(memory_space=pltpu.SMEM),
+            pl.BlockSpec((1, planes, span, depth), lambda f: (f, 0, 0, 0)),
+            pl.BlockSpec((planes, span, depth), lambda f: (0, 0, 0)),
+            pl.BlockSpec((planes, span, depth), lambda f: (0, 0, 0)),
+        ],
+        out_specs=pl.BlockSpec((1, planes - 2, span, depth), lambda f: (f, 0, 0, 0)),
+        out_shape=jax.ShapeDtypeStruct((fields, planes - 2, span, depth), jnp.bfloat16),
+        compiler_params=pltpu.CompilerParams(dimension_semantics=("arbitrary",)),
+    )(flag, state, diffusion, velocity)
 
 
 def two_steps(flag, state, before, after, diffusion, velocity, coef_before, coef_after):
@@ -141,10 +186,10 @@
             whole((2, halo, span, depth)),
             whole((2, halo, span, depth)),
         ],
-        out_specs=[field_block(planes), field_block(planes), field_block(planes)],
+        out_specs=[field_block(planes), field_block(2), field_block(planes)],
         out_shape=[
             jax.ShapeDtypeStruct(state.shape, jnp.float32),
-            jax.ShapeDtypeStruct(state.shape, jnp.bfloat16),
+            jax.ShapeDtypeStruct((fields, 2, span, depth), jnp.bfloat16),
             jax.ShapeDtypeStruct(state.shape, jnp.bfloat16),
         ],
         scratch_shapes=[pltpu.VMEM((planes + 2 * halo - 2, span, depth), jnp.float32)],
@@ -181,7 +226,7 @@
     return value
 
 
-def body(owner, offset, profile, diffusion, velocity):
+def work(owner, offset, profile, diffusion, velocity):
     count = lax.axis_size("space")
     fields_dev, rows_dev = offset.shape
     planes, span, depth = diffusion.shape
@@ -213,15 +258,17 @@
     adjoint = lax.axis_index("batch") >= lax.axis_size("batch") // 2
     flag = adjoint.astype(jnp.int32).reshape(1)
     coef_before, coef_after = halos_shared(jnp.stack([diffusion, velocity]), STEPS, 1)
+    inner = interior_step(flag, state, diffusion, velocity)
     before, after = halos(state, "space", STEPS, 1)
-    state, snap1, snap2 = two_steps(flag, state, before, after, diffusion, velocity, coef_before, coef_after)
-
-    share = lax.axis_size("batch")
-    cut = 1 if planes % share == 0 else 2
-    snaps = []
-    for snap in (snap1, snap2):
-        mixed = lax.all_to_all(snap, "batch", split_axis=cut, concat_axis=0, tiled=True)
-        snaps.append(mixed.reshape(mixed.shape[0], -1))
+    state, outer, snap2 = two_steps(flag, state, before, after, diffusion, velocity, coef_before, coef_after)
+
+    def spread(snap):
+        return lax.all_to_all(snap, "batch", split_axis=2, concat_axis=0, tiled=True)
+
+    inner, outer = spread(inner), spread(outer)
+    first = jnp.concatenate([outer[:, :1], inner, outer[:, 1:]], axis=1)
+    second = spread(snap2)
+    snaps = [first.reshape(first.shape[0], -1), second.reshape(second.shape[0], -1)]
     rows = []
     for sensed in snaps:
         row = []
@@ -245,4 +292,4 @@
         P("space", None, None),
     )
     out_specs = (P("batch", "space", None, None), P())
-    return jax.shard_map(body, mesh=mesh, in_specs=in_specs, out_specs=out_specs, check_vma=False)
+    return jax.shard_map(work, mesh=mesh, in_specs=in_specs, out_specs=out_specs, check_vma=False)

time: 146 us -> 142 us (0.973)
  waiting for transfers between devices: 86.5 us -> 68.8 us
  local copies, waits for them, and re-layouts: 7.19 us -> 13.3 us
  starting transfers between devices: 26.9 us -> 30.7 us
  Pallas kernels: 7.52 us -> 10.8 us
    ppermute x2, waiting for transfers between devices: 21.9 us -> 12.6 us  [halos(): return (lax.ppermute(last, axis, up), lax.ppermute(initial, axis, down))]
    all_to_all x3 -> x4, waiting for transfers between devices: 27.8 us -> 19.5 us  [the longest x3 19.5 us: spread(): lax.all_to_all(snap, 'batch', split_axis=2, concat_axis=0, tiled=True)]
    all_to_all x3 -> x4, starting transfers between devices: 14.4 us -> 18 us  [the longest x3 10.7 us: spread(): lax.all_to_all(snap, 'batch', split_axis=2, concat_axis=0, tiled=True)]
    pallas_call x0 -> x1, Pallas kernels: none -> 3.38 us  [interior_step(): pl.pallas_call(interior_kernel, grid=(fields,), in_specs=[pl.BlockSpec(me...]
    pallas_call x0 -> x1, local copies, waits for them, and re-layouts: none -> 2.37 us  [interior_step(): pl.pallas_call(interior_kernel, grid=(fields,), in_specs=[pl.BlockSpec(me...]
    slice x4 -> x7, local copies, waits for them, and re-layouts: 0.31 us -> 2.26 us  [the longest x2 1.4 us: work(): got_vals = got[:, :, :cap].reshape(fields_dev, slots, depth)]
  transfers between devices with their start and end apart: 12 -> 13, of which waited for: 10 -> 10; matrix products, arithmetic and copies ran while one was open for 5% -> 13% of each run, Pallas kernels for 0% -> 8%
where the time goes in v7:
time: 142 us; the launch traced here: 141 us
  waiting for transfers between devices  68.8 us (48%)
  starting transfers between devices  30.7 us (22%)
  local copies, waits for them, and re-layouts  13.3 us (9%)
  Pallas kernels  10.8 us (8%)
  matrix products  8.41 us (6%)
  other arithmetic  8.17 us (6%)
    ppermute x1, waiting for transfers between devices, halos_shared(): lax.ppermute(jnp.where(odd, initial, last).astype(LINK), ('space', 'batch...  25.5 us
    all_to_all x3, waiting for transfers between devices, spread(): lax.all_to_all(snap, 'batch', split_axis=2, concat_axis=0, tiled=True)  19.5 us
    ppermute x2, waiting for transfers between devices, halos(): return (lax.ppermute(last, axis, up), lax.ppermute(initial, axis, down))  12.6 us
    ppermute x5, waiting for transfers between devices, butterfly(): value = value + lax.ppermute(value, axis, [(i, i ^ step) for i in range(n)])  11.2 us
    all_to_all x3, starting transfers between devices, spread(): lax.all_to_all(snap, 'batch', split_axis=2, concat_axis=0, tiled=True)  10.7 us
    pallas_call x1, Pallas kernels, two_steps(): pl.pallas_call(stencil_kernel, grid=(fields,), in_specs=[pl.BlockSpec(mem...  7.41 us
    all_to_all x1, starting transfers between devices, work(): lax.all_to_all(payload, 'space', split_axis=1, concat_axis=1, tiled=True)  7.28 us
    ppermute x2, starting transfers between devices, halos(): return (lax.ppermute(last, axis, up), lax.ppermute(initial, axis, down))  5.37 us
  transfers between devices with their start and end apart: 13, of which 10 were waited for; matrix products, arithmetic and copies ran while one was open for 13% of the time, Pallas kernels for 8%

profile of v7, /device:TPU:0, one launch (start us, length us, event | category | flops | bytes accessed | tf_op | source)
XLA Modules:
  0.0 141.1 jit_solution(3347898798440271448)
XLA Ops:
  6.2 1.5 %pad_maximum_fusion = f32[2,8,129,128]{3,0,2,1:T(2,128)} fusion(f32[2,8,1,128]{3,0,2,1:T(2,128)S(1)} %convert_bitcast_fusion, f32[2,8,128,128]{3,0,2,1:T(2,128)S(1)} %copy.20), kind=kLoop, calls=%fused_computation.20 | loop fusion | flops 264192 | bytes 2113536 | tf_op jit(solution)/shard_map/concatenate | solution.py:246
  7.6 7.3 %all-to-all-start = ((f32[2,8,129,128]{3,0,2,1:T(2,128)}), f32[2,8,129,128]{3,0,2,1:T(2,128)}, u32[]{:S(2)}, u32[]{:S(2)}) async-start(f32[2,8,129,128]{3,0,2,1:T(2,128)} %pad_maximum_fusion), calls=%async_computation | async-start | bytes 2113536 | tf_op jit(solution)/shard_map/all_to_all | solution.py:250
  15.1 2.1 %collective-permute-start.2 = (bf16[2,2,512,128]{3,2,1,0:T(8,128)(2,1)S(1)}, bf16[2,2,512,128]{3,2,1,0:T(8,128)(2,1)S(1)}, u32[]{:S(2)}, u32[]{:S(2)}) collective-permute-start(bf16[2,2,512,128]{3,2,1,0:T(8,128)(2,1)S(1)} %fusion.12), channel_id=1, source_target_pairs={{0,4},{1,29},{2,6},{3,31},{4,8},{5,1},{6,10},{7,3},{8,12},{9,5},{1... | collective-permute-start | bytes 1572872 | tf_op jit(solution)/shard_map/ppermute | solution.py:40
  17.1 25.5 %collective-permute-done.2 = bf16[2,2,512,128]{3,2,1,0:T(8,128)(2,1)S(1)} collective-permute-done((bf16[2,2,512,128]{3,2,1,0:T(8,128)(2,1)S(1)}, bf16[2,2,512,128]{3,2,1,0:T(8,128)(2,1)S(1)}, u32[]{:S(2)}, u32[]{:S(2)}) %collective-permute-start.2) | collective-permute-done | bytes 524320 | tf_op jit(solution)/shard_map/ppermute | solution.py:40
  42.6 1.3 slice.98
  45.0 4.5 %fusion = f32[2,2048,384]{2,1,0:T(8,128)S(1)} fusion(s32[2,1024]{1,0:T(2,128)S(1)} %fusion.21, bf16[2,1024,128]{2,1,0:T(8,128)(2,1)S(1)} %get-tuple-element.17, bf16[2,1024,128]{2,1,0:T(8,128)(2,1)S(1)} %get-tuple-element.18, bf16[2,1024,128]{2,1,0:T(8,128)(2,1)S(1)} %get-tuple-element.16), kind=kOutput, calls=%fused_computation.1 | convolution fusion | flops 3230138368 | bytes 7872512 | tf_op jit(solution)/shard_map/fmk,fkd->fmd/dot_general | solution.py:212
  51.3 5.4 %collective-permute-start = (bf16[2,2,512,128]{3,2,1,0:T(8,128)(2,1)}, bf16[2,2,512,128]{3,2,1,0:T(8,128)(2,1)S(1)}, u32[]{:S(2)}, u32[]{:S(2)}) collective-permute-start(bf16[2,2,512,128]{3,2,1,0:T(8,128)(2,1)} %get-tuple-element.15), channel_id=1, source_target_pairs={{0,4},{4,8},{8,12},{12,16},{16,20},{20,24},{24,28},{28,0},{1,5},{5... | collective-permute-start | bytes 1572872 | tf_op jit(solution)/shard_map/ppermute | solution.py:24
  56.7 3.4 %shard_map.69 = bf16[2,2,512,128]{3,2,1,0:T(8,128)(2,1)} custom-call(s32[1]{0:T(128)} %bitcast.flag_ref, f32[2,4,512,128]{3,2,1,0:T(8,128)} %bitcast.52, f32[4,512,128]{2,1,0:T(8,128)} %d_ref.3, f32[4,512,128]{2,1,0:T(8,128)} %v_ref.3), custom_call_target="tpu_custom_call" | custom-call | tf_op jit(solution)/shard_map/pallas_call | solution.py:156
  60.0 2.4 %copy.24 = bf16[2,2,512,128]{3,1,0,2:T(2,128)(2,1)} copy(bf16[2,2,512,128]{3,2,1,0:T(8,128)(2,1)} %shard_map.69) | data formatting | bytes 1048576 | tf_op jit(solution)/shard_map/pallas_call | solution.py:156
  62.4 3.6 %all-to-all-start.2 = ((bf16[2,2,512,128]{3,1,0,2:T(2,128)(2,1)}), bf16[2,2,512,128]{3,1,0,2:T(2,128)(2,1)S(1)}, u32[]{:S(2)}, u32[]{:S(2)}) async-start(bf16[2,2,512,128]{3,1,0,2:T(2,128)(2,1)} %copy.24), calls=%async_computation.2 | async-start | bytes 1048576 | tf_op jit(solution)/shard_map/all_to_all | solution.py:266
  67.2 11.5 %collective-permute-done.xb_ref = bf16[2,2,512,128]{3,2,1,0:T(8,128)(2,1)S(1)} collective-permute-done((bf16[2,2,512,128]{3,2,1,0:T(8,128)(2,1)}, bf16[2,2,512,128]{3,2,1,0:T(8,128)(2,1)S(1)}, u32[]{:S(2)}, u32[]{:S(2)}) %collective-permute-start) | collective-permute-done | bytes 524320 | tf_op jit(solution)/shard_map/ppermute | solution.py:24
  80.6 7.4 %shard_map.68 = (f32[2,4,512,128]{3,2,1,0:T(8,128)}, bf16[2,2,512,128]{3,2,1,0:T(8,128)(2,1)}, bf16[2,4,512,128]{3,2,1,0:T(8,128)(2,1)}) custom-call(s32[1]{0:T(128)} %bitcast.flag_ref, f32[2,4,512,128]{3,2,1,0:T(8,128)} %bitcast.53, bf16[2,2,512,128]{3,2,1,0:T(8,128)(2,1)} %copy-done.4, bf16[2,2,512,128]{3,2,1,0:T(8,128)(2,1)} %copy-done.5, ...), custom_call_target="tpu_custom_call" | custom-call | tf_op jit(solution)/shard_map/pallas_call | solution.py:176
  88.0 2.5 %copy.22 = bf16[2,2,512,128]{3,1,0,2:T(2,128)(2,1)} copy(bf16[2,2,512,128]{3,2,1,0:T(8,128)(2,1)} %get-tuple-element.6) | data formatting | bytes 1048576 | tf_op jit(solution)/shard_map/pallas_call | solution.py:176
  90.5 3.6 %all-to-all-start.1 = ((bf16[2,2,512,128]{3,1,0,2:T(2,128)(2,1)}), bf16[2,2,512,128]{3,1,0,2:T(2,128)(2,1)S(1)}, u32[]{:S(2)}, u32[]{:S(2)}) async-start(bf16[2,2,512,128]{3,1,0,2:T(2,128)(2,1)} %copy.22), calls=%async_computation.1 | async-start | bytes 1048576 | tf_op jit(solution)/shard_map/all_to_all | solution.py:266
  94.3 1.8 %copy.26 = bf16[2,4,512,128]{3,1,0,2:T(4,128)(2,1)} copy(bf16[2,4,512,128]{3,2,1,0:T(8,128)(2,1)S(1)} %copy-done.3) | data formatting | bytes 2097152 | tf_op jit(solution)/shard_map/pallas_call | solution.py:176
  96.1 6.8 %all-to-all-done.1 = bf16[2,2,512,128]{3,1,0,2:T(2,128)(2,1)S(1)} async-done(((bf16[2,2,512,128]{3,1,0,2:T(2,128)(2,1)}), bf16[2,2,512,128]{3,1,0,2:T(2,128)(2,1)S(1)}, u32[]{:S(2)}, u32[]{:S(2)}) %all-to-all-start.1) | async-done | bytes 524320 | tf_op jit(solution)/shard_map/all_to_all | solution.py:266
  102.9 3.5 %all-to-all-start.3 = ((bf16[2,4,512,128]{3,1,0,2:T(4,128)(2,1)}), bf16[2,4,512,128]{3,1,0,2:T(4,128)(2,1)S(1)}, u32[]{:S(2)}, u32[]{:S(2)}) async-start(bf16[2,4,512,128]{3,1,0,2:T(4,128)(2,1)} %copy.26), calls=%async_computation.3 | async-start | bytes 2097152 | tf_op jit(solution)/shard_map/all_to_all | solution.py:266
  108.1 12.7 %all-to-all-done.3 = bf16[2,4,512,128]{3,1,0,2:T(4,128)(2,1)S(1)} async-done(((bf16[2,4,512,128]{3,1,0,2:T(4,128)(2,1)}), bf16[2,4,512,128]{3,1,0,2:T(4,128)(2,1)S(1)}, u32[]{:S(2)}, u32[]{:S(2)}) %all-to-all-start.3) | async-done | bytes 1048608 | tf_op jit(solution)/shard_map/all_to_all | solution.py:266
  125.6 3.2 %collective-permute-done.5 = f32[8,8]{1,0:T(8,128)S(1)} collective-permute-done((f32[8,8]{1,0:T(8,128)S(1)}, f32[8,8]{1,0:T(8,128)S(1)}, u32[]{:S(2)}, u32[]{:S(2)}) %collective-permute-start.5) | collective-permute-done | bytes 288 | tf_op jit(solution)/shard_map/ppermute | solution.py:224
  128.8 1.4 %collective-permute-start.6 = (f32[8,8]{1,0:T(8,128)S(1)}, f32[8,8]{1,0:T(8,128)S(1)}, u32[]{:S(2)}, u32[]{:S(2)}) collective-permute-start(f32[8,8]{1,0:T(8,128)S(1)} %add.56), channel_id=1, source_target_pairs={{0,4},{4,0},{8,12},{12,8},{16,20},{20,16},{24,28},{28,24},{1,5},{5... | collective-permute-start | bytes 776 | tf_op jit(solution)/shard_map/ppermute | solution.py:224
  130.2 2.2 %collective-permute-done.6 = f32[8,8]{1,0:T(8,128)S(1)} collective-permute-done((f32[8,8]{1,0:T(8,128)S(1)}, f32[8,8]{1,0:T(8,128)S(1)}, u32[]{:S(2)}, u32[]{:S(2)}) %collective-permute-start.6) | collective-permute-done | bytes 288 | tf_op jit(solution)/shard_map/ppermute | solution.py:224
  133.4 2.6 %collective-permute-done.7 = f32[8,8]{1,0:T(8,128)S(1)} collective-permute-done((f32[8,8]{1,0:T(8,128)S(1)}, f32[8,8]{1,0:T(8,128)S(1)}, u32[]{:S(2)}, u32[]{:S(2)}) %collective-permute-start.7) | collective-permute-done | bytes 288 | tf_op jit(solution)/shard_map/ppermute | solution.py:224
  136.0 2.4 %collective-permute-start.8 = (f32[8,8]{1,0:T(8,128)S(1)}, f32[8,8]{1,0:T(8,128)S(1)}, u32[]{:S(2)}, u32[]{:S(2)}) collective-permute-start(f32[8,8]{1,0:T(8,128)S(1)} %add.58), channel_id=1, source_target_pairs={{0,16},{4,20},{8,24},{12,28},{16,0},{20,4},{24,8},{28,12},{1,17},{... | collective-permute-start | bytes 776 | tf_op jit(solution)/shard_map/ppermute | solution.py:224
  138.4 2.1 %collective-permute-done.8 = f32[8,8]{1,0:T(8,128)S(1)} collective-permute-done((f32[8,8]{1,0:T(8,128)S(1)}, f32[8,8]{1,0:T(8,128)S(1)}, u32[]{:S(2)}, u32[]{:S(2)}) %collective-permute-start.8) | collective-permute-done | bytes 288 | tf_op jit(solution)/shard_map/ppermute | solution.py:224
  (60 shorter events, 19.7 us)
Async XLA Ops:
  6.1 8.8 %copy-start.1 = (f32[4,512,128]{2,1,0:T(8,128)S(1)}, f32[4,512,128]{2,1,0:T(8,128)}, u32[]{:S(2)}) copy-start(f32[4,512,128]{2,1,0:T(8,128)} %d_ref.3) | copy-start | bytes 3145732
  6.2 8.8 %copy-start.2 = (f32[4,512,128]{2,1,0:T(8,128)S(1)}, f32[4,512,128]{2,1,0:T(8,128)}, u32[]{:S(2)}) copy-start(f32[4,512,128]{2,1,0:T(8,128)} %v_ref.3) | copy-start | bytes 3145732
  7.6 35.0 %all-to-all-start = ((f32[2,8,129,128]{3,0,2,1:T(2,128)}), f32[2,8,129,128]{3,0,2,1:T(2,128)}, u32[]{:S(2)}, u32[]{:S(2)}) async-start(f32[2,8,129,128]{3,0,2,1:T(2,128)} %pad_maximum_fusion), calls=%async_computation | async-start | bytes 2113536 | tf_op jit(solution)/shard_map/all_to_all | solution.py:250
  15.1 27.5 %collective-permute-start.2 = (bf16[2,2,512,128]{3,2,1,0:T(8,128)(2,1)S(1)}, bf16[2,2,512,128]{3,2,1,0:T(8,128)(2,1)S(1)}, u32[]{:S(2)}, u32[]{:S(2)}) collective-permute-start(bf16[2,2,512,128]{3,2,1,0:T(8,128)(2,1)S(1)} %fusion.12), channel_id=1, source_target_pairs={{0,4},{1,29},{2,6},{3,31},{4,8},{5,1},{6,10},{7,3},{8,12},{9,5},{1... | collective-permute-start | bytes 1572872 | tf_op jit(solution)/shard_map/ppermute | solution.py:40
  42.6 23.5 %collective-permute-start.3 = (bf16[2,2,512,128]{3,2,1,0:T(8,128)(2,1)S(1)}, bf16[2,2,512,128]{3,2,1,0:T(8,128)(2,1)S(1)}, u32[]{:S(2)}, u32[]{:S(2)}) collective-permute-start(bf16[2,2,512,128]{3,2,1,0:T(8,128)(2,1)S(1)} %collective-permute-done.2), channel_id=1, source_target_pairs={{0,1},{1,0},{2,3},{3,2},{4,5},{5,4},{6,7},{7,6},{8,9},{9,8},{10,11... | collective-permute-start | bytes 1572872 | tf_op jit(solution)/shard_map/ppermute | solution.py:41
  49.8 1.5 %copy-start = (f32[2,2048,128]{2,1,0:T(8,128)}, f32[2,2048,128]{2,1,0:T(8,128)S(1)}, u32[]{:S(2)}) copy-start(f32[2,2048,128]{2,1,0:T(8,128)S(1)} %slice_add_fusion) | copy-start | bytes 6291460
  51.3 27.4 %collective-permute-start = (bf16[2,2,512,128]{3,2,1,0:T(8,128)(2,1)}, bf16[2,2,512,128]{3,2,1,0:T(8,128)(2,1)S(1)}, u32[]{:S(2)}, u32[]{:S(2)}) collective-permute-start(bf16[2,2,512,128]{3,2,1,0:T(8,128)(2,1)} %get-tuple-element.15), channel_id=1, source_target_pairs={{0,4},{4,8},{8,12},{12,16},{16,20},{20,24},{24,28},{28,0},{1,5},{5... | collective-permute-start | bytes 1572872 | tf_op jit(solution)/shard_map/ppermute | solution.py:24
  56.7 23.1 %collective-permute-start.1 = (bf16[2,2,512,128]{3,2,1,0:T(8,128)(2,1)S(1)}, bf16[2,2,512,128]{3,2,1,0:T(8,128)(2,1)S(1)}, u32[]{:S(2)}, u32[]{:S(2)}) collective-permute-start(bf16[2,2,512,128]{3,2,1,0:T(8,128)(2,1)S(1)} %get-tuple-element.14), channel_id=1, source_target_pairs={{4,0},{8,4},{12,8},{16,12},{20,16},{24,20},{28,24},{0,28},{5,1},{9... | collective-permute-start | bytes 1572872 | tf_op jit(solution)/shard_map/ppermute | solution.py:24
  62.4 28.0 %all-to-all-start.2 = ((bf16[2,2,512,128]{3,1,0,2:T(2,128)(2,1)}), bf16[2,2,512,128]{3,1,0,2:T(2,128)(2,1)S(1)}, u32[]{:S(2)}, u32[]{:S(2)}) async-start(bf16[2,2,512,128]{3,1,0,2:T(2,128)(2,1)} %copy.24), calls=%async_computation.2 | async-start | bytes 1048576 | tf_op jit(solution)/shard_map/all_to_all | solution.py:266
  78.7 1.1 copy-start.4
  79.8 0.8 copy-start.5
  88.0 6.3 %copy-start.3 = (bf16[2,4,512,128]{3,2,1,0:T(8,128)(2,1)S(1)}, bf16[2,4,512,128]{3,2,1,0:T(8,128)(2,1)}, u32[]{:S(2)}) copy-start(bf16[2,4,512,128]{3,2,1,0:T(8,128)(2,1)} %get-tuple-element.7) | copy-start | bytes 3145732
  90.5 12.4 %all-to-all-start.1 = ((bf16[2,2,512,128]{3,1,0,2:T(2,128)(2,1)}), bf16[2,2,512,128]{3,1,0,2:T(2,128)(2,1)S(1)}, u32[]{:S(2)}, u32[]{:S(2)}) async-start(bf16[2,2,512,128]{3,1,0,2:T(2,128)(2,1)} %copy.22), calls=%async_computation.1 | async-start | bytes 1048576 | tf_op jit(solution)/shard_map/all_to_all | solution.py:266
  102.9 17.9 %all-to-all-start.3 = ((bf16[2,4,512,128]{3,1,0,2:T(4,128)(2,1)}), bf16[2,4,512,128]{3,1,0,2:T(4,128)(2,1)S(1)}, u32[]{:S(2)}, u32[]{:S(2)}) async-start(bf16[2,4,512,128]{3,1,0,2:T(4,128)(2,1)} %copy.26), calls=%async_computation.3 | async-start | bytes 2097152 | tf_op jit(solution)/shard_map/all_to_all | solution.py:266
  124.0 1.2 collective-permute-start.4
  125.2 3.6 %collective-permute-start.5 = (f32[8,8]{1,0:T(8,128)S(1)}, f32[8,8]{1,0:T(8,128)S(1)}, u32[]{:S(2)}, u32[]{:S(2)}) collective-permute-start(f32[8,8]{1,0:T(8,128)S(1)} %add.55), channel_id=1, source_target_pairs={{0,2},{1,3},{2,0},{3,1},{4,6},{5,7},{6,4},{7,5},{8,10},{9,11},{10,... | collective-permute-start | bytes 776 | tf_op jit(solution)/shard_map/ppermute | solution.py:224
  128.8 3.6 %collective-permute-start.6 = (f32[8,8]{1,0:T(8,128)S(1)}, f32[8,8]{1,0:T(8,128)S(1)}, u32[]{:S(2)}, u32[]{:S(2)}) collective-permute-start(f32[8,8]{1,0:T(8,128)S(1)} %add.56), channel_id=1, source_target_pairs={{0,4},{4,0},{8,12},{12,8},{16,20},{20,16},{24,28},{28,24},{1,5},{5... | collective-permute-start | bytes 776 | tf_op jit(solution)/shard_map/ppermute | solution.py:224
  132.4 3.6 %collective-permute-start.7 = (f32[8,8]{1,0:T(8,128)S(1)}, f32[8,8]{1,0:T(8,128)S(1)}, u32[]{:S(2)}, u32[]{:S(2)}) collective-permute-start(f32[8,8]{1,0:T(8,128)S(1)} %add.57), channel_id=1, source_target_pairs={{0,8},{4,12},{8,0},{12,4},{16,24},{20,28},{24,16},{28,20},{1,9},{5... | collective-permute-start | bytes 776 | tf_op jit(solution)/shard_map/ppermute | solution.py:224
  136.0 4.5 %collective-permute-start.8 = (f32[8,8]{1,0:T(8,128)S(1)}, f32[8,8]{1,0:T(8,128)S(1)}, u32[]{:S(2)}, u32[]{:S(2)}) collective-permute-start(f32[8,8]{1,0:T(8,128)S(1)} %add.58), channel_id=1, source_target_pairs={{0,16},{4,20},{8,24},{12,28},{16,0},{20,4},{24,8},{28,12},{1,17},{... | collective-permute-start | bytes 776 | tf_op jit(solution)/shard_map/ppermute | solution.py:224

commit v8 on v7

--- a/solution.py
+++ b/solution.py
@@ -92,6 +92,12 @@
         slope = 0.5 * (xp - xm)
         return x0 + coef(0, k, c) * lifted - coef(1, k, c) * slope
 
+    def store(ref, slot, c, value):
+        quarter = ref.shape[3]
+        per = block // quarter
+        for j in range(per):
+            ref[0, c * per + j, slot] = value[j * quarter:(j + 1) * quarter].astype(ref.dtype)
+
     def both(run):
         @pl.when(flag_ref[0] == 0)
         def _():
@@ -101,18 +107,18 @@
         def _():
             run(True)
 
-    return planes, tiles, rows, level0, update, both
+    return planes, tiles, rows, level0, update, both, store
 
 
 def interior_kernel(flag_ref, x_ref, d_ref, v_ref, s_ref):
     halo = STEPS
-    planes, tiles, rows, level0, update, both = stencil_parts(
+    planes, tiles, _, level0, update, both, store = stencil_parts(
         flag_ref, x_ref, None, None, d_ref, v_ref, None, None, halo)
 
     def run(adjoint):
         for k in range(halo + 1, halo + planes - 1):
             def first(c, carry, k=k):
-                s_ref[0, k - halo - 1, rows(c), :] = update(level0, k, c, adjoint).astype(s_ref.dtype)
+                store(s_ref, k - halo - 1, c, update(level0, k, c, adjoint))
                 return carry
 
             lax.fori_loop(0, tiles, first, 0, unroll=2)
@@ -120,9 +126,9 @@
     both(run)
 
 
-def stencil_kernel(flag_ref, x_ref, xb_ref, xa_ref, d_ref, v_ref, cb_ref, ca_ref, out_ref, s1_ref, s2_ref, mid_ref):
+def stencil_kernel(flag_ref, x_ref, xb_ref, xa_ref, d_ref, v_ref, cb_ref, ca_ref, out_ref, late_ref, mid_ref):
     halo = xb_ref.shape[1]
-    planes, tiles, rows, level0, update, both = stencil_parts(
+    planes, tiles, rows, level0, update, both, store = stencil_parts(
         flag_ref, x_ref, xb_ref, xa_ref, d_ref, v_ref, cb_ref, ca_ref, halo)
     ext = planes + 2 * halo
 
@@ -135,7 +141,7 @@
                 value = update(level0, k, c, adjoint)
                 mid_ref[k - 1, rows(c), :] = value
                 if k == halo or k == halo + planes - 1:
-                    s1_ref[0, 0 if k == halo else 1, rows(c), :] = value.astype(s1_ref.dtype)
+                    store(late_ref, 0 if k == halo else 1, c, value)
                 return carry
 
             lax.fori_loop(0, tiles, first, 0, unroll=2)
@@ -143,7 +149,8 @@
             def second(c, carry, k=k):
                 value = update(level1, k, c, adjoint)
                 out_ref[0, k - halo, rows(c), :] = value
-                s2_ref[0, k - halo, rows(c), :] = value.astype(s2_ref.dtype)
+                p = k - halo
+                store(late_ref, 2 + (0 if p == 0 else 1 if p == planes - 1 else 1 + p), c, value)
                 return carry
 
             lax.fori_loop(0, tiles, second, 0, unroll=2)
@@ -151,7 +158,7 @@
     both(run)
 
 
-def interior_step(flag, state, diffusion, velocity):
+def interior_step(flag, state, diffusion, velocity, share):
     fields, planes, span, depth = state.shape
     return pl.pallas_call(
         interior_kernel,
@@ -162,13 +169,13 @@
             pl.BlockSpec((planes, span, depth), lambda f: (0, 0, 0)),
             pl.BlockSpec((planes, span, depth), lambda f: (0, 0, 0)),
         ],
-        out_specs=pl.BlockSpec((1, planes - 2, span, depth), lambda f: (f, 0, 0, 0)),
-        out_shape=jax.ShapeDtypeStruct((fields, planes - 2, span, depth), jnp.bfloat16),
+        out_specs=pl.BlockSpec((1, share, planes - 2, span // share, depth), lambda f: (f, 0, 0, 0, 0)),
+        out_shape=jax.ShapeDtypeStruct((fields, share, planes - 2, span // share, depth), jnp.bfloat16),
         compiler_params=pltpu.CompilerParams(dimension_semantics=("arbitrary",)),
     )(flag, state, diffusion, velocity)
 
 
-def two_steps(flag, state, before, after, diffusion, velocity, coef_before, coef_after):
+def two_steps(flag, state, before, after, diffusion, velocity, coef_before, coef_after, share):
     fields, planes, span, depth = state.shape
     halo = before.shape[1]
     field_block = lambda n: pl.BlockSpec((1, n, span, depth), lambda f: (f, 0, 0, 0))
@@ -186,11 +193,13 @@
             whole((2, halo, span, depth)),
             whole((2, halo, span, depth)),
         ],
-        out_specs=[field_block(planes), field_block(2), field_block(planes)],
+        out_specs=[
+            field_block(planes),
+            pl.BlockSpec((1, share, 2 + planes, span // share, depth), lambda f: (f, 0, 0, 0, 0)),
+        ],
         out_shape=[
             jax.ShapeDtypeStruct(state.shape, jnp.float32),
-            jax.ShapeDtypeStruct((fields, 2, span, depth), jnp.bfloat16),
-            jax.ShapeDtypeStruct(state.shape, jnp.bfloat16),
+            jax.ShapeDtypeStruct((fields, share, 2 + planes, span // share, depth), jnp.bfloat16),
         ],
         scratch_shapes=[pltpu.VMEM((planes + 2 * halo - 2, span, depth), jnp.float32)],
         compiler_params=pltpu.CompilerParams(dimension_semantics=("arbitrary",)),
@@ -258,24 +267,29 @@
     adjoint = lax.axis_index("batch") >= lax.axis_size("batch") // 2
     flag = adjoint.astype(jnp.int32).reshape(1)
     coef_before, coef_after = halos_shared(jnp.stack([diffusion, velocity]), STEPS, 1)
-    inner = interior_step(flag, state, diffusion, velocity)
+    share = lax.axis_size("batch")
+    inner = interior_step(flag, state, diffusion, velocity, share)
     before, after = halos(state, "space", STEPS, 1)
-    state, outer, snap2 = two_steps(flag, state, before, after, diffusion, velocity, coef_before, coef_after)
+    state, late = two_steps(flag, state, before, after, diffusion, velocity, coef_before, coef_after, share)
 
     def spread(snap):
-        return lax.all_to_all(snap, "batch", split_axis=2, concat_axis=0, tiled=True)
-
-    inner, outer = spread(inner), spread(outer)
-    first = jnp.concatenate([outer[:, :1], inner, outer[:, 1:]], axis=1)
-    second = spread(snap2)
-    snaps = [first.reshape(first.shape[0], -1), second.reshape(second.shape[0], -1)]
+        mixed = lax.all_to_all(snap, "batch", split_axis=1, concat_axis=0, tiled=True)
+        return mixed.reshape(mixed.shape[0], mixed.shape[2], -1)
+
+    inner, late = spread(inner), spread(late)
+    snaps = [(late[:, 0:2], inner), (late[:, 2:4], late[:, 4:])]
     rows = []
     for sensed in snaps:
         row = []
         for actuated in snaps:
-            row.append(lax.dot_general(
-                sensed[ACT:ACT + SENS], actuated[:ACT], (((1,), (1,)), ((), ())), preferred_element_type=jnp.float32
-            ))
+            block = None
+            for s_part, a_part in zip(sensed, actuated):
+                term = lax.dot_general(
+                    s_part[ACT:ACT + SENS].reshape(SENS, -1), a_part[:ACT].reshape(ACT, -1),
+                    (((1,), (1,)), ((), ())), preferred_element_type=jnp.float32,
+                )
+                block = term if block is None else block + term
+            row.append(block)
         rows.append(jnp.concatenate(row, axis=1))
     partial_gram = jnp.concatenate(rows, axis=0)
     scale = 4.0 / math.sqrt(planes * count * span * depth)

time: 142 us -> 136 us (0.958)
  starting transfers between devices: 30.7 us -> 26.9 us
  local copies, waits for them, and re-layouts: 13.3 us -> 11.7 us
    all_to_all x3 -> x2, starting transfers between devices: 10.7 us -> 7.21 us  [spread(): lax.all_to_all(snap, 'batch', split_axis=1, concat_axis=0, tiled=True)]
    reshape x0 -> x3, local copies, waits for them, and re-layouts: none -> 1.62 us  [the longest x1 0.8 us: work(): s_part[ACT:ACT + SENS].reshape(SENS, -1)]
    pallas_call x2 -> x1, local copies, waits for them, and re-layouts: 4.29 us -> 2.75 us  [two_steps(): pl.pallas_call(stencil_kernel, grid=(fields,), in_specs=[pl.BlockSpec(mem...]
    all_to_all x3 -> x2, waiting for transfers between devices: 19.5 us -> 19.2 us  [spread(): lax.all_to_all(snap, 'batch', split_axis=1, concat_axis=0, tiled=True)]
    dot_general x4 -> x8, matrix products: 3.19 us -> 3.09 us  [work(): lax.dot_general(s_part[ACT:ACT + SENS].reshape(SENS, -1), a_part[:ACT].re...]
  transfers between devices with their start and end apart: 13 -> 12, of which waited for: 10 -> 9; matrix products, arithmetic and copies ran while one was open for 13% -> 11% of each run, Pallas kernels for 8% -> 8%
where the time goes in v8:
time: 136 us
  waiting for transfers between devices  69.4 us (51%)
  starting transfers between devices  26.9 us (20%)
  local copies, waits for them, and re-layouts  11.7 us (9%)
  Pallas kernels  10.8 us (8%)
  matrix products  8.3 us (6%)
  other arithmetic  8.04 us (6%)
    ppermute x1, waiting for transfers between devices, halos_shared(): lax.ppermute(jnp.where(odd, initial, last).astype(LINK), ('space', 'batch...  25.5 us
    all_to_all x2, waiting for transfers between devices, spread(): lax.all_to_all(snap, 'batch', split_axis=1, concat_axis=0, tiled=True)  19.2 us
    ppermute x2, waiting for transfers between devices, halos(): return (lax.ppermute(last, axis, up), lax.ppermute(initial, axis, down))  13.1 us
    ppermute x5, waiting for transfers between devices, butterfly(): value = value + lax.ppermute(value, axis, [(i, i ^ step) for i in range(n)])  11.5 us
    pallas_call x1, Pallas kernels, two_steps(): pl.pallas_call(stencil_kernel, grid=(fields,), in_specs=[pl.BlockSpec(mem...  7.41 us
    all_to_all x1, starting transfers between devices, work(): lax.all_to_all(payload, 'space', split_axis=1, concat_axis=1, tiled=True)  7.28 us
    all_to_all x2, starting transfers between devices, spread(): lax.all_to_all(snap, 'batch', split_axis=1, concat_axis=0, tiled=True)  7.21 us
    ppermute x2, starting transfers between devices, halos(): return (lax.ppermute(last, axis, up), lax.ppermute(initial, axis, down))  5.37 us
  transfers between devices with their start and end apart: 12, of which 9 were waited for; matrix products, arithmetic and copies ran while one was open for 11% of the time, Pallas kernels for 8%

profile of v8, /device:TPU:0, one launch (start us, length us, event | category | flops | bytes accessed | tf_op | source)
XLA Modules:
  0.0 135.9 jit_solution(5196707816828410789)
XLA Ops:
  6.2 1.5 %pad_maximum_fusion = f32[2,8,129,128]{3,0,2,1:T(2,128)} fusion(f32[2,8,1,128]{3,0,2,1:T(2,128)S(1)} %convert_bitcast_fusion, f32[2,8,128,128]{3,0,2,1:T(2,128)S(1)} %copy.15), kind=kLoop, calls=%fused_computation.28 | loop fusion | flops 264192 | bytes 2113536 | tf_op jit(solution)/shard_map/concatenate | solution.py:255
  7.6 7.3 %all-to-all-start = ((f32[2,8,129,128]{3,0,2,1:T(2,128)}), f32[2,8,129,128]{3,0,2,1:T(2,128)}, u32[]{:S(2)}, u32[]{:S(2)}) async-start(f32[2,8,129,128]{3,0,2,1:T(2,128)} %pad_maximum_fusion), calls=%async_computation | async-start | bytes 2113536 | tf_op jit(solution)/shard_map/all_to_all | solution.py:259
  15.1 2.1 %collective-permute-start.2 = (bf16[2,2,512,128]{3,2,1,0:T(8,128)(2,1)S(1)}, bf16[2,2,512,128]{3,2,1,0:T(8,128)(2,1)S(1)}, u32[]{:S(2)}, u32[]{:S(2)}) collective-permute-start(bf16[2,2,512,128]{3,2,1,0:T(8,128)(2,1)S(1)} %fusion.13), channel_id=1, source_target_pairs={{0,4},{1,29},{2,6},{3,31},{4,8},{5,1},{6,10},{7,3},{8,12},{9,5},{1... | collective-permute-start | bytes 1572872 | tf_op jit(solution)/shard_map/ppermute | solution.py:40
  17.1 25.5 %collective-permute-done.2 = bf16[2,2,512,128]{3,2,1,0:T(8,128)(2,1)S(1)} collective-permute-done((bf16[2,2,512,128]{3,2,1,0:T(8,128)(2,1)S(1)}, bf16[2,2,512,128]{3,2,1,0:T(8,128)(2,1)S(1)}, u32[]{:S(2)}, u32[]{:S(2)}) %collective-permute-start.2) | collective-permute-done | bytes 524320 | tf_op jit(solution)/shard_map/ppermute | solution.py:40
  42.6 1.3 slice.105
  45.0 4.5 %fusion = f32[2,2048,384]{2,1,0:T(8,128)S(1)} fusion(s32[2,1024]{1,0:T(2,128)S(1)} %fusion.30, bf16[2,1024,128]{2,1,0:T(8,128)(2,1)S(1)} %get-tuple-element.13, bf16[2,1024,128]{2,1,0:T(8,128)(2,1)S(1)} %get-tuple-element.14, bf16[2,1024,128]{2,1,0:T(8,128)(2,1)S(1)} %get-tuple-element.12), kind=kOutput, calls=%fused_computation.1 | convolution fusion | flops 3230138368 | bytes 7872512 | tf_op jit(solution)/shard_map/fmk,fkd->fmd/dot_general | solution.py:221
  50.0 1.1 fusion.34
  51.3 5.4 %collective-permute-start = (bf16[2,2,512,128]{3,2,1,0:T(8,128)(2,1)}, bf16[2,2,512,128]{3,2,1,0:T(8,128)(2,1)S(1)}, u32[]{:S(2)}, u32[]{:S(2)}) collective-permute-start(bf16[2,2,512,128]{3,2,1,0:T(8,128)(2,1)} %get-tuple-element.11), channel_id=1, source_target_pairs={{0,4},{4,8},{8,12},{12,16},{16,20},{20,24},{24,28},{28,0},{1,5},{5... | collective-permute-start | bytes 1572872 | tf_op jit(solution)/shard_map/ppermute | solution.py:24
  56.7 3.4 %shard_map.69 = bf16[2,4,2,128,128]{4,3,2,1,0:T(8,128)(2,1)} custom-call(s32[1]{0:T(128)} %bitcast.flag_ref, f32[2,4,512,128]{3,2,1,0:T(8,128)} %bitcast.62, f32[4,512,128]{2,1,0:T(8,128)} %d_ref.3, f32[4,512,128]{2,1,0:T(8,128)} %v_ref.3), custom_call_target="tpu_custom_call" | custom-call | tf_op jit(solution)/shard_map/pallas_call | solution.py:163
  60.0 1.9 %copy.19 = bf16[2,4,2,128,128]{4,3,2,0,1:T(8,128)(2,1)} copy(bf16[2,4,2,128,128]{4,3,2,1,0:T(8,128)(2,1)} %shard_map.69) | data formatting | bytes 1048576 | tf_op jit(solution)/shard_map/pallas_call | solution.py:163
  61.9 3.6 %all-to-all-start.2 = ((bf16[2,4,2,128,128]{4,3,2,0,1:T(8,128)(2,1)}), bf16[2,4,2,128,128]{4,3,2,0,1:T(8,128)(2,1)S(1)}, u32[]{:S(2)}, u32[]{:S(2)}) async-start(bf16[2,4,2,128,128]{4,3,2,0,1:T(8,128)(2,1)} %copy.19), calls=%async_computation.2 | async-start | bytes 1048576 | tf_op jit(solution)/shard_map/all_to_all | solution.py:276
  66.7 12.0 %collective-permute-done.xb_ref = bf16[2,2,512,128]{3,2,1,0:T(8,128)(2,1)S(1)} collective-permute-done((bf16[2,2,512,128]{3,2,1,0:T(8,128)(2,1)}, bf16[2,2,512,128]{3,2,1,0:T(8,128)(2,1)S(1)}, u32[]{:S(2)}, u32[]{:S(2)}) %collective-permute-start) | collective-permute-done | bytes 524320 | tf_op jit(solution)/shard_map/ppermute | solution.py:24
  78.7 1.1 collective-permute-done.1.xa_ref
  80.6 7.4 %shard_map.68 = (f32[2,4,512,128]{3,2,1,0:T(8,128)}, bf16[2,4,6,128,128]{4,3,2,1,0:T(8,128)(2,1)}) custom-call(s32[1]{0:T(128)} %bitcast.flag_ref, f32[2,4,512,128]{3,2,1,0:T(8,128)} %bitcast.63, bf16[2,2,512,128]{3,2,1,0:T(8,128)(2,1)} %copy-done.3, bf16[2,2,512,128]{3,2,1,0:T(8,128)(2,1)} %copy-done.4, f32[4,512,128]{2,1,0:T(8,128)} %d_ref.3, ...), custom_call_target="tpu_custom_call" | custom-call | tf_op jit(solution)/shard_map/pallas_call | solution.py:183
  88.0 2.7 %copy.17 = bf16[2,4,6,128,128]{4,3,2,0,1:T(8,128)(2,1)} copy(bf16[2,4,6,128,128]{4,3,2,1,0:T(8,128)(2,1)} %get-tuple-element.5) | data formatting | bytes 3145728 | tf_op jit(solution)/shard_map/pallas_call | solution.py:183
  90.7 3.6 %all-to-all-start.1 = ((bf16[2,4,6,128,128]{4,3,2,0,1:T(8,128)(2,1)}), bf16[2,4,6,128,128]{4,3,2,0,1:T(8,128)(2,1)S(1)}, u32[]{:S(2)}, u32[]{:S(2)}) async-start(bf16[2,4,6,128,128]{4,3,2,0,1:T(8,128)(2,1)} %copy.17), calls=%async_computation.1 | async-start | bytes 3145728 | tf_op jit(solution)/shard_map/all_to_all | solution.py:276
  95.3 19.2 %all-to-all-done.1 = bf16[2,4,6,128,128]{4,3,2,0,1:T(8,128)(2,1)S(1)} async-done(((bf16[2,4,6,128,128]{4,3,2,0,1:T(8,128)(2,1)}), bf16[2,4,6,128,128]{4,3,2,0,1:T(8,128)(2,1)S(1)}, u32[]{:S(2)}, u32[]{:S(2)}) %all-to-all-start.1) | async-done | bytes 1572896 | tf_op jit(solution)/shard_map/all_to_all | solution.py:276
  118.8 1.2 collective-permute-done.4
  120.2 3.4 %collective-permute-done.5 = f32[8,8]{1,0:T(8,128)S(1)} collective-permute-done((f32[8,8]{1,0:T(8,128)S(1)}, f32[8,8]{1,0:T(8,128)S(1)}, u32[]{:S(2)}, u32[]{:S(2)}) %collective-permute-start.5) | collective-permute-done | bytes 288 | tf_op jit(solution)/shard_map/ppermute | solution.py:233
  123.6 1.3 collective-permute-start.6
  124.9 2.3 %collective-permute-done.6 = f32[8,8]{1,0:T(8,128)S(1)} collective-permute-done((f32[8,8]{1,0:T(8,128)S(1)}, f32[8,8]{1,0:T(8,128)S(1)}, u32[]{:S(2)}, u32[]{:S(2)}) %collective-permute-start.6) | collective-permute-done | bytes 288 | tf_op jit(solution)/shard_map/ppermute | solution.py:233
  128.2 2.6 %collective-permute-done.7 = f32[8,8]{1,0:T(8,128)S(1)} collective-permute-done((f32[8,8]{1,0:T(8,128)S(1)}, f32[8,8]{1,0:T(8,128)S(1)}, u32[]{:S(2)}, u32[]{:S(2)}) %collective-permute-start.7) | collective-permute-done | bytes 288 | tf_op jit(solution)/shard_map/ppermute | solution.py:233
  130.8 2.3 %collective-permute-start.8 = (f32[8,8]{1,0:T(8,128)S(1)}, f32[8,8]{1,0:T(8,128)S(1)}, u32[]{:S(2)}, u32[]{:S(2)}) collective-permute-start(f32[8,8]{1,0:T(8,128)S(1)} %add.74), channel_id=1, source_target_pairs={{0,16},{4,20},{8,24},{12,28},{16,0},{20,4},{24,8},{28,12},{1,17},{... | collective-permute-start | bytes 776 | tf_op jit(solution)/shard_map/ppermute | solution.py:233
  133.1 2.2 %collective-permute-done.8 = f32[8,8]{1,0:T(8,128)S(1)} collective-permute-done((f32[8,8]{1,0:T(8,128)S(1)}, f32[8,8]{1,0:T(8,128)S(1)}, u32[]{:S(2)}, u32[]{:S(2)}) %collective-permute-start.8) | collective-permute-done | bytes 288 | tf_op jit(solution)/shard_map/ppermute | solution.py:233
  (58 shorter events, 16.3 us)
Async XLA Ops:
  6.1 8.8 %copy-start.1 = (f32[4,512,128]{2,1,0:T(8,128)S(1)}, f32[4,512,128]{2,1,0:T(8,128)}, u32[]{:S(2)}) copy-start(f32[4,512,128]{2,1,0:T(8,128)} %d_ref.3) | copy-start | bytes 3145732
  6.2 8.8 %copy-start.2 = (f32[4,512,128]{2,1,0:T(8,128)S(1)}, f32[4,512,128]{2,1,0:T(8,128)}, u32[]{:S(2)}) copy-start(f32[4,512,128]{2,1,0:T(8,128)} %v_ref.3) | copy-start | bytes 3145732
  7.6 35.0 %all-to-all-start = ((f32[2,8,129,128]{3,0,2,1:T(2,128)}), f32[2,8,129,128]{3,0,2,1:T(2,128)}, u32[]{:S(2)}, u32[]{:S(2)}) async-start(f32[2,8,129,128]{3,0,2,1:T(2,128)} %pad_maximum_fusion), calls=%async_computation | async-start | bytes 2113536 | tf_op jit(solution)/shard_map/all_to_all | solution.py:259
  15.1 27.5 %collective-permute-start.2 = (bf16[2,2,512,128]{3,2,1,0:T(8,128)(2,1)S(1)}, bf16[2,2,512,128]{3,2,1,0:T(8,128)(2,1)S(1)}, u32[]{:S(2)}, u32[]{:S(2)}) collective-permute-start(bf16[2,2,512,128]{3,2,1,0:T(8,128)(2,1)S(1)} %fusion.13), channel_id=1, source_target_pairs={{0,4},{1,29},{2,6},{3,31},{4,8},{5,1},{6,10},{7,3},{8,12},{9,5},{1... | collective-permute-start | bytes 1572872 | tf_op jit(solution)/shard_map/ppermute | solution.py:40
  42.6 23.0 %collective-permute-start.3 = (bf16[2,2,512,128]{3,2,1,0:T(8,128)(2,1)S(1)}, bf16[2,2,512,128]{3,2,1,0:T(8,128)(2,1)S(1)}, u32[]{:S(2)}, u32[]{:S(2)}) collective-permute-start(bf16[2,2,512,128]{3,2,1,0:T(8,128)(2,1)S(1)} %collective-permute-done.2), channel_id=1, source_target_pairs={{0,1},{1,0},{2,3},{3,2},{4,5},{5,4},{6,7},{7,6},{8,9},{9,8},{10,11... | collective-permute-start | bytes 1572872 | tf_op jit(solution)/shard_map/ppermute | solution.py:41
  49.8 1.5 %copy-start = (f32[2,2048,128]{2,1,0:T(8,128)}, f32[2,2048,128]{2,1,0:T(8,128)S(1)}, u32[]{:S(2)}) copy-start(f32[2,2048,128]{2,1,0:T(8,128)S(1)} %slice_add_fusion) | copy-start | bytes 6291460
  51.3 27.4 %collective-permute-start = (bf16[2,2,512,128]{3,2,1,0:T(8,128)(2,1)}, bf16[2,2,512,128]{3,2,1,0:T(8,128)(2,1)S(1)}, u32[]{:S(2)}, u32[]{:S(2)}) collective-permute-start(bf16[2,2,512,128]{3,2,1,0:T(8,128)(2,1)} %get-tuple-element.11), channel_id=1, source_target_pairs={{0,4},{4,8},{8,12},{12,16},{16,20},{20,24},{24,28},{28,0},{1,5},{5... | collective-permute-start | bytes 1572872 | tf_op jit(solution)/shard_map/ppermute | solution.py:24
  56.7 23.1 %collective-permute-start.1 = (bf16[2,2,512,128]{3,2,1,0:T(8,128)(2,1)S(1)}, bf16[2,2,512,128]{3,2,1,0:T(8,128)(2,1)S(1)}, u32[]{:S(2)}, u32[]{:S(2)}) collective-permute-start(bf16[2,2,512,128]{3,2,1,0:T(8,128)(2,1)S(1)} %get-tuple-element.10), channel_id=1, source_target_pairs={{4,0},{8,4},{12,8},{16,12},{20,16},{24,20},{28,24},{0,28},{5,1},{9... | collective-permute-start | bytes 1572872 | tf_op jit(solution)/shard_map/ppermute | solution.py:24
  61.9 28.8 %all-to-all-start.2 = ((bf16[2,4,2,128,128]{4,3,2,0,1:T(8,128)(2,1)}), bf16[2,4,2,128,128]{4,3,2,0,1:T(8,128)(2,1)S(1)}, u32[]{:S(2)}, u32[]{:S(2)}) async-start(bf16[2,4,2,128,128]{4,3,2,0,1:T(8,128)(2,1)} %copy.19), calls=%async_computation.2 | async-start | bytes 1048576 | tf_op jit(solution)/shard_map/all_to_all | solution.py:276
  78.7 1.1 copy-start.3
  79.8 0.8 copy-start.4
  90.7 23.8 %all-to-all-start.1 = ((bf16[2,4,6,128,128]{4,3,2,0,1:T(8,128)(2,1)}), bf16[2,4,6,128,128]{4,3,2,0,1:T(8,128)(2,1)S(1)}, u32[]{:S(2)}, u32[]{:S(2)}) async-start(bf16[2,4,6,128,128]{4,3,2,0,1:T(8,128)(2,1)} %copy.17), calls=%async_computation.1 | async-start | bytes 3145728 | tf_op jit(solution)/shard_map/all_to_all | solution.py:276
  117.0 1.1 copy-start.5
  118.8 1.2 collective-permute-start.4
  120.0 3.6 %collective-permute-start.5 = (f32[8,8]{1,0:T(8,128)S(1)}, f32[8,8]{1,0:T(8,128)S(1)}, u32[]{:S(2)}, u32[]{:S(2)}) collective-permute-start(f32[8,8]{1,0:T(8,128)S(1)} %add.71), channel_id=1, source_target_pairs={{0,2},{1,3},{2,0},{3,1},{4,6},{5,7},{6,4},{7,5},{8,10},{9,11},{10,... | collective-permute-start | bytes 776 | tf_op jit(solution)/shard_map/ppermute | solution.py:233
  123.6 3.6 %collective-permute-start.6 = (f32[8,8]{1,0:T(8,128)S(1)}, f32[8,8]{1,0:T(8,128)S(1)}, u32[]{:S(2)}, u32[]{:S(2)}) collective-permute-start(f32[8,8]{1,0:T(8,128)S(1)} %add.72), channel_id=1, source_target_pairs={{0,4},{4,0},{8,12},{12,8},{16,20},{20,16},{24,28},{28,24},{1,5},{5... | collective-permute-start | bytes 776 | tf_op jit(solution)/shard_map/ppermute | solution.py:233
  127.2 3.6 %collective-permute-start.7 = (f32[8,8]{1,0:T(8,128)S(1)}, f32[8,8]{1,0:T(8,128)S(1)}, u32[]{:S(2)}, u32[]{:S(2)}) collective-permute-start(f32[8,8]{1,0:T(8,128)S(1)} %add.73), channel_id=1, source_target_pairs={{0,8},{4,12},{8,0},{12,4},{16,24},{20,28},{24,16},{28,20},{1,9},{5... | collective-permute-start | bytes 776 | tf_op jit(solution)/shard_map/ppermute | solution.py:233
  130.8 4.5 %collective-permute-start.8 = (f32[8,8]{1,0:T(8,128)S(1)}, f32[8,8]{1,0:T(8,128)S(1)}, u32[]{:S(2)}, u32[]{:S(2)}) collective-permute-start(f32[8,8]{1,0:T(8,128)S(1)} %add.74), channel_id=1, source_target_pairs={{0,16},{4,20},{8,24},{12,28},{16,0},{20,4},{24,8},{28,12},{1,17},{... | collective-permute-start | bytes 776 | tf_op jit(solution)/shard_map/ppermute | solution.py:233

commit v9 on v8

--- a/solution.py
+++ b/solution.py
@@ -96,7 +96,7 @@
         quarter = ref.shape[3]
         per = block // quarter
         for j in range(per):
-            ref[0, c * per + j, slot] = value[j * quarter:(j + 1) * quarter].astype(ref.dtype)
+            ref[c * per + j, 0, slot] = value[j * quarter:(j + 1) * quarter].astype(ref.dtype)
 
     def both(run):
         @pl.when(flag_ref[0] == 0)
@@ -169,8 +169,8 @@
             pl.BlockSpec((planes, span, depth), lambda f: (0, 0, 0)),
             pl.BlockSpec((planes, span, depth), lambda f: (0, 0, 0)),
         ],
-        out_specs=pl.BlockSpec((1, share, planes - 2, span // share, depth), lambda f: (f, 0, 0, 0, 0)),
-        out_shape=jax.ShapeDtypeStruct((fields, share, planes - 2, span // share, depth), jnp.bfloat16),
+        out_specs=pl.BlockSpec((share, 1, planes - 2, span // share, depth), lambda f: (0, f, 0, 0, 0)),
+        out_shape=jax.ShapeDtypeStruct((share, fields, planes - 2, span // share, depth), jnp.bfloat16),
         compiler_params=pltpu.CompilerParams(dimension_semantics=("arbitrary",)),
     )(flag, state, diffusion, velocity)
 
@@ -195,11 +195,11 @@
         ],
         out_specs=[
             field_block(planes),
-            pl.BlockSpec((1, share, 2 + planes, span // share, depth), lambda f: (f, 0, 0, 0, 0)),
+            pl.BlockSpec((share, 1, 2 + planes, span // share, depth), lambda f: (0, f, 0, 0, 0)),
         ],
         out_shape=[
             jax.ShapeDtypeStruct(state.shape, jnp.float32),
-            jax.ShapeDtypeStruct((fields, share, 2 + planes, span // share, depth), jnp.bfloat16),
+            jax.ShapeDtypeStruct((share, fields, 2 + planes, span // share, depth), jnp.bfloat16),
         ],
         scratch_shapes=[pltpu.VMEM((planes + 2 * halo - 2, span, depth), jnp.float32)],
         compiler_params=pltpu.CompilerParams(dimension_semantics=("arbitrary",)),
@@ -273,8 +273,8 @@
     state, late = two_steps(flag, state, before, after, diffusion, velocity, coef_before, coef_after, share)
 
     def spread(snap):
-        mixed = lax.all_to_all(snap, "batch", split_axis=1, concat_axis=0, tiled=True)
-        return mixed.reshape(mixed.shape[0], mixed.shape[2], -1)
+        mixed = lax.all_to_all(snap, "batch", split_axis=0, concat_axis=0, tiled=True)
+        return mixed.reshape(mixed.shape[0] * mixed.shape[1], mixed.shape[2], -1)
 
     inner, late = spread(inner), spread(late)
     snaps = [(late[:, 0:2], inner), (late[:, 2:4], late[:, 4:])]

time: 136 us -> 134 us (0.985)
  local copies, waits for them, and re-layouts: 11.7 us -> 7.01 us
  waiting for transfers between devices: 69.4 us -> 71.2 us
    pallas_call x2 -> x0, local copies, waits for them, and re-layouts: 4.64 us -> none  [the longest x1 2.75 us: two_steps(): pl.pallas_call(stencil_kernel, grid=(fields,), in_specs=[pl.BlockSpec(mem...]
    ppermute x2, waiting for transfers between devices: 13.1 us -> 15 us  [halos(): return (lax.ppermute(last, axis, up), lax.ppermute(initial, axis, down))]
  transfers between devices with their start and end apart: 12 -> 12, of which waited for: 9 -> 9; matrix products, arithmetic and copies ran while one was open for 11% -> 8% of each run, Pallas kernels for 8% -> 8%
where the time goes in v9:
time: 134 us; the launch traced here: 133 us
  waiting for transfers between devices  71.2 us (53%)
  starting transfers between devices  26.9 us (20%)
  Pallas kernels  10.8 us (8%)
  matrix products  8.3 us (6%)
  other arithmetic  8.04 us (6%)
  local copies, waits for them, and re-layouts  7.01 us (5%)
    ppermute x1, waiting for transfers between devices, halos_shared(): lax.ppermute(jnp.where(odd, initial, last).astype(LINK), ('space', 'batch...  25.5 us
    all_to_all x2, waiting for transfers between devices, spread(): lax.all_to_all(snap, 'batch', split_axis=0, concat_axis=0, tiled=True)  19.2 us
    ppermute x2, waiting for transfers between devices, halos(): return (lax.ppermute(last, axis, up), lax.ppermute(initial, axis, down))  15 us
    ppermute x5, waiting for transfers between devices, butterfly(): value = value + lax.ppermute(value, axis, [(i, i ^ step) for i in range(n)])  11.5 us
    pallas_call x1, Pallas kernels, two_steps(): pl.pallas_call(stencil_kernel, grid=(fields,), in_specs=[pl.BlockSpec(mem...  7.42 us
    all_to_all x1, starting transfers between devices, work(): lax.all_to_all(payload, 'space', split_axis=1, concat_axis=1, tiled=True)  7.28 us
    all_to_all x2, starting transfers between devices, spread(): lax.all_to_all(snap, 'batch', split_axis=0, concat_axis=0, tiled=True)  7.22 us
    ppermute x2, starting transfers between devices, halos(): return (lax.ppermute(last, axis, up), lax.ppermute(initial, axis, down))  5.37 us
  transfers between devices with their start and end apart: 12, of which 9 were waited for; matrix products, arithmetic and copies ran while one was open for 8% of the time, Pallas kernels for 8%

profile of v9, /device:TPU:0, one launch (start us, length us, event | category | flops | bytes accessed | tf_op | source)
XLA Modules:
  0.0 133.2 jit_solution(16427298429364259619)
XLA Ops:
  2.4 1.0 select_reduce_fusion
  6.2 1.5 %pad_maximum_fusion = f32[2,8,129,128]{3,0,2,1:T(2,128)} fusion(f32[2,8,1,128]{3,0,2,1:T(2,128)S(1)} %convert_bitcast_fusion, f32[2,8,128,128]{3,0,2,1:T(2,128)S(1)} %copy.17), kind=kLoop, calls=%fused_computation.28 | loop fusion | flops 264192 | bytes 2113536 | tf_op jit(solution)/shard_map/concatenate | solution.py:255
  7.6 7.3 %all-to-all-start = ((f32[2,8,129,128]{3,0,2,1:T(2,128)}), f32[2,8,129,128]{3,0,2,1:T(2,128)}, u32[]{:S(2)}, u32[]{:S(2)}) async-start(f32[2,8,129,128]{3,0,2,1:T(2,128)} %pad_maximum_fusion), calls=%async_computation | async-start | bytes 2113536 | tf_op jit(solution)/shard_map/all_to_all | solution.py:259
  15.1 2.1 %collective-permute-start.2 = (bf16[2,2,512,128]{3,2,1,0:T(8,128)(2,1)S(1)}, bf16[2,2,512,128]{3,2,1,0:T(8,128)(2,1)S(1)}, u32[]{:S(2)}, u32[]{:S(2)}) collective-permute-start(bf16[2,2,512,128]{3,2,1,0:T(8,128)(2,1)S(1)} %fusion.13), channel_id=1, source_target_pairs={{0,4},{1,29},{2,6},{3,31},{4,8},{5,1},{6,10},{7,3},{8,12},{9,5},{1... | collective-permute-start | bytes 1572872 | tf_op jit(solution)/shard_map/ppermute | solution.py:40
  17.1 25.5 %collective-permute-done.2 = bf16[2,2,512,128]{3,2,1,0:T(8,128)(2,1)S(1)} collective-permute-done((bf16[2,2,512,128]{3,2,1,0:T(8,128)(2,1)S(1)}, bf16[2,2,512,128]{3,2,1,0:T(8,128)(2,1)S(1)}, u32[]{:S(2)}, u32[]{:S(2)}) %collective-permute-start.2) | collective-permute-done | bytes 524320 | tf_op jit(solution)/shard_map/ppermute | solution.py:40
  42.6 1.3 slice.105
  45.0 4.5 %fusion = f32[2,2048,384]{2,1,0:T(8,128)S(1)} fusion(s32[2,1024]{1,0:T(2,128)S(1)} %fusion.30, bf16[2,1024,128]{2,1,0:T(8,128)(2,1)S(1)} %get-tuple-element.13, bf16[2,1024,128]{2,1,0:T(8,128)(2,1)S(1)} %get-tuple-element.14, bf16[2,1024,128]{2,1,0:T(8,128)(2,1)S(1)} %get-tuple-element.12), kind=kOutput, calls=%fused_computation.1 | convolution fusion | flops 3230138368 | bytes 7872512 | tf_op jit(solution)/shard_map/fmk,fkd->fmd/dot_general | solution.py:221
  50.0 1.1 fusion.34
  51.3 5.4 %collective-permute-start = (bf16[2,2,512,128]{3,2,1,0:T(8,128)(2,1)}, bf16[2,2,512,128]{3,2,1,0:T(8,128)(2,1)S(1)}, u32[]{:S(2)}, u32[]{:S(2)}) collective-permute-start(bf16[2,2,512,128]{3,2,1,0:T(8,128)(2,1)} %get-tuple-element.11), channel_id=1, source_target_pairs={{0,4},{4,8},{8,12},{12,16},{16,20},{20,24},{24,28},{28,0},{1,5},{5... | collective-permute-start | bytes 1572872 | tf_op jit(solution)/shard_map/ppermute | solution.py:24
  56.7 3.4 %shard_map.69 = bf16[4,2,2,128,128]{4,3,2,1,0:T(8,128)(2,1)} custom-call(s32[1]{0:T(128)} %bitcast.flag_ref, f32[2,4,512,128]{3,2,1,0:T(8,128)} %bitcast.52, f32[4,512,128]{2,1,0:T(8,128)} %d_ref.3, f32[4,512,128]{2,1,0:T(8,128)} %v_ref.3), custom_call_target="tpu_custom_call" | custom-call | tf_op jit(solution)/shard_map/pallas_call | solution.py:163
  60.1 3.6 %all-to-all-start.2 = ((bf16[4,2,2,128,128]{4,3,2,1,0:T(8,128)(2,1)}), bf16[4,2,2,128,128]{4,3,2,1,0:T(8,128)(2,1)S(1)}, u32[]{:S(2)}, u32[]{:S(2)}) async-start(bf16[4,2,2,128,128]{4,3,2,1,0:T(8,128)(2,1)} %shard_map.69), calls=%async_computation.2 | async-start | bytes 1048576 | tf_op jit(solution)/shard_map/all_to_all | solution.py:276
  63.7 1.1 broadcast_select_fusion
  64.8 13.9 %collective-permute-done.xb_ref = bf16[2,2,512,128]{3,2,1,0:T(8,128)(2,1)S(1)} collective-permute-done((bf16[2,2,512,128]{3,2,1,0:T(8,128)(2,1)}, bf16[2,2,512,128]{3,2,1,0:T(8,128)(2,1)S(1)}, u32[]{:S(2)}, u32[]{:S(2)}) %collective-permute-start) | collective-permute-done | bytes 524320 | tf_op jit(solution)/shard_map/ppermute | solution.py:24
  78.7 1.1 collective-permute-done.1.xa_ref
  80.6 7.4 %shard_map.68 = (f32[2,4,512,128]{3,2,1,0:T(8,128)}, bf16[4,2,6,128,128]{4,3,2,1,0:T(8,128)(2,1)}) custom-call(s32[1]{0:T(128)} %bitcast.flag_ref, f32[2,4,512,128]{3,2,1,0:T(8,128)} %bitcast.53, bf16[2,2,512,128]{3,2,1,0:T(8,128)(2,1)} %copy-done.3, bf16[2,2,512,128]{3,2,1,0:T(8,128)(2,1)} %copy-done.4, f32[4,512,128]{2,1,0:T(8,128)} %d_ref.3, ...), custom_call_target="tpu_custom_call" | custom-call | tf_op jit(solution)/shard_map/pallas_call | solution.py:183
  88.0 3.6 %all-to-all-start.1 = ((bf16[4,2,6,128,128]{4,3,2,1,0:T(8,128)(2,1)}), bf16[4,2,6,128,128]{4,3,2,1,0:T(8,128)(2,1)S(1)}, u32[]{:S(2)}, u32[]{:S(2)}) async-start(bf16[4,2,6,128,128]{4,3,2,1,0:T(8,128)(2,1)} %get-tuple-element.5), calls=%async_computation.1 | async-start | bytes 3145728 | tf_op jit(solution)/shard_map/all_to_all | solution.py:276
  92.5 19.2 %all-to-all-done.1 = bf16[4,2,6,128,128]{4,3,2,1,0:T(8,128)(2,1)S(1)} async-done(((bf16[4,2,6,128,128]{4,3,2,1,0:T(8,128)(2,1)}), bf16[4,2,6,128,128]{4,3,2,1,0:T(8,128)(2,1)S(1)}, u32[]{:S(2)}, u32[]{:S(2)}) %all-to-all-start.1) | async-done | bytes 1572896 | tf_op jit(solution)/shard_map/all_to_all | solution.py:276
  116.1 1.2 collective-permute-done.4
  117.5 3.4 %collective-permute-done.5 = f32[8,8]{1,0:T(8,128)S(1)} collective-permute-done((f32[8,8]{1,0:T(8,128)S(1)}, f32[8,8]{1,0:T(8,128)S(1)}, u32[]{:S(2)}, u32[]{:S(2)}) %collective-permute-start.5) | collective-permute-done | bytes 288 | tf_op jit(solution)/shard_map/ppermute | solution.py:233
  120.9 1.3 %collective-permute-start.6 = (f32[8,8]{1,0:T(8,128)S(1)}, f32[8,8]{1,0:T(8,128)S(1)}, u32[]{:S(2)}, u32[]{:S(2)}) collective-permute-start(f32[8,8]{1,0:T(8,128)S(1)} %add.72), channel_id=1, source_target_pairs={{0,4},{4,0},{8,12},{12,8},{16,20},{20,16},{24,28},{28,24},{1,5},{5... | collective-permute-start | bytes 776 | tf_op jit(solution)/shard_map/ppermute | solution.py:233
  122.2 2.3 %collective-permute-done.6 = f32[8,8]{1,0:T(8,128)S(1)} collective-permute-done((f32[8,8]{1,0:T(8,128)S(1)}, f32[8,8]{1,0:T(8,128)S(1)}, u32[]{:S(2)}, u32[]{:S(2)}) %collective-permute-start.6) | collective-permute-done | bytes 288 | tf_op jit(solution)/shard_map/ppermute | solution.py:233
  125.5 2.6 %collective-permute-done.7 = f32[8,8]{1,0:T(8,128)S(1)} collective-permute-done((f32[8,8]{1,0:T(8,128)S(1)}, f32[8,8]{1,0:T(8,128)S(1)}, u32[]{:S(2)}, u32[]{:S(2)}) %collective-permute-start.7) | collective-permute-done | bytes 288 | tf_op jit(solution)/shard_map/ppermute | solution.py:233
  128.1 2.3 %collective-permute-start.8 = (f32[8,8]{1,0:T(8,128)S(1)}, f32[8,8]{1,0:T(8,128)S(1)}, u32[]{:S(2)}, u32[]{:S(2)}) collective-permute-start(f32[8,8]{1,0:T(8,128)S(1)} %add.74), channel_id=1, source_target_pairs={{0,16},{4,20},{8,24},{12,28},{16,0},{20,4},{24,8},{28,12},{1,17},{... | collective-permute-start | bytes 776 | tf_op jit(solution)/shard_map/ppermute | solution.py:233
  130.4 2.2 %collective-permute-done.8 = f32[8,8]{1,0:T(8,128)S(1)} collective-permute-done((f32[8,8]{1,0:T(8,128)S(1)}, f32[8,8]{1,0:T(8,128)S(1)}, u32[]{:S(2)}, u32[]{:S(2)}) %collective-permute-start.8) | collective-permute-done | bytes 288 | tf_op jit(solution)/shard_map/ppermute | solution.py:233
  (56 shorter events, 14.2 us)
Async XLA Ops:
  6.1 8.8 %copy-start.1 = (f32[4,512,128]{2,1,0:T(8,128)S(1)}, f32[4,512,128]{2,1,0:T(8,128)}, u32[]{:S(2)}) copy-start(f32[4,512,128]{2,1,0:T(8,128)} %d_ref.3) | copy-start | bytes 3145732
  6.2 8.8 %copy-start.2 = (f32[4,512,128]{2,1,0:T(8,128)S(1)}, f32[4,512,128]{2,1,0:T(8,128)}, u32[]{:S(2)}) copy-start(f32[4,512,128]{2,1,0:T(8,128)} %v_ref.3) | copy-start | bytes 3145732
  7.6 35.0 %all-to-all-start = ((f32[2,8,129,128]{3,0,2,1:T(2,128)}), f32[2,8,129,128]{3,0,2,1:T(2,128)}, u32[]{:S(2)}, u32[]{:S(2)}) async-start(f32[2,8,129,128]{3,0,2,1:T(2,128)} %pad_maximum_fusion), calls=%async_computation | async-start | bytes 2113536 | tf_op jit(solution)/shard_map/all_to_all | solution.py:259
  15.1 27.5 %collective-permute-start.2 = (bf16[2,2,512,128]{3,2,1,0:T(8,128)(2,1)S(1)}, bf16[2,2,512,128]{3,2,1,0:T(8,128)(2,1)S(1)}, u32[]{:S(2)}, u32[]{:S(2)}) collective-permute-start(bf16[2,2,512,128]{3,2,1,0:T(8,128)(2,1)S(1)} %fusion.13), channel_id=1, source_target_pairs={{0,4},{1,29},{2,6},{3,31},{4,8},{5,1},{6,10},{7,3},{8,12},{9,5},{1... | collective-permute-start | bytes 1572872 | tf_op jit(solution)/shard_map/ppermute | solution.py:40
  42.6 21.1 %collective-permute-start.3 = (bf16[2,2,512,128]{3,2,1,0:T(8,128)(2,1)S(1)}, bf16[2,2,512,128]{3,2,1,0:T(8,128)(2,1)S(1)}, u32[]{:S(2)}, u32[]{:S(2)}) collective-permute-start(bf16[2,2,512,128]{3,2,1,0:T(8,128)(2,1)S(1)} %collective-permute-done.2), channel_id=1, source_target_pairs={{0,1},{1,0},{2,3},{3,2},{4,5},{5,4},{6,7},{7,6},{8,9},{9,8},{10,11... | collective-permute-start | bytes 1572872 | tf_op jit(solution)/shard_map/ppermute | solution.py:41
  49.8 1.5 %copy-start = (f32[2,2048,128]{2,1,0:T(8,128)}, f32[2,2048,128]{2,1,0:T(8,128)S(1)}, u32[]{:S(2)}) copy-start(f32[2,2048,128]{2,1,0:T(8,128)S(1)} %slice_add_fusion) | copy-start | bytes 6291460
  51.3 27.4 %collective-permute-start = (bf16[2,2,512,128]{3,2,1,0:T(8,128)(2,1)}, bf16[2,2,512,128]{3,2,1,0:T(8,128)(2,1)S(1)}, u32[]{:S(2)}, u32[]{:S(2)}) collective-permute-start(bf16[2,2,512,128]{3,2,1,0:T(8,128)(2,1)} %get-tuple-element.11), channel_id=1, source_target_pairs={{0,4},{4,8},{8,12},{12,16},{16,20},{20,24},{24,28},{28,0},{1,5},{5... | collective-permute-start | bytes 1572872 | tf_op jit(solution)/shard_map/ppermute | solution.py:24
  56.7 23.1 %collective-permute-start.1 = (bf16[2,2,512,128]{3,2,1,0:T(8,128)(2,1)S(1)}, bf16[2,2,512,128]{3,2,1,0:T(8,128)(2,1)S(1)}, u32[]{:S(2)}, u32[]{:S(2)}) collective-permute-start(bf16[2,2,512,128]{3,2,1,0:T(8,128)(2,1)S(1)} %get-tuple-element.10), channel_id=1, source_target_pairs={{4,0},{8,4},{12,8},{16,12},{20,16},{24,20},{28,24},{0,28},{5,1},{9... | collective-permute-start | bytes 1572872 | tf_op jit(solution)/shard_map/ppermute | solution.py:24
  60.1 27.9 %all-to-all-start.2 = ((bf16[4,2,2,128,128]{4,3,2,1,0:T(8,128)(2,1)}), bf16[4,2,2,128,128]{4,3,2,1,0:T(8,128)(2,1)S(1)}, u32[]{:S(2)}, u32[]{:S(2)}) async-start(bf16[4,2,2,128,128]{4,3,2,1,0:T(8,128)(2,1)} %shard_map.69), calls=%async_computation.2 | async-start | bytes 1048576 | tf_op jit(solution)/shard_map/all_to_all | solution.py:276
  78.7 1.1 copy-start.3
  79.8 0.8 copy-start.4
  88.0 23.8 %all-to-all-start.1 = ((bf16[4,2,6,128,128]{4,3,2,1,0:T(8,128)(2,1)}), bf16[4,2,6,128,128]{4,3,2,1,0:T(8,128)(2,1)S(1)}, u32[]{:S(2)}, u32[]{:S(2)}) async-start(bf16[4,2,6,128,128]{4,3,2,1,0:T(8,128)(2,1)} %get-tuple-element.5), calls=%async_computation.1 | async-start | bytes 3145728 | tf_op jit(solution)/shard_map/all_to_all | solution.py:276
  114.3 1.1 copy-start.5
  116.1 1.2 collective-permute-start.4
  117.2 3.6 %collective-permute-start.5 = (f32[8,8]{1,0:T(8,128)S(1)}, f32[8,8]{1,0:T(8,128)S(1)}, u32[]{:S(2)}, u32[]{:S(2)}) collective-permute-start(f32[8,8]{1,0:T(8,128)S(1)} %add.71), channel_id=1, source_target_pairs={{0,2},{1,3},{2,0},{3,1},{4,6},{5,7},{6,4},{7,5},{8,10},{9,11},{10,... | collective-permute-start | bytes 776 | tf_op jit(solution)/shard_map/ppermute | solution.py:233
  120.9 3.6 %collective-permute-start.6 = (f32[8,8]{1,0:T(8,128)S(1)}, f32[8,8]{1,0:T(8,128)S(1)}, u32[]{:S(2)}, u32[]{:S(2)}) collective-permute-start(f32[8,8]{1,0:T(8,128)S(1)} %add.72), channel_id=1, source_target_pairs={{0,4},{4,0},{8,12},{12,8},{16,20},{20,16},{24,28},{28,24},{1,5},{5... | collective-permute-start | bytes 776 | tf_op jit(solution)/shard_map/ppermute | solution.py:233
  124.5 3.6 %collective-permute-start.7 = (f32[8,8]{1,0:T(8,128)S(1)}, f32[8,8]{1,0:T(8,128)S(1)}, u32[]{:S(2)}, u32[]{:S(2)}) collective-permute-start(f32[8,8]{1,0:T(8,128)S(1)} %add.73), channel_id=1, source_target_pairs={{0,8},{4,12},{8,0},{12,4},{16,24},{20,28},{24,16},{28,20},{1,9},{5... | collective-permute-start | bytes 776 | tf_op jit(solution)/shard_map/ppermute | solution.py:233
  128.1 4.5 %collective-permute-start.8 = (f32[8,8]{1,0:T(8,128)S(1)}, f32[8,8]{1,0:T(8,128)S(1)}, u32[]{:S(2)}, u32[]{:S(2)}) collective-permute-start(f32[8,8]{1,0:T(8,128)S(1)} %add.74), channel_id=1, source_target_pairs={{0,16},{4,20},{8,24},{12,28},{16,0},{20,4},{24,8},{28,12},{1,17},{... | collective-permute-start | bytes 776 | tf_op jit(solution)/shard_map/ppermute | solution.py:233

commit v10 on v9

--- a/solution.py
+++ b/solution.py
@@ -26,20 +26,27 @@
 
 def halos_shared(value, width, dim):
     peers, pair = lax.axis_size("space"), lax.axis_size("batch")
-    if pair % 2:
+    if pair % 4 or value.shape[0] != 2:
         return halos(value, "space", width, dim)
     length = value.shape[dim]
-    odd = lax.axis_index("batch") % 2 == 1
+    index = lax.axis_index("batch")
+    upper = index % 2 == 1
+    second = (index // 2) % 2 == 1
     last = lax.slice_in_dim(value, length - width, length, axis=dim)
     initial = lax.slice_in_dim(value, 0, width, axis=dim)
+    side = jnp.where(upper, initial, last)
     routes = []
     for s in range(peers):
         for b in range(pair):
             ahead = (s + 1) % peers if b % 2 == 0 else (s - 1) % peers
             routes.append((s * pair + b, ahead * pair + b))
-    got = lax.ppermute(jnp.where(odd, initial, last).astype(LINK), ("space", "batch"), routes)
+    got = lax.ppermute(jnp.where(second, side[1], side[0]).astype(LINK), ("space", "batch"), routes)
     other = lax.ppermute(got, "batch", [(b, b ^ 1) for b in range(pair)])
-    return jnp.where(odd, other, got), jnp.where(odd, got, other)
+    mine = jnp.stack([jnp.where(upper, other, got), jnp.where(upper, got, other)])
+    theirs = lax.ppermute(mine, "batch", [(b, b ^ 2) for b in range(pair)])
+    first_coef = jnp.where(second, theirs, mine)
+    second_coef = jnp.where(second, mine, theirs)
+    return jnp.stack([first_coef[0], second_coef[0]]), jnp.stack([first_coef[1], second_coef[1]])
 
 
 ROWS = 256
@@ -208,7 +215,7 @@
 
 def pieces(x):
     out, rest = [], x
-    for _ in range(3):
+    for _ in range(2):
         part = lax.reduce_precision(rest, exponent_bits=8, mantissa_bits=7)
         out.append(part.astype(jnp.bfloat16))
         rest = rest - part

time: 134 us -> 131 us (0.978)
  waiting for transfers between devices: 71.2 us -> 65.9 us
  starting transfers between devices: 26.9 us -> 30.6 us
  matrix products: 8.3 us -> 6.5 us
    ppermute x2, waiting for transfers between devices: 15 us -> 12 us  [halos(): return (lax.ppermute(last, axis, up), lax.ppermute(initial, axis, down))]
    ppermute x5, starting transfers between devices: 4.94 us -> 7.72 us  [butterfly(): value = value + lax.ppermute(value, axis, [(i, i ^ step) for i in range(n)])]
    ppermute x1 -> x2, waiting for transfers between devices: 25.5 us -> 23.2 us  [the longest x1 22.6 us: halos_shared(): lax.ppermute(jnp.where(second, side[1], side[0]).astype(LINK), ('space',...]
    another operation x1 -> x5, other arithmetic: 0.16 us -> 1.96 us  [the longest x1 0.85 us: halos_shared(): jnp.stack([first_coef[1], second_coef[1]])]
    dot_general x2, matrix products: 5.21 us -> 3.43 us  [select(): jnp.einsum('fmk,fkd->fmd', onehot, jnp.concatenate(parts, axis=-1), prefe...]
    ppermute x1 -> x2, starting transfers between devices: 2.07 us -> 3.64 us  [the longest x1 2.07 us: halos_shared(): lax.ppermute(jnp.where(second, side[1], side[0]).astype(LINK), ('space',...]
    ppermute x1, waiting for transfers between devices: 0.01 us -> 1.53 us  [halos_shared(): other = lax.ppermute(got, 'batch', [(b, b ^ 1) for b in range(pair)])]
    ppermute x5, waiting for transfers between devices: 11.5 us -> 10.1 us  [butterfly(): value = value + lax.ppermute(value, axis, [(i, i ^ step) for i in range(n)])]
  transfers between devices with their start and end apart: 12 -> 13, of which waited for: 9 -> 11; matrix products, arithmetic and copies ran while one was open for 8% -> 8% of each run, Pallas kernels for 8% -> 8%
where the time goes in v10:
time: 131 us; the launch traced here: 130 us
  waiting for transfers between devices  65.9 us (50%)
  starting transfers between devices  30.6 us (23%)
  Pallas kernels  10.8 us (8%)
  other arithmetic  7.95 us (6%)
  local copies, waits for them, and re-layouts  7.41 us (6%)
  matrix products  6.5 us (5%)
    ppermute x1, waiting for transfers between devices, halos_shared(): lax.ppermute(jnp.where(second, side[1], side[0]).astype(LINK), ('space',...  22.6 us
    all_to_all x2, waiting for transfers between devices, spread(): lax.all_to_all(snap, 'batch', split_axis=0, concat_axis=0, tiled=True)  19.1 us
    ppermute x2, waiting for transfers between devices, halos(): return (lax.ppermute(last, axis, up), lax.ppermute(initial, axis, down))  12 us
    ppermute x5, waiting for transfers between devices, butterfly(): value = value + lax.ppermute(value, axis, [(i, i ^ step) for i in range(n)])  10.1 us
    ppermute x5, starting transfers between devices, butterfly(): value = value + lax.ppermute(value, axis, [(i, i ^ step) for i in range(n)])  7.72 us
    pallas_call x1, Pallas kernels, two_steps(): pl.pallas_call(stencil_kernel, grid=(fields,), in_specs=[pl.BlockSpec(mem...  7.42 us
    all_to_all x1, starting transfers between devices, work(): lax.all_to_all(payload, 'space', split_axis=1, concat_axis=1, tiled=True)  7.28 us
    all_to_all x2, starting transfers between devices, spread(): lax.all_to_all(snap, 'batch', split_axis=0, concat_axis=0, tiled=True)  7.22 us
  transfers between devices with their start and end apart: 13, of which 11 were waited for; matrix products, arithmetic and copies ran while one was open for 8% of the time, Pallas kernels for 8%

profile of v10, /device:TPU:0, one launch (start us, length us, event | category | flops | bytes accessed | tf_op | source)
XLA Modules:
  0.0 130.2 jit_solution(13742152567307943200)
XLA Ops:
  5.2 1.5 %pad_maximum_fusion = f32[2,8,129,128]{3,0,2,1:T(2,128)} fusion(f32[2,8,1,128]{3,0,2,1:T(2,128)S(1)} %convert_bitcast_fusion, f32[2,8,128,128]{3,0,2,1:T(2,128)S(1)} %copy.17), kind=kLoop, calls=%fused_computation.20 | loop fusion | flops 264192 | bytes 2113536 | tf_op jit(solution)/shard_map/concatenate | solution.py:262
  6.7 7.3 %all-to-all-start = ((f32[2,8,129,128]{3,0,2,1:T(2,128)}), f32[2,8,129,128]{3,0,2,1:T(2,128)}, u32[]{:S(2)}, u32[]{:S(2)}) async-start(f32[2,8,129,128]{3,0,2,1:T(2,128)} %pad_maximum_fusion), calls=%async_computation | async-start | bytes 2113536 | tf_op jit(solution)/shard_map/all_to_all | solution.py:266
  14.1 2.1 %collective-permute-start.2 = (bf16[2,512,128]{2,1,0:T(8,128)(2,1)S(1)}, bf16[2,512,128]{2,1,0:T(8,128)(2,1)S(1)}, u32[]{:S(2)}, u32[]{:S(2)}) collective-permute-start(bf16[2,512,128]{2,1,0:T(8,128)(2,1)S(1)} %fusion.15), channel_id=1, source_target_pairs={{0,4},{1,29},{2,6},{3,31},{4,8},{5,1},{6,10},{7,3},{8,12},{9,5},{1... | collective-permute-start | bytes 786440 | tf_op jit(solution)/shard_map/ppermute | solution.py:43
  16.2 22.6 %collective-permute-done.2 = bf16[2,512,128]{2,1,0:T(8,128)(2,1)S(1)} collective-permute-done((bf16[2,512,128]{2,1,0:T(8,128)(2,1)S(1)}, bf16[2,512,128]{2,1,0:T(8,128)(2,1)S(1)}, u32[]{:S(2)}, u32[]{:S(2)}) %collective-permute-start.2) | collective-permute-done | bytes 262176 | tf_op jit(solution)/shard_map/ppermute | solution.py:43
  38.8 1.5 %collective-permute-done.3 = bf16[2,512,128]{2,1,0:T(8,128)(2,1)S(1)} collective-permute-done((bf16[2,512,128]{2,1,0:T(8,128)(2,1)S(1)}, bf16[2,512,128]{2,1,0:T(8,128)(2,1)S(1)}, u32[]{:S(2)}, u32[]{:S(2)}) %collective-permute-start.3) | collective-permute-done | bytes 262176 | tf_op jit(solution)/shard_map/ppermute | solution.py:44
  40.5 1.6 %collective-permute-start.4 = (bf16[2,2,512,128]{3,2,1,0:T(8,128)(2,1)S(1)}, bf16[2,2,512,128]{3,2,1,0:T(8,128)(2,1)S(1)}, u32[]{:S(2)}, u32[]{:S(2)}) collective-permute-start(bf16[2,2,512,128]{3,2,1,0:T(8,128)(2,1)S(1)} %pad_maximum_fusion.2), channel_id=1, source_target_pairs={{0,2},{1,3},{2,0},{3,1},{4,6},{5,7},{6,4},{7,5},{8,10},{9,11},{10,... | collective-permute-start | bytes 1572872 | tf_op jit(solution)/shard_map/ppermute | solution.py:46
  42.1 1.3 slice.120
  44.3 3.0 %fusion = f32[2,2048,256]{2,1,0:T(8,128)S(1)} fusion(s32[2,1024]{1,0:T(2,128)S(1)} %fusion.27, bf16[2,1024,128]{2,1,0:T(8,128)(2,1)S(1)} %get-tuple-element.13, bf16[2,1024,128]{2,1,0:T(8,128)(2,1)S(1)} %get-tuple-element.12), kind=kOutput, calls=%fused_computation.1 | convolution fusion | flops 2153775104 | bytes 5251072 | tf_op jit(solution)/shard_map/fmk,fkd->fmd/dot_general | solution.py:228
  47.7 1.3 fusion.31
  49.2 2.2 %collective-permute-start = (bf16[2,2,512,128]{3,2,1,0:T(8,128)(2,1)}, bf16[2,2,512,128]{3,2,1,0:T(8,128)(2,1)S(1)}, u32[]{:S(2)}, u32[]{:S(2)}) collective-permute-start(bf16[2,2,512,128]{3,2,1,0:T(8,128)(2,1)} %get-tuple-element.11), channel_id=1, source_target_pairs={{0,4},{4,8},{8,12},{12,16},{16,20},{20,24},{24,28},{28,0},{1,5},{5... | collective-permute-start | bytes 1572872 | tf_op jit(solution)/shard_map/ppermute | solution.py:24
  51.4 2.6 %collective-permute-start.1 = (bf16[2,2,512,128]{3,2,1,0:T(8,128)(2,1)}, bf16[2,2,512,128]{3,2,1,0:T(8,128)(2,1)S(1)}, u32[]{:S(2)}, u32[]{:S(2)}) collective-permute-start(bf16[2,2,512,128]{3,2,1,0:T(8,128)(2,1)} %get-tuple-element.10), channel_id=1, source_target_pairs={{4,0},{8,4},{12,8},{16,12},{20,16},{24,20},{28,24},{0,28},{5,1},{9... | collective-permute-start | bytes 1572872 | tf_op jit(solution)/shard_map/ppermute | solution.py:24
  54.6 3.4 %shard_map.69 = bf16[4,2,2,128,128]{4,3,2,1,0:T(8,128)(2,1)} custom-call(s32[1]{0:T(128)} %bitcast.flag_ref, f32[2,4,512,128]{3,2,1,0:T(8,128)} %bitcast.54, f32[4,512,128]{2,1,0:T(8,128)} %d_ref.3, f32[4,512,128]{2,1,0:T(8,128)} %v_ref.3), custom_call_target="tpu_custom_call" | custom-call | tf_op jit(solution)/shard_map/pallas_call | solution.py:170
  58.0 3.6 %all-to-all-start.2 = ((bf16[4,2,2,128,128]{4,3,2,1,0:T(8,128)(2,1)}), bf16[4,2,2,128,128]{4,3,2,1,0:T(8,128)(2,1)S(1)}, u32[]{:S(2)}, u32[]{:S(2)}) async-start(bf16[4,2,2,128,128]{4,3,2,1,0:T(8,128)(2,1)} %shard_map.69), calls=%async_computation.2 | async-start | bytes 1048576 | tf_op jit(solution)/shard_map/all_to_all | solution.py:283
  63.4 10.0 %collective-permute-done.xb_ref = bf16[2,2,512,128]{3,2,1,0:T(8,128)(2,1)S(1)} collective-permute-done((bf16[2,2,512,128]{3,2,1,0:T(8,128)(2,1)}, bf16[2,2,512,128]{3,2,1,0:T(8,128)(2,1)S(1)}, u32[]{:S(2)}, u32[]{:S(2)}) %collective-permute-start) | collective-permute-done | bytes 524320 | tf_op jit(solution)/shard_map/ppermute | solution.py:24
  73.4 2.1 %collective-permute-done.1.xa_ref = bf16[2,2,512,128]{3,2,1,0:T(8,128)(2,1)S(1)} collective-permute-done((bf16[2,2,512,128]{3,2,1,0:T(8,128)(2,1)}, bf16[2,2,512,128]{3,2,1,0:T(8,128)(2,1)S(1)}, u32[]{:S(2)}, u32[]{:S(2)}) %collective-permute-start.1) | collective-permute-done | bytes 524320 | tf_op jit(solution)/shard_map/ppermute | solution.py:24
  76.3 7.4 %shard_map.68 = (f32[2,4,512,128]{3,2,1,0:T(8,128)}, bf16[4,2,6,128,128]{4,3,2,1,0:T(8,128)(2,1)}) custom-call(s32[1]{0:T(128)} %bitcast.flag_ref, f32[2,4,512,128]{3,2,1,0:T(8,128)} %bitcast.55, bf16[2,2,512,128]{3,2,1,0:T(8,128)(2,1)} %copy-done.3, bf16[2,2,512,128]{3,2,1,0:T(8,128)(2,1)} %copy-done.4, f32[4,512,128]{2,1,0:T(8,128)} %d_ref.3, ...), custom_call_target="tpu_custom_call" | custom-call | tf_op jit(solution)/shard_map/pallas_call | solution.py:190
  83.7 3.6 %all-to-all-start.1 = ((bf16[4,2,6,128,128]{4,3,2,1,0:T(8,128)(2,1)}), bf16[4,2,6,128,128]{4,3,2,1,0:T(8,128)(2,1)S(1)}, u32[]{:S(2)}, u32[]{:S(2)}) async-start(bf16[4,2,6,128,128]{4,3,2,1,0:T(8,128)(2,1)} %get-tuple-element.5), calls=%async_computation.1 | async-start | bytes 3145728 | tf_op jit(solution)/shard_map/all_to_all | solution.py:283
  88.3 19.1 %all-to-all-done.1 = bf16[4,2,6,128,128]{4,3,2,1,0:T(8,128)(2,1)S(1)} async-done(((bf16[4,2,6,128,128]{4,3,2,1,0:T(8,128)(2,1)}), bf16[4,2,6,128,128]{4,3,2,1,0:T(8,128)(2,1)S(1)}, u32[]{:S(2)}, u32[]{:S(2)}) %all-to-all-start.1) | async-done | bytes 1572896 | tf_op jit(solution)/shard_map/all_to_all | solution.py:283
  113.3 3.2 %collective-permute-done.6 = f32[8,8]{1,0:T(8,128)S(1)} collective-permute-done((f32[8,8]{1,0:T(8,128)S(1)}, f32[8,8]{1,0:T(8,128)S(1)}, u32[]{:S(2)}, u32[]{:S(2)}) %collective-permute-start.6) | collective-permute-done | bytes 288 | tf_op jit(solution)/shard_map/ppermute | solution.py:240
  117.6 2.5 %collective-permute-done.7 = f32[8,8]{1,0:T(8,128)S(1)} collective-permute-done((f32[8,8]{1,0:T(8,128)S(1)}, f32[8,8]{1,0:T(8,128)S(1)}, u32[]{:S(2)}, u32[]{:S(2)}) %collective-permute-start.7) | collective-permute-done | bytes 288 | tf_op jit(solution)/shard_map/ppermute | solution.py:240
  120.1 3.2 %collective-permute-start.8 = (f32[8,8]{1,0:T(8,128)S(1)}, f32[8,8]{1,0:T(8,128)S(1)}, u32[]{:S(2)}, u32[]{:S(2)}) collective-permute-start(f32[8,8]{1,0:T(8,128)S(1)} %add.70), channel_id=1, source_target_pairs={{0,8},{4,12},{8,0},{12,4},{16,24},{20,28},{24,16},{28,20},{1,9},{5... | collective-permute-start | bytes 776 | tf_op jit(solution)/shard_map/ppermute | solution.py:240
  123.3 1.6 %collective-permute-done.8 = f32[8,8]{1,0:T(8,128)S(1)} collective-permute-done((f32[8,8]{1,0:T(8,128)S(1)}, f32[8,8]{1,0:T(8,128)S(1)}, u32[]{:S(2)}, u32[]{:S(2)}) %collective-permute-start.8) | collective-permute-done | bytes 288 | tf_op jit(solution)/shard_map/ppermute | solution.py:240
  124.9 3.1 %collective-permute-start.9 = (f32[8,8]{1,0:T(8,128)S(1)}, f32[8,8]{1,0:T(8,128)S(1)}, u32[]{:S(2)}, u32[]{:S(2)}) collective-permute-start(f32[8,8]{1,0:T(8,128)S(1)} %add.71), channel_id=1, source_target_pairs={{0,16},{4,20},{8,24},{12,28},{16,0},{20,4},{24,8},{28,12},{1,17},{... | collective-permute-start | bytes 776 | tf_op jit(solution)/shard_map/ppermute | solution.py:240
  128.0 1.6 %collective-permute-done.9 = f32[8,8]{1,0:T(8,128)S(1)} collective-permute-done((f32[8,8]{1,0:T(8,128)S(1)}, f32[8,8]{1,0:T(8,128)S(1)}, u32[]{:S(2)}, u32[]{:S(2)}) %collective-permute-start.9) | collective-permute-done | bytes 288 | tf_op jit(solution)/shard_map/ppermute | solution.py:240
  (66 shorter events, 18.0 us)
Async XLA Ops:
  3.8 0.9 copy-start.6
  5.2 8.8 %copy-start.1 = (f32[4,512,128]{2,1,0:T(8,128)S(1)}, f32[4,512,128]{2,1,0:T(8,128)}, u32[]{:S(2)}) copy-start(f32[4,512,128]{2,1,0:T(8,128)} %d_ref.3) | copy-start | bytes 3145732
  5.2 8.8 %copy-start.2 = (f32[4,512,128]{2,1,0:T(8,128)S(1)}, f32[4,512,128]{2,1,0:T(8,128)}, u32[]{:S(2)}) copy-start(f32[4,512,128]{2,1,0:T(8,128)} %v_ref.3) | copy-start | bytes 3145732
  6.7 35.4 %all-to-all-start = ((f32[2,8,129,128]{3,0,2,1:T(2,128)}), f32[2,8,129,128]{3,0,2,1:T(2,128)}, u32[]{:S(2)}, u32[]{:S(2)}) async-start(f32[2,8,129,128]{3,0,2,1:T(2,128)} %pad_maximum_fusion), calls=%async_computation | async-start | bytes 2113536 | tf_op jit(solution)/shard_map/all_to_all | solution.py:266
  14.1 24.7 %collective-permute-start.2 = (bf16[2,512,128]{2,1,0:T(8,128)(2,1)S(1)}, bf16[2,512,128]{2,1,0:T(8,128)(2,1)S(1)}, u32[]{:S(2)}, u32[]{:S(2)}) collective-permute-start(bf16[2,512,128]{2,1,0:T(8,128)(2,1)S(1)} %fusion.15), channel_id=1, source_target_pairs={{0,4},{1,29},{2,6},{3,31},{4,8},{5,1},{6,10},{7,3},{8,12},{9,5},{1... | collective-permute-start | bytes 786440 | tf_op jit(solution)/shard_map/ppermute | solution.py:43
  38.8 1.5 %collective-permute-start.3 = (bf16[2,512,128]{2,1,0:T(8,128)(2,1)S(1)}, bf16[2,512,128]{2,1,0:T(8,128)(2,1)S(1)}, u32[]{:S(2)}, u32[]{:S(2)}) collective-permute-start(bf16[2,512,128]{2,1,0:T(8,128)(2,1)S(1)} %collective-permute-done.2), channel_id=1, source_target_pairs={{0,1},{1,0},{2,3},{3,2},{4,5},{5,4},{6,7},{7,6},{8,9},{9,8},{10,11... | collective-permute-start | bytes 786440 | tf_op jit(solution)/shard_map/ppermute | solution.py:44
  40.5 14.0 %collective-permute-start.4 = (bf16[2,2,512,128]{3,2,1,0:T(8,128)(2,1)S(1)}, bf16[2,2,512,128]{3,2,1,0:T(8,128)(2,1)S(1)}, u32[]{:S(2)}, u32[]{:S(2)}) collective-permute-start(bf16[2,2,512,128]{3,2,1,0:T(8,128)(2,1)S(1)} %pad_maximum_fusion.2), channel_id=1, source_target_pairs={{0,2},{1,3},{2,0},{3,1},{4,6},{5,7},{6,4},{7,5},{8,10},{9,11},{10,... | collective-permute-start | bytes 1572872 | tf_op jit(solution)/shard_map/ppermute | solution.py:46
  47.6 1.7 %copy-start = (f32[2,2048,128]{2,1,0:T(8,128)}, f32[2,2048,128]{2,1,0:T(8,128)S(1)}, u32[]{:S(2)}) copy-start(f32[2,2048,128]{2,1,0:T(8,128)S(1)} %slice_add_fusion) | copy-start | bytes 6291460
  49.2 24.2 %collective-permute-start = (bf16[2,2,512,128]{3,2,1,0:T(8,128)(2,1)}, bf16[2,2,512,128]{3,2,1,0:T(8,128)(2,1)S(1)}, u32[]{:S(2)}, u32[]{:S(2)}) collective-permute-start(bf16[2,2,512,128]{3,2,1,0:T(8,128)(2,1)} %get-tuple-element.11), channel_id=1, source_target_pairs={{0,4},{4,8},{8,12},{12,16},{16,20},{20,24},{24,28},{28,0},{1,5},{5... | collective-permute-start | bytes 1572872 | tf_op jit(solution)/shard_map/ppermute | solution.py:24
  51.4 24.1 %collective-permute-start.1 = (bf16[2,2,512,128]{3,2,1,0:T(8,128)(2,1)}, bf16[2,2,512,128]{3,2,1,0:T(8,128)(2,1)S(1)}, u32[]{:S(2)}, u32[]{:S(2)}) collective-permute-start(bf16[2,2,512,128]{3,2,1,0:T(8,128)(2,1)} %get-tuple-element.10), channel_id=1, source_target_pairs={{4,0},{8,4},{12,8},{16,12},{20,16},{24,20},{28,24},{0,28},{5,1},{9... | collective-permute-start | bytes 1572872 | tf_op jit(solution)/shard_map/ppermute | solution.py:24
  58.0 25.7 %all-to-all-start.2 = ((bf16[4,2,2,128,128]{4,3,2,1,0:T(8,128)(2,1)}), bf16[4,2,2,128,128]{4,3,2,1,0:T(8,128)(2,1)S(1)}, u32[]{:S(2)}, u32[]{:S(2)}) async-start(bf16[4,2,2,128,128]{4,3,2,1,0:T(8,128)(2,1)} %shard_map.69), calls=%async_computation.2 | async-start | bytes 1048576 | tf_op jit(solution)/shard_map/all_to_all | solution.py:283
  73.4 2.1 %copy-start.3 = (bf16[2,2,512,128]{3,2,1,0:T(8,128)(2,1)}, bf16[2,2,512,128]{3,2,1,0:T(8,128)(2,1)S(1)}, u32[]{:S(2)}) copy-start(bf16[2,2,512,128]{3,2,1,0:T(8,128)(2,1)S(1)} %collective-permute-done.xb_ref) | copy-start | bytes 1572868
  75.5 0.8 copy-start.4
  83.7 23.6 %all-to-all-start.1 = ((bf16[4,2,6,128,128]{4,3,2,1,0:T(8,128)(2,1)}), bf16[4,2,6,128,128]{4,3,2,1,0:T(8,128)(2,1)S(1)}, u32[]{:S(2)}, u32[]{:S(2)}) async-start(bf16[4,2,6,128,128]{4,3,2,1,0:T(8,128)(2,1)} %get-tuple-element.5), calls=%async_computation.1 | async-start | bytes 3145728 | tf_op jit(solution)/shard_map/all_to_all | solution.py:283
  109.8 1.0 copy-start.5
  111.7 1.2 collective-permute-start.5
  112.9 3.6 %collective-permute-start.6 = (f32[8,8]{1,0:T(8,128)S(1)}, f32[8,8]{1,0:T(8,128)S(1)}, u32[]{:S(2)}, u32[]{:S(2)}) collective-permute-start(f32[8,8]{1,0:T(8,128)S(1)} %add.68), channel_id=1, source_target_pairs={{0,2},{1,3},{2,0},{3,1},{4,6},{5,7},{6,4},{7,5},{8,10},{9,11},{10,... | collective-permute-start | bytes 776 | tf_op jit(solution)/shard_map/ppermute | solution.py:240
  116.5 3.6 %collective-permute-start.7 = (f32[8,8]{1,0:T(8,128)S(1)}, f32[8,8]{1,0:T(8,128)S(1)}, u32[]{:S(2)}, u32[]{:S(2)}) collective-permute-start(f32[8,8]{1,0:T(8,128)S(1)} %add.69), channel_id=1, source_target_pairs={{0,4},{4,0},{8,12},{12,8},{16,20},{20,16},{24,28},{28,24},{1,5},{5... | collective-permute-start | bytes 776 | tf_op jit(solution)/shard_map/ppermute | solution.py:240
  120.1 4.8 %collective-permute-start.8 = (f32[8,8]{1,0:T(8,128)S(1)}, f32[8,8]{1,0:T(8,128)S(1)}, u32[]{:S(2)}, u32[]{:S(2)}) collective-permute-start(f32[8,8]{1,0:T(8,128)S(1)} %add.70), channel_id=1, source_target_pairs={{0,8},{4,12},{8,0},{12,4},{16,24},{20,28},{24,16},{28,20},{1,9},{5... | collective-permute-start | bytes 776 | tf_op jit(solution)/shard_map/ppermute | solution.py:240
  124.9 4.6 %collective-permute-start.9 = (f32[8,8]{1,0:T(8,128)S(1)}, f32[8,8]{1,0:T(8,128)S(1)}, u32[]{:S(2)}, u32[]{:S(2)}) collective-permute-start(f32[8,8]{1,0:T(8,128)S(1)} %add.71), channel_id=1, source_target_pairs={{0,16},{4,20},{8,24},{12,28},{16,0},{20,4},{24,8},{28,12},{1,17},{... | collective-permute-start | bytes 776 | tf_op jit(solution)/shard_map/ppermute | solution.py:240

commit v11 on v9

--- a/solution.py
+++ b/solution.py
@@ -208,7 +208,7 @@
 
 def pieces(x):
     out, rest = [], x
-    for _ in range(3):
+    for _ in range(2):
         part = lax.reduce_precision(rest, exponent_bits=8, mantissa_bits=7)
         out.append(part.astype(jnp.bfloat16))
         rest = rest - part
@@ -277,21 +277,13 @@
         return mixed.reshape(mixed.shape[0] * mixed.shape[1], mixed.shape[2], -1)
 
     inner, late = spread(inner), spread(late)
-    snaps = [(late[:, 0:2], inner), (late[:, 2:4], late[:, 4:])]
-    rows = []
-    for sensed in snaps:
-        row = []
-        for actuated in snaps:
-            block = None
-            for s_part, a_part in zip(sensed, actuated):
-                term = lax.dot_general(
-                    s_part[ACT:ACT + SENS].reshape(SENS, -1), a_part[:ACT].reshape(ACT, -1),
-                    (((1,), (1,)), ((), ())), preferred_element_type=jnp.float32,
-                )
-                block = term if block is None else block + term
-            row.append(block)
-        rows.append(jnp.concatenate(row, axis=1))
-    partial_gram = jnp.concatenate(rows, axis=0)
+    levels = [late[:, 0:4].reshape(late.shape[0], STEPS, 2, -1), jnp.stack([inner, late[:, 4:]], axis=1)]
+    partial_gram = None
+    for group in levels:
+        term = jnp.einsum(
+            "jtpc,iupc->tjui", group[ACT:ACT + SENS], group[:ACT], preferred_element_type=jnp.float32
+        ).reshape(STEPS * SENS, STEPS * ACT)
+        partial_gram = term if partial_gram is None else partial_gram + term
     scale = 4.0 / math.sqrt(planes * count * span * depth)
     gram = butterfly(partial_gram, ("batch", "space")) * scale
     return (state, gram)

time: 134 us -> 134 us (level)
    dot_general x8 -> x2, matrix products: 3.09 us -> 5.02 us  [work(): jnp.einsum('jtpc,iupc->tjui', group[ACT:ACT + SENS], group[:ACT], preferr...]
    dot_general x2, matrix products: 5.21 us -> 3.43 us  [select(): jnp.einsum('fmk,fkd->fmd', onehot, jnp.concatenate(parts, axis=-1), prefe...]
  transfers between devices with their start and end apart: 12 -> 12, of which waited for: 9 -> 9; matrix products, arithmetic and copies ran while one was open for 8% -> 7% of each run, Pallas kernels for 8% -> 8%
where the time goes in v11:
time: 134 us; the launch traced here: 133 us
  waiting for transfers between devices  71 us (53%)
  starting transfers between devices  26.9 us (20%)
  Pallas kernels  10.8 us (8%)
  matrix products  8.45 us (6%)
  local copies, waits for them, and re-layouts  8.35 us (6%)
  other arithmetic  7.05 us (5%)
    ppermute x1, waiting for transfers between devices, halos_shared(): lax.ppermute(jnp.where(odd, initial, last).astype(LINK), ('space', 'batch...  25.5 us
    all_to_all x2, waiting for transfers between devices, spread(): lax.all_to_all(snap, 'batch', split_axis=0, concat_axis=0, tiled=True)  19 us
    ppermute x2, waiting for transfers between devices, halos(): return (lax.ppermute(last, axis, up), lax.ppermute(initial, axis, down))  15 us
    ppermute x5, waiting for transfers between devices, butterfly(): value = value + lax.ppermute(value, axis, [(i, i ^ step) for i in range(n)])  11.6 us
    pallas_call x1, Pallas kernels, two_steps(): pl.pallas_call(stencil_kernel, grid=(fields,), in_specs=[pl.BlockSpec(mem...  7.42 us
    all_to_all x1, starting transfers between devices, work(): lax.all_to_all(payload, 'space', split_axis=1, concat_axis=1, tiled=True)  7.28 us
    all_to_all x2, starting transfers between devices, spread(): lax.all_to_all(snap, 'batch', split_axis=0, concat_axis=0, tiled=True)  7.23 us
    ppermute x2, starting transfers between devices, halos(): return (lax.ppermute(last, axis, up), lax.ppermute(initial, axis, down))  5.37 us
  transfers between devices with their start and end apart: 12, of which 9 were waited for; matrix products, arithmetic and copies ran while one was open for 7% of the time, Pallas kernels for 8%

profile of v11, /device:TPU:0, one launch (start us, length us, event | category | flops | bytes accessed | tf_op | source)
XLA Modules:
  0.0 133.4 jit_solution(6092268174460452298)
XLA Ops:
  5.2 1.5 %pad_maximum_fusion = f32[2,8,129,128]{3,0,2,1:T(2,128)} fusion(f32[2,8,1,128]{3,0,2,1:T(2,128)S(1)} %convert_bitcast_fusion, f32[2,8,128,128]{3,0,2,1:T(2,128)S(1)} %copy.20), kind=kLoop, calls=%fused_computation.15 | loop fusion | flops 264192 | bytes 2113536 | tf_op jit(solution)/shard_map/concatenate | solution.py:255
  6.7 7.3 %all-to-all-start = ((f32[2,8,129,128]{3,0,2,1:T(2,128)}), f32[2,8,129,128]{3,0,2,1:T(2,128)}, u32[]{:S(2)}, u32[]{:S(2)}) async-start(f32[2,8,129,128]{3,0,2,1:T(2,128)} %pad_maximum_fusion), calls=%async_computation | async-start | bytes 2113536 | tf_op jit(solution)/shard_map/all_to_all | solution.py:259
  14.1 2.1 %collective-permute-start.2 = (bf16[2,2,512,128]{3,2,1,0:T(8,128)(2,1)S(1)}, bf16[2,2,512,128]{3,2,1,0:T(8,128)(2,1)S(1)}, u32[]{:S(2)}, u32[]{:S(2)}) collective-permute-start(bf16[2,2,512,128]{3,2,1,0:T(8,128)(2,1)S(1)} %fusion.9), channel_id=1, source_target_pairs={{0,4},{1,29},{2,6},{3,31},{4,8},{5,1},{6,10},{7,3},{8,12},{9,5},{1... | collective-permute-start | bytes 1572872 | tf_op jit(solution)/shard_map/ppermute | solution.py:40
  16.2 25.5 %collective-permute-done.2 = bf16[2,2,512,128]{3,2,1,0:T(8,128)(2,1)S(1)} collective-permute-done((bf16[2,2,512,128]{3,2,1,0:T(8,128)(2,1)S(1)}, bf16[2,2,512,128]{3,2,1,0:T(8,128)(2,1)S(1)}, u32[]{:S(2)}, u32[]{:S(2)}) %collective-permute-start.2) | collective-permute-done | bytes 524320 | tf_op jit(solution)/shard_map/ppermute | solution.py:40
  41.6 1.3 slice.76
  43.9 3.0 %fusion = f32[2,2048,256]{2,1,0:T(8,128)S(1)} fusion(s32[2,1024]{1,0:T(2,128)S(1)} %fusion.25, bf16[2,1024,128]{2,1,0:T(8,128)(2,1)S(1)} %get-tuple-element.13, bf16[2,1024,128]{2,1,0:T(8,128)(2,1)S(1)} %get-tuple-element.12), kind=kOutput, calls=%fused_computation.1 | convolution fusion | flops 2153775104 | bytes 5251072 | tf_op jit(solution)/shard_map/fmk,fkd->fmd/dot_general | solution.py:221
  48.6 5.4 %collective-permute-start = (bf16[2,2,512,128]{3,2,1,0:T(8,128)(2,1)}, bf16[2,2,512,128]{3,2,1,0:T(8,128)(2,1)S(1)}, u32[]{:S(2)}, u32[]{:S(2)}) collective-permute-start(bf16[2,2,512,128]{3,2,1,0:T(8,128)(2,1)} %get-tuple-element.11), channel_id=1, source_target_pairs={{0,4},{4,8},{8,12},{12,16},{16,20},{20,24},{24,28},{28,0},{1,5},{5... | collective-permute-start | bytes 1572872 | tf_op jit(solution)/shard_map/ppermute | solution.py:24
  54.0 3.4 %shard_map.69 = bf16[4,2,2,128,128]{4,3,2,1,0:T(8,128)(2,1)} custom-call(s32[1]{0:T(128)} %bitcast.flag_ref, f32[2,4,512,128]{3,2,1,0:T(8,128)} %bitcast.56, f32[4,512,128]{2,1,0:T(8,128)} %d_ref.3, f32[4,512,128]{2,1,0:T(8,128)} %v_ref.3), custom_call_target="tpu_custom_call" | custom-call | tf_op jit(solution)/shard_map/pallas_call | solution.py:163
  57.4 3.6 %all-to-all-start.2 = ((bf16[4,2,2,128,128]{4,3,2,1,0:T(8,128)(2,1)}), bf16[4,2,2,128,128]{4,3,2,1,0:T(8,128)(2,1)S(1)}, u32[]{:S(2)}, u32[]{:S(2)}) async-start(bf16[4,2,2,128,128]{4,3,2,1,0:T(8,128)(2,1)} %shard_map.69), calls=%async_computation.2 | async-start | bytes 1048576 | tf_op jit(solution)/shard_map/all_to_all | solution.py:276
  62.1 13.9 %collective-permute-done.xb_ref = bf16[2,2,512,128]{3,2,1,0:T(8,128)(2,1)S(1)} collective-permute-done((bf16[2,2,512,128]{3,2,1,0:T(8,128)(2,1)}, bf16[2,2,512,128]{3,2,1,0:T(8,128)(2,1)S(1)}, u32[]{:S(2)}, u32[]{:S(2)}) %collective-permute-start) | collective-permute-done | bytes 524320 | tf_op jit(solution)/shard_map/ppermute | solution.py:24
  76.0 1.1 collective-permute-done.1.xa_ref
  77.9 7.4 %shard_map.68 = (f32[2,4,512,128]{3,2,1,0:T(8,128)}, bf16[4,2,6,128,128]{4,3,2,1,0:T(8,128)(2,1)}) custom-call(s32[1]{0:T(128)} %bitcast.flag_ref, f32[2,4,512,128]{3,2,1,0:T(8,128)} %bitcast.57, bf16[2,2,512,128]{3,2,1,0:T(8,128)(2,1)} %copy-done.3, bf16[2,2,512,128]{3,2,1,0:T(8,128)(2,1)} %copy-done.4, f32[4,512,128]{2,1,0:T(8,128)} %d_ref.3, ...), custom_call_target="tpu_custom_call" | custom-call | tf_op jit(solution)/shard_map/pallas_call | solution.py:183
  85.3 3.6 %all-to-all-start.1 = ((bf16[4,2,6,128,128]{4,3,2,1,0:T(8,128)(2,1)}), bf16[4,2,6,128,128]{4,3,2,1,0:T(8,128)(2,1)S(1)}, u32[]{:S(2)}, u32[]{:S(2)}) async-start(bf16[4,2,6,128,128]{4,3,2,1,0:T(8,128)(2,1)} %get-tuple-element.5), calls=%async_computation.1 | async-start | bytes 3145728 | tf_op jit(solution)/shard_map/all_to_all | solution.py:276
  89.0 1.1 copy.23
  90.1 19.0 %all-to-all-done.1 = bf16[4,2,6,128,128]{4,3,2,1,0:T(8,128)(2,1)S(1)} async-done(((bf16[4,2,6,128,128]{4,3,2,1,0:T(8,128)(2,1)}), bf16[4,2,6,128,128]{4,3,2,1,0:T(8,128)(2,1)S(1)}, u32[]{:S(2)}, u32[]{:S(2)}) %all-to-all-start.1) | async-done | bytes 1572896 | tf_op jit(solution)/shard_map/all_to_all | solution.py:276
  111.1 2.5 %convolution_bitcast_fusion = f32[4,2,4,2]{2,0,3,1:T(4,128)S(1)} fusion(bf16[8,1,2,16384]{3,0,2,1:T(8,128)(2,1)S(1)} %copy-done.5, bf16[8,1,2,16384]{3,0,2,1:T(8,128)(2,1)S(1)} %slice_bitcast_fusion), kind=kOutput, calls=%fused_computation.11 | convolution fusion | flops 6291456 | bytes 2097408 | tf_op jit(solution)/shard_map/jtpc,iupc->tjui/dot_general | solution.py:283
  113.6 2.5 %fusion.4 = f32[2,4,2,4]{1,3,0,2:T(4,128)S(1)} fusion(f32[4,2,4,2]{2,0,3,1:T(4,128)S(1)} %convolution_bitcast_fusion, bf16[4,2,2,16384,1]{3,0,2,4,1:T(4,128)(2,1)S(1)} %bitcast.62, bf16[4,2,2,16384,1]{3,0,2,1,4:T(4,128)(2,1)S(1)} %bitcast.61), kind=kOutput, calls=%fused_computation.14 | convolution fusion | flops 4194368 | bytes 1049088 | tf_op jit(solution)/shard_map/jtpc,iupc->tjui/dot_general | solution.py:283
  116.3 1.2 collective-permute-done.4
  117.7 3.4 %collective-permute-done.5 = f32[8,8]{1,0:T(8,128)S(1)} collective-permute-done((f32[8,8]{1,0:T(8,128)S(1)}, f32[8,8]{1,0:T(8,128)S(1)}, u32[]{:S(2)}, u32[]{:S(2)}) %collective-permute-start.5) | collective-permute-done | bytes 288 | tf_op jit(solution)/shard_map/ppermute | solution.py:233
  121.1 1.3 collective-permute-start.6
  122.4 2.3 %collective-permute-done.6 = f32[8,8]{1,0:T(8,128)S(1)} collective-permute-done((f32[8,8]{1,0:T(8,128)S(1)}, f32[8,8]{1,0:T(8,128)S(1)}, u32[]{:S(2)}, u32[]{:S(2)}) %collective-permute-start.6) | collective-permute-done | bytes 288 | tf_op jit(solution)/shard_map/ppermute | solution.py:233
  125.7 2.6 %collective-permute-done.7 = f32[8,8]{1,0:T(8,128)S(1)} collective-permute-done((f32[8,8]{1,0:T(8,128)S(1)}, f32[8,8]{1,0:T(8,128)S(1)}, u32[]{:S(2)}, u32[]{:S(2)}) %collective-permute-start.7) | collective-permute-done | bytes 288 | tf_op jit(solution)/shard_map/ppermute | solution.py:233
  128.3 2.3 %collective-permute-start.8 = (f32[8,8]{1,0:T(8,128)S(1)}, f32[8,8]{1,0:T(8,128)S(1)}, u32[]{:S(2)}, u32[]{:S(2)}) collective-permute-start(f32[8,8]{1,0:T(8,128)S(1)} %add.62), channel_id=1, source_target_pairs={{0,16},{4,20},{8,24},{12,28},{16,0},{20,4},{24,8},{28,12},{1,17},{... | collective-permute-start | bytes 776 | tf_op jit(solution)/shard_map/ppermute | solution.py:233
  130.6 2.2 %collective-permute-done.8 = f32[8,8]{1,0:T(8,128)S(1)} collective-permute-done((f32[8,8]{1,0:T(8,128)S(1)}, f32[8,8]{1,0:T(8,128)S(1)}, u32[]{:S(2)}, u32[]{:S(2)}) %collective-permute-start.8) | collective-permute-done | bytes 288 | tf_op jit(solution)/shard_map/ppermute | solution.py:233
  (53 shorter events, 13.3 us)
Async XLA Ops:
  3.8 0.9 copy-start.6
  5.2 8.8 %copy-start.1 = (f32[4,512,128]{2,1,0:T(8,128)S(1)}, f32[4,512,128]{2,1,0:T(8,128)}, u32[]{:S(2)}) copy-start(f32[4,512,128]{2,1,0:T(8,128)} %d_ref.3) | copy-start | bytes 3145732
  5.2 8.8 %copy-start.2 = (f32[4,512,128]{2,1,0:T(8,128)S(1)}, f32[4,512,128]{2,1,0:T(8,128)}, u32[]{:S(2)}) copy-start(f32[4,512,128]{2,1,0:T(8,128)} %v_ref.3) | copy-start | bytes 3145732
  6.7 35.0 %all-to-all-start = ((f32[2,8,129,128]{3,0,2,1:T(2,128)}), f32[2,8,129,128]{3,0,2,1:T(2,128)}, u32[]{:S(2)}, u32[]{:S(2)}) async-start(f32[2,8,129,128]{3,0,2,1:T(2,128)} %pad_maximum_fusion), calls=%async_computation | async-start | bytes 2113536 | tf_op jit(solution)/shard_map/all_to_all | solution.py:259
  14.1 27.5 %collective-permute-start.2 = (bf16[2,2,512,128]{3,2,1,0:T(8,128)(2,1)S(1)}, bf16[2,2,512,128]{3,2,1,0:T(8,128)(2,1)S(1)}, u32[]{:S(2)}, u32[]{:S(2)}) collective-permute-start(bf16[2,2,512,128]{3,2,1,0:T(8,128)(2,1)S(1)} %fusion.9), channel_id=1, source_target_pairs={{0,4},{1,29},{2,6},{3,31},{4,8},{5,1},{6,10},{7,3},{8,12},{9,5},{1... | collective-permute-start | bytes 1572872 | tf_op jit(solution)/shard_map/ppermute | solution.py:40
  41.6 19.4 %collective-permute-start.3 = (bf16[2,2,512,128]{3,2,1,0:T(8,128)(2,1)S(1)}, bf16[2,2,512,128]{3,2,1,0:T(8,128)(2,1)S(1)}, u32[]{:S(2)}, u32[]{:S(2)}) collective-permute-start(bf16[2,2,512,128]{3,2,1,0:T(8,128)(2,1)S(1)} %collective-permute-done.2), channel_id=1, source_target_pairs={{0,1},{1,0},{2,3},{3,2},{4,5},{5,4},{6,7},{7,6},{8,9},{9,8},{10,11... | collective-permute-start | bytes 1572872 | tf_op jit(solution)/shard_map/ppermute | solution.py:41
  47.1 1.5 %copy-start = (f32[2,2048,128]{2,1,0:T(8,128)}, f32[2,2048,128]{2,1,0:T(8,128)S(1)}, u32[]{:S(2)}) copy-start(f32[2,2048,128]{2,1,0:T(8,128)S(1)} %slice_add_fusion) | copy-start | bytes 6291460
  48.6 27.4 %collective-permute-start = (bf16[2,2,512,128]{3,2,1,0:T(8,128)(2,1)}, bf16[2,2,512,128]{3,2,1,0:T(8,128)(2,1)S(1)}, u32[]{:S(2)}, u32[]{:S(2)}) collective-permute-start(bf16[2,2,512,128]{3,2,1,0:T(8,128)(2,1)} %get-tuple-element.11), channel_id=1, source_target_pairs={{0,4},{4,8},{8,12},{12,16},{16,20},{20,24},{24,28},{28,0},{1,5},{5... | collective-permute-start | bytes 1572872 | tf_op jit(solution)/shard_map/ppermute | solution.py:24
  54.0 23.1 %collective-permute-start.1 = (bf16[2,2,512,128]{3,2,1,0:T(8,128)(2,1)S(1)}, bf16[2,2,512,128]{3,2,1,0:T(8,128)(2,1)S(1)}, u32[]{:S(2)}, u32[]{:S(2)}) collective-permute-start(bf16[2,2,512,128]{3,2,1,0:T(8,128)(2,1)S(1)} %get-tuple-element.10), channel_id=1, source_target_pairs={{4,0},{8,4},{12,8},{16,12},{20,16},{24,20},{28,24},{0,28},{5,1},{9... | collective-permute-start | bytes 1572872 | tf_op jit(solution)/shard_map/ppermute | solution.py:24
  57.4 27.9 %all-to-all-start.2 = ((bf16[4,2,2,128,128]{4,3,2,1,0:T(8,128)(2,1)}), bf16[4,2,2,128,128]{4,3,2,1,0:T(8,128)(2,1)S(1)}, u32[]{:S(2)}, u32[]{:S(2)}) async-start(bf16[4,2,2,128,128]{4,3,2,1,0:T(8,128)(2,1)} %shard_map.69), calls=%async_computation.2 | async-start | bytes 1048576 | tf_op jit(solution)/shard_map/all_to_all | solution.py:276
  76.0 1.1 copy-start.3
  77.1 0.8 copy-start.4
  85.3 23.8 %all-to-all-start.1 = ((bf16[4,2,6,128,128]{4,3,2,1,0:T(8,128)(2,1)}), bf16[4,2,6,128,128]{4,3,2,1,0:T(8,128)(2,1)S(1)}, u32[]{:S(2)}, u32[]{:S(2)}) async-start(bf16[4,2,6,128,128]{4,3,2,1,0:T(8,128)(2,1)} %get-tuple-element.5), calls=%async_computation.1 | async-start | bytes 3145728 | tf_op jit(solution)/shard_map/all_to_all | solution.py:276
  110.0 1.0 copy-start.5
  116.3 1.2 collective-permute-start.4
  117.5 3.6 %collective-permute-start.5 = (f32[8,8]{1,0:T(8,128)S(1)}, f32[8,8]{1,0:T(8,128)S(1)}, u32[]{:S(2)}, u32[]{:S(2)}) collective-permute-start(f32[8,8]{1,0:T(8,128)S(1)} %add.59), channel_id=1, source_target_pairs={{0,2},{1,3},{2,0},{3,1},{4,6},{5,7},{6,4},{7,5},{8,10},{9,11},{10,... | collective-permute-start | bytes 776 | tf_op jit(solution)/shard_map/ppermute | solution.py:233
  121.1 3.6 %collective-permute-start.6 = (f32[8,8]{1,0:T(8,128)S(1)}, f32[8,8]{1,0:T(8,128)S(1)}, u32[]{:S(2)}, u32[]{:S(2)}) collective-permute-start(f32[8,8]{1,0:T(8,128)S(1)} %add.60), channel_id=1, source_target_pairs={{0,4},{4,0},{8,12},{12,8},{16,20},{20,16},{24,28},{28,24},{1,5},{5... | collective-permute-start | bytes 776 | tf_op jit(solution)/shard_map/ppermute | solution.py:233
  124.7 3.6 %collective-permute-start.7 = (f32[8,8]{1,0:T(8,128)S(1)}, f32[8,8]{1,0:T(8,128)S(1)}, u32[]{:S(2)}, u32[]{:S(2)}) collective-permute-start(f32[8,8]{1,0:T(8,128)S(1)} %add.61), channel_id=1, source_target_pairs={{0,8},{4,12},{8,0},{12,4},{16,24},{20,28},{24,16},{28,20},{1,9},{5... | collective-permute-start | bytes 776 | tf_op jit(solution)/shard_map/ppermute | solution.py:233
  128.3 4.5 %collective-permute-start.8 = (f32[8,8]{1,0:T(8,128)S(1)}, f32[8,8]{1,0:T(8,128)S(1)}, u32[]{:S(2)}, u32[]{:S(2)}) collective-permute-start(f32[8,8]{1,0:T(8,128)S(1)} %add.62), channel_id=1, source_target_pairs={{0,16},{4,20},{8,24},{12,28},{16,0},{20,4},{24,8},{28,12},{1,17},{... | collective-permute-start | bytes 776 | tf_op jit(solution)/shard_map/ppermute | solution.py:233

commit v12 on v9

--- a/solution.py
+++ b/solution.py
@@ -208,7 +208,7 @@
 
 def pieces(x):
     out, rest = [], x
-    for _ in range(3):
+    for _ in range(2):
         part = lax.reduce_precision(rest, exponent_bits=8, mantissa_bits=7)
         out.append(part.astype(jnp.bfloat16))
         rest = rest - part
@@ -251,15 +251,18 @@
     hit = slot[:, None, :] == lax.broadcasted_iota(jnp.int32, (fields_dev, slots, rows_dev), 1)
     send_vals = select(hit.astype(jnp.bfloat16), profile)
     send_cols = jnp.sum(jnp.where(hit, offset[:, None, :], 0), axis=2).astype(jnp.float32)
-    send_cols = jnp.pad(send_cols.reshape(fields_dev, count, cap), ((0, 0), (0, 0), (0, col_rows * depth - cap)))
+    col_rows = -(-fields_dev * cap // depth)
+    send_cols = send_cols.reshape(fields_dev, count, cap).transpose(1, 0, 2).reshape(count, fields_dev * cap)
+    send_cols = jnp.pad(send_cols, ((0, 0), (0, col_rows * depth - fields_dev * cap)))
+    vals = send_vals.reshape(fields_dev, count, cap, depth).transpose(1, 0, 2, 3)
     payload = jnp.concatenate(
-        [send_vals.reshape(fields_dev, count, cap, depth), send_cols.reshape(fields_dev, count, col_rows, depth)],
-        axis=2,
+        [vals.reshape(count, fields_dev * cap, depth), send_cols.reshape(count, col_rows, depth)], axis=1
     )
-    got = lax.all_to_all(payload, "space", split_axis=1, concat_axis=1, tiled=True)
-    got_vals = got[:, :, :cap].reshape(fields_dev, slots, depth)
-    got_cols = got[:, :, cap:].reshape(fields_dev, count, col_rows * depth)[:, :, :cap]
-    got_cols = got_cols.reshape(fields_dev, slots).astype(jnp.int32)
+    got = lax.all_to_all(payload, "space", split_axis=0, concat_axis=0, tiled=True)
+    got_vals = got[:, :fields_dev * cap].reshape(count, fields_dev, cap, depth).transpose(1, 0, 2, 3)
+    got_vals = got_vals.reshape(fields_dev, slots, depth)
+    got_cols = got[:, fields_dev * cap:].reshape(count, col_rows * depth)[:, :fields_dev * cap]
+    got_cols = got_cols.reshape(count, fields_dev, cap).transpose(1, 0, 2).reshape(fields_dev, slots).astype(jnp.int32)
 
     place = got_cols[:, None, :] == lax.broadcasted_iota(jnp.int32, (fields_dev, planes * span, slots), 1)
     state = select(place.astype(jnp.bfloat16), got_vals).reshape(fields_dev, planes, span, depth)

time: 134 us -> 129 us (0.963)
  other arithmetic: 8.04 us -> 6 us
  matrix products: 8.3 us -> 6.5 us
  local copies, waits for them, and re-layouts: 7.01 us -> 5.61 us
    dot_general x2, matrix products: 5.21 us -> 3.44 us  [select(): jnp.einsum('fmk,fkd->fmd', onehot, jnp.concatenate(parts, axis=-1), prefe...]
  transfers between devices with their start and end apart: 12 -> 12, of which waited for: 9 -> 9; matrix products, arithmetic and copies ran while one was open for 8% -> 5% of each run, Pallas kernels for 8% -> 8%
where the time goes in v12:
time: 129 us
  waiting for transfers between devices  72.1 us (56%)
  starting transfers between devices  26.6 us (21%)
  Pallas kernels  10.8 us (8%)
  matrix products  6.5 us (5%)
  other arithmetic  6 us (5%)
  local copies, waits for them, and re-layouts  5.61 us (4%)
    ppermute x1, waiting for transfers between devices, halos_shared(): lax.ppermute(jnp.where(odd, initial, last).astype(LINK), ('space', 'batch...  25.9 us
    all_to_all x2, waiting for transfers between devices, spread(): lax.all_to_all(snap, 'batch', split_axis=0, concat_axis=0, tiled=True)  19.2 us
    ppermute x2, waiting for transfers between devices, halos(): return (lax.ppermute(last, axis, up), lax.ppermute(initial, axis, down))  15.1 us
    ppermute x5, waiting for transfers between devices, butterfly(): value = value + lax.ppermute(value, axis, [(i, i ^ step) for i in range(n)])  11.9 us
    pallas_call x1, Pallas kernels, two_steps(): pl.pallas_call(stencil_kernel, grid=(fields,), in_specs=[pl.BlockSpec(mem...  7.41 us
    all_to_all x1, starting transfers between devices, work(): lax.all_to_all(payload, 'space', split_axis=0, concat_axis=0, tiled=True)  7.28 us
    all_to_all x2, starting transfers between devices, spread(): lax.all_to_all(snap, 'batch', split_axis=0, concat_axis=0, tiled=True)  7.22 us
    ppermute x2, starting transfers between devices, halos(): return (lax.ppermute(last, axis, up), lax.ppermute(initial, axis, down))  5.41 us
  transfers between devices with their start and end apart: 12, of which 9 were waited for; matrix products, arithmetic and copies ran while one was open for 5% of the time, Pallas kernels for 8%

profile of v12, /device:TPU:0, one launch (start us, length us, event | category | flops | bytes accessed | tf_op | source)
XLA Modules:
  0.0 128.5 jit_solution(10467276391305799678)
XLA Ops:
  0.6 1.0 reduce-precision_convert_fusion.1
  4.9 1.1 pad_maximum_fusion
  6.0 7.3 %all-to-all-start = ((f32[8,258,128]{2,1,0:T(8,128)}), f32[8,258,128]{2,1,0:T(8,128)S(1)}, u32[]{:S(2)}, u32[]{:S(2)}) async-start(f32[8,258,128]{2,1,0:T(8,128)} %pad_maximum_fusion), calls=%async_computation | async-start | bytes 2162688 | tf_op jit(solution)/shard_map/all_to_all | solution.py:261
  13.4 2.1 %collective-permute-start.2 = (bf16[2,2,512,128]{3,2,1,0:T(8,128)(2,1)S(1)}, bf16[2,2,512,128]{3,2,1,0:T(8,128)(2,1)S(1)}, u32[]{:S(2)}, u32[]{:S(2)}) collective-permute-start(bf16[2,2,512,128]{3,2,1,0:T(8,128)(2,1)S(1)} %fusion.8), channel_id=1, source_target_pairs={{0,4},{1,29},{2,6},{3,31},{4,8},{5,1},{6,10},{7,3},{8,12},{9,5},{1... | collective-permute-start | bytes 1572872 | tf_op jit(solution)/shard_map/ppermute | solution.py:40
  15.5 25.9 %collective-permute-done.2 = bf16[2,2,512,128]{3,2,1,0:T(8,128)(2,1)S(1)} collective-permute-done((bf16[2,2,512,128]{3,2,1,0:T(8,128)(2,1)S(1)}, bf16[2,2,512,128]{3,2,1,0:T(8,128)(2,1)S(1)}, u32[]{:S(2)}, u32[]{:S(2)}) %collective-permute-start.2) | collective-permute-done | bytes 524320 | tf_op jit(solution)/shard_map/ppermute | solution.py:40
  41.7 3.0 %fusion = f32[2,2048,256]{2,1,0:T(8,128)S(1)} fusion(s32[2,1024]{1,0:T(2,128)S(1)} %fusion.26, bf16[2,1024,128]{2,1,0:T(8,128)(2,1)S(1)} %get-tuple-element.13, bf16[2,1024,128]{2,1,0:T(8,128)(2,1)S(1)} %get-tuple-element.12), kind=kOutput, calls=%fused_computation.1 | convolution fusion | flops 2153775104 | bytes 5251072 | tf_op jit(solution)/shard_map/fmk,fkd->fmd/dot_general | solution.py:221
  45.1 1.1 fusion.30
  46.4 5.4 %collective-permute-start = (bf16[2,2,512,128]{3,2,1,0:T(8,128)(2,1)}, bf16[2,2,512,128]{3,2,1,0:T(8,128)(2,1)S(1)}, u32[]{:S(2)}, u32[]{:S(2)}) collective-permute-start(bf16[2,2,512,128]{3,2,1,0:T(8,128)(2,1)} %get-tuple-element.11), channel_id=1, source_target_pairs={{0,4},{4,8},{8,12},{12,16},{16,20},{20,24},{24,28},{28,0},{1,5},{5... | collective-permute-start | bytes 1572872 | tf_op jit(solution)/shard_map/ppermute | solution.py:24
  51.8 3.4 %shard_map.69 = bf16[4,2,2,128,128]{4,3,2,1,0:T(8,128)(2,1)} custom-call(s32[1]{0:T(128)} %bitcast.flag_ref, f32[2,4,512,128]{3,2,1,0:T(8,128)} %bitcast.58, f32[4,512,128]{2,1,0:T(8,128)} %d_ref.3, f32[4,512,128]{2,1,0:T(8,128)} %v_ref.3), custom_call_target="tpu_custom_call" | custom-call | tf_op jit(solution)/shard_map/pallas_call | solution.py:163
  55.2 3.5 %all-to-all-start.2 = ((bf16[4,2,2,128,128]{4,3,2,1,0:T(8,128)(2,1)}), bf16[4,2,2,128,128]{4,3,2,1,0:T(8,128)(2,1)S(1)}, u32[]{:S(2)}, u32[]{:S(2)}) async-start(bf16[4,2,2,128,128]{4,3,2,1,0:T(8,128)(2,1)} %shard_map.69), calls=%async_computation.2 | async-start | bytes 1048576 | tf_op jit(solution)/shard_map/all_to_all | solution.py:279
  58.7 1.1 broadcast_select_fusion
  59.7 14.1 %collective-permute-done.xb_ref = bf16[2,2,512,128]{3,2,1,0:T(8,128)(2,1)S(1)} collective-permute-done((bf16[2,2,512,128]{3,2,1,0:T(8,128)(2,1)}, bf16[2,2,512,128]{3,2,1,0:T(8,128)(2,1)S(1)}, u32[]{:S(2)}, u32[]{:S(2)}) %collective-permute-start) | collective-permute-done | bytes 524320 | tf_op jit(solution)/shard_map/ppermute | solution.py:24
  73.8 1.1 collective-permute-done.1.xa_ref
  75.7 7.4 %shard_map.68 = (f32[2,4,512,128]{3,2,1,0:T(8,128)}, bf16[4,2,6,128,128]{4,3,2,1,0:T(8,128)(2,1)}) custom-call(s32[1]{0:T(128)} %bitcast.flag_ref, f32[2,4,512,128]{3,2,1,0:T(8,128)} %bitcast.59, bf16[2,2,512,128]{3,2,1,0:T(8,128)(2,1)} %copy-done.3, bf16[2,2,512,128]{3,2,1,0:T(8,128)(2,1)} %copy-done.4, f32[4,512,128]{2,1,0:T(8,128)} %d_ref.3, ...), custom_call_target="tpu_custom_call" | custom-call | tf_op jit(solution)/shard_map/pallas_call | solution.py:183
  83.1 3.8 %all-to-all-start.1 = ((bf16[4,2,6,128,128]{4,3,2,1,0:T(8,128)(2,1)}), bf16[4,2,6,128,128]{4,3,2,1,0:T(8,128)(2,1)S(1)}, u32[]{:S(2)}, u32[]{:S(2)}) async-start(bf16[4,2,6,128,128]{4,3,2,1,0:T(8,128)(2,1)} %get-tuple-element.5), calls=%async_computation.1 | async-start | bytes 3145728 | tf_op jit(solution)/shard_map/all_to_all | solution.py:279
  87.8 19.2 %all-to-all-done.1 = bf16[4,2,6,128,128]{4,3,2,1,0:T(8,128)(2,1)S(1)} async-done(((bf16[4,2,6,128,128]{4,3,2,1,0:T(8,128)(2,1)}), bf16[4,2,6,128,128]{4,3,2,1,0:T(8,128)(2,1)S(1)}, u32[]{:S(2)}, u32[]{:S(2)}) %all-to-all-start.1) | async-done | bytes 1572896 | tf_op jit(solution)/shard_map/all_to_all | solution.py:279
  111.4 1.2 collective-permute-done.4
  112.7 3.5 %collective-permute-done.5 = f32[8,8]{1,0:T(8,128)S(1)} collective-permute-done((f32[8,8]{1,0:T(8,128)S(1)}, f32[8,8]{1,0:T(8,128)S(1)}, u32[]{:S(2)}, u32[]{:S(2)}) %collective-permute-start.5) | collective-permute-done | bytes 288 | tf_op jit(solution)/shard_map/ppermute | solution.py:233
  116.2 1.2 collective-permute-start.6
  117.4 2.4 %collective-permute-done.6 = f32[8,8]{1,0:T(8,128)S(1)} collective-permute-done((f32[8,8]{1,0:T(8,128)S(1)}, f32[8,8]{1,0:T(8,128)S(1)}, u32[]{:S(2)}, u32[]{:S(2)}) %collective-permute-start.6) | collective-permute-done | bytes 288 | tf_op jit(solution)/shard_map/ppermute | solution.py:233
  119.8 1.1 collective-permute-start.7
  120.9 2.6 %collective-permute-done.7 = f32[8,8]{1,0:T(8,128)S(1)} collective-permute-done((f32[8,8]{1,0:T(8,128)S(1)}, f32[8,8]{1,0:T(8,128)S(1)}, u32[]{:S(2)}, u32[]{:S(2)}) %collective-permute-start.7) | collective-permute-done | bytes 288 | tf_op jit(solution)/shard_map/ppermute | solution.py:233
  123.4 2.3 %collective-permute-start.8 = (f32[8,8]{1,0:T(8,128)S(1)}, f32[8,8]{1,0:T(8,128)S(1)}, u32[]{:S(2)}, u32[]{:S(2)}) collective-permute-start(f32[8,8]{1,0:T(8,128)S(1)} %add.66), channel_id=1, source_target_pairs={{0,16},{4,20},{8,24},{12,28},{16,0},{20,4},{24,8},{28,12},{1,17},{... | collective-permute-start | bytes 776 | tf_op jit(solution)/shard_map/ppermute | solution.py:233
  125.7 2.2 %collective-permute-done.8 = f32[8,8]{1,0:T(8,128)S(1)} collective-permute-done((f32[8,8]{1,0:T(8,128)S(1)}, f32[8,8]{1,0:T(8,128)S(1)}, u32[]{:S(2)}, u32[]{:S(2)}) %collective-permute-start.8) | collective-permute-done | bytes 288 | tf_op jit(solution)/shard_map/ppermute | solution.py:233
  (58 shorter events, 11.0 us)
Async XLA Ops:
  3.8 0.7 copy-start.6
  4.9 8.4 %copy-start.1 = (f32[4,512,128]{2,1,0:T(8,128)S(1)}, f32[4,512,128]{2,1,0:T(8,128)}, u32[]{:S(2)}) copy-start(f32[4,512,128]{2,1,0:T(8,128)} %d_ref.3) | copy-start | bytes 3145732
  4.9 8.4 %copy-start.2 = (f32[4,512,128]{2,1,0:T(8,128)S(1)}, f32[4,512,128]{2,1,0:T(8,128)}, u32[]{:S(2)}) copy-start(f32[4,512,128]{2,1,0:T(8,128)} %v_ref.3) | copy-start | bytes 3145732
  6.0 35.4 %all-to-all-start = ((f32[8,258,128]{2,1,0:T(8,128)}), f32[8,258,128]{2,1,0:T(8,128)S(1)}, u32[]{:S(2)}, u32[]{:S(2)}) async-start(f32[8,258,128]{2,1,0:T(8,128)} %pad_maximum_fusion), calls=%async_computation | async-start | bytes 2162688 | tf_op jit(solution)/shard_map/all_to_all | solution.py:261
  13.4 27.9 %collective-permute-start.2 = (bf16[2,2,512,128]{3,2,1,0:T(8,128)(2,1)S(1)}, bf16[2,2,512,128]{3,2,1,0:T(8,128)(2,1)S(1)}, u32[]{:S(2)}, u32[]{:S(2)}) collective-permute-start(bf16[2,2,512,128]{3,2,1,0:T(8,128)(2,1)S(1)} %fusion.8), channel_id=1, source_target_pairs={{0,4},{1,29},{2,6},{3,31},{4,8},{5,1},{6,10},{7,3},{8,12},{9,5},{1... | collective-permute-start | bytes 1572872 | tf_op jit(solution)/shard_map/ppermute | solution.py:40
  41.3 17.3 %collective-permute-start.3 = (bf16[2,2,512,128]{3,2,1,0:T(8,128)(2,1)S(1)}, bf16[2,2,512,128]{3,2,1,0:T(8,128)(2,1)S(1)}, u32[]{:S(2)}, u32[]{:S(2)}) collective-permute-start(bf16[2,2,512,128]{3,2,1,0:T(8,128)(2,1)S(1)} %collective-permute-done.2), channel_id=1, source_target_pairs={{0,1},{1,0},{2,3},{3,2},{4,5},{5,4},{6,7},{7,6},{8,9},{9,8},{10,11... | collective-permute-start | bytes 1572872 | tf_op jit(solution)/shard_map/ppermute | solution.py:41
  44.9 1.5 %copy-start = (f32[2,2048,128]{2,1,0:T(8,128)}, f32[2,2048,128]{2,1,0:T(8,128)S(1)}, u32[]{:S(2)}) copy-start(f32[2,2048,128]{2,1,0:T(8,128)S(1)} %slice_add_fusion) | copy-start | bytes 6291460
  46.4 27.4 %collective-permute-start = (bf16[2,2,512,128]{3,2,1,0:T(8,128)(2,1)}, bf16[2,2,512,128]{3,2,1,0:T(8,128)(2,1)S(1)}, u32[]{:S(2)}, u32[]{:S(2)}) collective-permute-start(bf16[2,2,512,128]{3,2,1,0:T(8,128)(2,1)} %get-tuple-element.11), channel_id=1, source_target_pairs={{0,4},{4,8},{8,12},{12,16},{16,20},{20,24},{24,28},{28,0},{1,5},{5... | collective-permute-start | bytes 1572872 | tf_op jit(solution)/shard_map/ppermute | solution.py:24
  51.8 23.1 %collective-permute-start.1 = (bf16[2,2,512,128]{3,2,1,0:T(8,128)(2,1)S(1)}, bf16[2,2,512,128]{3,2,1,0:T(8,128)(2,1)S(1)}, u32[]{:S(2)}, u32[]{:S(2)}) collective-permute-start(bf16[2,2,512,128]{3,2,1,0:T(8,128)(2,1)S(1)} %get-tuple-element.10), channel_id=1, source_target_pairs={{4,0},{8,4},{12,8},{16,12},{20,16},{24,20},{28,24},{0,28},{5,1},{9... | collective-permute-start | bytes 1572872 | tf_op jit(solution)/shard_map/ppermute | solution.py:24
  55.2 27.9 %all-to-all-start.2 = ((bf16[4,2,2,128,128]{4,3,2,1,0:T(8,128)(2,1)}), bf16[4,2,2,128,128]{4,3,2,1,0:T(8,128)(2,1)S(1)}, u32[]{:S(2)}, u32[]{:S(2)}) async-start(bf16[4,2,2,128,128]{4,3,2,1,0:T(8,128)(2,1)} %shard_map.69), calls=%async_computation.2 | async-start | bytes 1048576 | tf_op jit(solution)/shard_map/all_to_all | solution.py:279
  73.8 1.1 copy-start.3
  74.9 0.8 copy-start.4
  83.1 23.9 %all-to-all-start.1 = ((bf16[4,2,6,128,128]{4,3,2,1,0:T(8,128)(2,1)}), bf16[4,2,6,128,128]{4,3,2,1,0:T(8,128)(2,1)S(1)}, u32[]{:S(2)}, u32[]{:S(2)}) async-start(bf16[4,2,6,128,128]{4,3,2,1,0:T(8,128)(2,1)} %get-tuple-element.5), calls=%async_computation.1 | async-start | bytes 3145728 | tf_op jit(solution)/shard_map/all_to_all | solution.py:279
  109.5 1.0 copy-start.5
  111.4 1.2 collective-permute-start.4
  112.6 3.6 %collective-permute-start.5 = (f32[8,8]{1,0:T(8,128)S(1)}, f32[8,8]{1,0:T(8,128)S(1)}, u32[]{:S(2)}, u32[]{:S(2)}) collective-permute-start(f32[8,8]{1,0:T(8,128)S(1)} %add.63), channel_id=1, source_target_pairs={{0,2},{1,3},{2,0},{3,1},{4,6},{5,7},{6,4},{7,5},{8,10},{9,11},{10,... | collective-permute-start | bytes 776 | tf_op jit(solution)/shard_map/ppermute | solution.py:233
  116.2 3.6 %collective-permute-start.6 = (f32[8,8]{1,0:T(8,128)S(1)}, f32[8,8]{1,0:T(8,128)S(1)}, u32[]{:S(2)}, u32[]{:S(2)}) collective-permute-start(f32[8,8]{1,0:T(8,128)S(1)} %add.64), channel_id=1, source_target_pairs={{0,4},{4,0},{8,12},{12,8},{16,20},{20,16},{24,28},{28,24},{1,5},{5... | collective-permute-start | bytes 776 | tf_op jit(solution)/shard_map/ppermute | solution.py:233
  119.8 3.6 %collective-permute-start.7 = (f32[8,8]{1,0:T(8,128)S(1)}, f32[8,8]{1,0:T(8,128)S(1)}, u32[]{:S(2)}, u32[]{:S(2)}) collective-permute-start(f32[8,8]{1,0:T(8,128)S(1)} %add.65), channel_id=1, source_target_pairs={{0,8},{4,12},{8,0},{12,4},{16,24},{20,28},{24,16},{28,20},{1,9},{5... | collective-permute-start | bytes 776 | tf_op jit(solution)/shard_map/ppermute | solution.py:233
  123.4 4.5 %collective-permute-start.8 = (f32[8,8]{1,0:T(8,128)S(1)}, f32[8,8]{1,0:T(8,128)S(1)}, u32[]{:S(2)}, u32[]{:S(2)}) collective-permute-start(f32[8,8]{1,0:T(8,128)S(1)} %add.66), channel_id=1, source_target_pairs={{0,16},{4,20},{8,24},{12,28},{16,0},{20,4},{24,8},{28,12},{1,17},{... | collective-permute-start | bytes 776 | tf_op jit(solution)/shard_map/ppermute | solution.py:233

commit v13 on v9

--- a/solution.py
+++ b/solution.py
@@ -208,7 +208,7 @@
 
 def pieces(x):
     out, rest = [], x
-    for _ in range(3):
+    for _ in range(2):
         part = lax.reduce_precision(rest, exponent_bits=8, mantissa_bits=7)
         out.append(part.astype(jnp.bfloat16))
         rest = rest - part
@@ -276,7 +276,8 @@
         mixed = lax.all_to_all(snap, "batch", split_axis=0, concat_axis=0, tiled=True)
         return mixed.reshape(mixed.shape[0] * mixed.shape[1], mixed.shape[2], -1)
 
-    inner, late = spread(inner), spread(late)
+    inner = spread(inner)
+    late = spread(late)
     snaps = [(late[:, 0:2], inner), (late[:, 2:4], late[:, 4:])]
     rows = []
     for sensed in snaps:

time: 134 us -> 131 us (0.978)
  matrix products: 8.3 us -> 6.5 us
    dot_general x2, matrix products: 5.21 us -> 3.43 us  [select(): jnp.einsum('fmk,fkd->fmd', onehot, jnp.concatenate(parts, axis=-1), prefe...]
  transfers between devices with their start and end apart: 12 -> 12, of which waited for: 9 -> 9; matrix products, arithmetic and copies ran while one was open for 8% -> 7% of each run, Pallas kernels for 8% -> 8%
where the time goes in v13:
time: 131 us
  waiting for transfers between devices  71.3 us (54%)
  starting transfers between devices  26.8 us (20%)
  Pallas kernels  10.8 us (8%)
  local copies, waits for them, and re-layouts  7.13 us (5%)
  other arithmetic  7.12 us (5%)
  matrix products  6.5 us (5%)
    ppermute x1, waiting for transfers between devices, halos_shared(): lax.ppermute(jnp.where(odd, initial, last).astype(LINK), ('space', 'batch...  25.5 us
    all_to_all x2, waiting for transfers between devices, spread(): lax.all_to_all(snap, 'batch', split_axis=0, concat_axis=0, tiled=True)  19.2 us
    ppermute x2, waiting for transfers between devices, halos(): return (lax.ppermute(last, axis, up), lax.ppermute(initial, axis, down))  15 us
    ppermute x5, waiting for transfers between devices, butterfly(): value = value + lax.ppermute(value, axis, [(i, i ^ step) for i in range(n)])  11.6 us
    pallas_call x1, Pallas kernels, two_steps(): pl.pallas_call(stencil_kernel, grid=(fields,), in_specs=[pl.BlockSpec(mem...  7.41 us
    all_to_all x1, starting transfers between devices, work(): lax.all_to_all(payload, 'space', split_axis=1, concat_axis=1, tiled=True)  7.28 us
    all_to_all x2, starting transfers between devices, spread(): lax.all_to_all(snap, 'batch', split_axis=0, concat_axis=0, tiled=True)  7.23 us
    ppermute x2, starting transfers between devices, halos(): return (lax.ppermute(last, axis, up), lax.ppermute(initial, axis, down))  5.37 us
  transfers between devices with their start and end apart: 12, of which 9 were waited for; matrix products, arithmetic and copies ran while one was open for 7% of the time, Pallas kernels for 8%

profile of v13, /device:TPU:0, one launch (start us, length us, event | category | flops | bytes accessed | tf_op | source)
XLA Modules:
  0.0 130.6 jit_solution(1417805387829949864)
XLA Ops:
  5.2 1.5 %pad_maximum_fusion = f32[2,8,129,128]{3,0,2,1:T(2,128)} fusion(f32[2,8,1,128]{3,0,2,1:T(2,128)S(1)} %convert_bitcast_fusion, f32[2,8,128,128]{3,0,2,1:T(2,128)S(1)} %copy.17), kind=kLoop, calls=%fused_computation.20 | loop fusion | flops 264192 | bytes 2113536 | tf_op jit(solution)/shard_map/concatenate | solution.py:255
  6.7 7.3 %all-to-all-start = ((f32[2,8,129,128]{3,0,2,1:T(2,128)}), f32[2,8,129,128]{3,0,2,1:T(2,128)}, u32[]{:S(2)}, u32[]{:S(2)}) async-start(f32[2,8,129,128]{3,0,2,1:T(2,128)} %pad_maximum_fusion), calls=%async_computation | async-start | bytes 2113536 | tf_op jit(solution)/shard_map/all_to_all | solution.py:259
  14.1 2.1 %collective-permute-start.2 = (bf16[2,2,512,128]{3,2,1,0:T(8,128)(2,1)S(1)}, bf16[2,2,512,128]{3,2,1,0:T(8,128)(2,1)S(1)}, u32[]{:S(2)}, u32[]{:S(2)}) collective-permute-start(bf16[2,2,512,128]{3,2,1,0:T(8,128)(2,1)S(1)} %fusion.8), channel_id=1, source_target_pairs={{0,4},{1,29},{2,6},{3,31},{4,8},{5,1},{6,10},{7,3},{8,12},{9,5},{1... | collective-permute-start | bytes 1572872 | tf_op jit(solution)/shard_map/ppermute | solution.py:40
  16.2 25.5 %collective-permute-done.2 = bf16[2,2,512,128]{3,2,1,0:T(8,128)(2,1)S(1)} collective-permute-done((bf16[2,2,512,128]{3,2,1,0:T(8,128)(2,1)S(1)}, bf16[2,2,512,128]{3,2,1,0:T(8,128)(2,1)S(1)}, u32[]{:S(2)}, u32[]{:S(2)}) %collective-permute-start.2) | collective-permute-done | bytes 524320 | tf_op jit(solution)/shard_map/ppermute | solution.py:40
  41.6 1.3 slice.96
  43.9 3.0 %fusion = f32[2,2048,256]{2,1,0:T(8,128)S(1)} fusion(s32[2,1024]{1,0:T(2,128)S(1)} %fusion.26, bf16[2,1024,128]{2,1,0:T(8,128)(2,1)S(1)} %get-tuple-element.13, bf16[2,1024,128]{2,1,0:T(8,128)(2,1)S(1)} %get-tuple-element.12), kind=kOutput, calls=%fused_computation.1 | convolution fusion | flops 2153775104 | bytes 5251072 | tf_op jit(solution)/shard_map/fmk,fkd->fmd/dot_general | solution.py:221
  47.3 1.1 fusion.30
  48.6 5.4 %collective-permute-start = (bf16[2,2,512,128]{3,2,1,0:T(8,128)(2,1)}, bf16[2,2,512,128]{3,2,1,0:T(8,128)(2,1)S(1)}, u32[]{:S(2)}, u32[]{:S(2)}) collective-permute-start(bf16[2,2,512,128]{3,2,1,0:T(8,128)(2,1)} %get-tuple-element.11), channel_id=1, source_target_pairs={{0,4},{4,8},{8,12},{12,16},{16,20},{20,24},{24,28},{28,0},{1,5},{5... | collective-permute-start | bytes 1572872 | tf_op jit(solution)/shard_map/ppermute | solution.py:24
  54.0 3.4 %shard_map.69 = bf16[4,2,2,128,128]{4,3,2,1,0:T(8,128)(2,1)} custom-call(s32[1]{0:T(128)} %bitcast.flag_ref, f32[2,4,512,128]{3,2,1,0:T(8,128)} %bitcast.48, f32[4,512,128]{2,1,0:T(8,128)} %d_ref.3, f32[4,512,128]{2,1,0:T(8,128)} %v_ref.3), custom_call_target="tpu_custom_call" | custom-call | tf_op jit(solution)/shard_map/pallas_call | solution.py:163
  57.4 3.6 %all-to-all-start.2 = ((bf16[4,2,2,128,128]{4,3,2,1,0:T(8,128)(2,1)}), bf16[4,2,2,128,128]{4,3,2,1,0:T(8,128)(2,1)S(1)}, u32[]{:S(2)}, u32[]{:S(2)}) async-start(bf16[4,2,2,128,128]{4,3,2,1,0:T(8,128)(2,1)} %shard_map.69), calls=%async_computation.2 | async-start | bytes 1048576 | tf_op jit(solution)/shard_map/all_to_all | solution.py:276
  61.1 1.1 broadcast_select_fusion
  62.1 13.9 %collective-permute-done.xb_ref = bf16[2,2,512,128]{3,2,1,0:T(8,128)(2,1)S(1)} collective-permute-done((bf16[2,2,512,128]{3,2,1,0:T(8,128)(2,1)}, bf16[2,2,512,128]{3,2,1,0:T(8,128)(2,1)S(1)}, u32[]{:S(2)}, u32[]{:S(2)}) %collective-permute-start) | collective-permute-done | bytes 524320 | tf_op jit(solution)/shard_map/ppermute | solution.py:24
  76.0 1.1 collective-permute-done.1.xa_ref
  77.9 7.4 %shard_map.68 = (f32[2,4,512,128]{3,2,1,0:T(8,128)}, bf16[4,2,6,128,128]{4,3,2,1,0:T(8,128)(2,1)}) custom-call(s32[1]{0:T(128)} %bitcast.flag_ref, f32[2,4,512,128]{3,2,1,0:T(8,128)} %bitcast.49, bf16[2,2,512,128]{3,2,1,0:T(8,128)(2,1)} %copy-done.3, bf16[2,2,512,128]{3,2,1,0:T(8,128)(2,1)} %copy-done.4, f32[4,512,128]{2,1,0:T(8,128)} %d_ref.3, ...), custom_call_target="tpu_custom_call" | custom-call | tf_op jit(solution)/shard_map/pallas_call | solution.py:183
  85.3 3.6 %all-to-all-start.1 = ((bf16[4,2,6,128,128]{4,3,2,1,0:T(8,128)(2,1)}), bf16[4,2,6,128,128]{4,3,2,1,0:T(8,128)(2,1)S(1)}, u32[]{:S(2)}, u32[]{:S(2)}) async-start(bf16[4,2,6,128,128]{4,3,2,1,0:T(8,128)(2,1)} %get-tuple-element.5), calls=%async_computation.1 | async-start | bytes 3145728 | tf_op jit(solution)/shard_map/all_to_all | solution.py:276
  89.8 19.2 %all-to-all-done.1 = bf16[4,2,6,128,128]{4,3,2,1,0:T(8,128)(2,1)S(1)} async-done(((bf16[4,2,6,128,128]{4,3,2,1,0:T(8,128)(2,1)}), bf16[4,2,6,128,128]{4,3,2,1,0:T(8,128)(2,1)S(1)}, u32[]{:S(2)}, u32[]{:S(2)}) %all-to-all-start.1) | async-done | bytes 1572896 | tf_op jit(solution)/shard_map/all_to_all | solution.py:276
  113.5 1.2 collective-permute-done.4
  114.9 3.4 %collective-permute-done.5 = f32[8,8]{1,0:T(8,128)S(1)} collective-permute-done((f32[8,8]{1,0:T(8,128)S(1)}, f32[8,8]{1,0:T(8,128)S(1)}, u32[]{:S(2)}, u32[]{:S(2)}) %collective-permute-start.5) | collective-permute-done | bytes 288 | tf_op jit(solution)/shard_map/ppermute | solution.py:233
  118.3 1.3 %collective-permute-start.6 = (f32[8,8]{1,0:T(8,128)S(1)}, f32[8,8]{1,0:T(8,128)S(1)}, u32[]{:S(2)}, u32[]{:S(2)}) collective-permute-start(f32[8,8]{1,0:T(8,128)S(1)} %add.64), channel_id=1, source_target_pairs={{0,4},{4,0},{8,12},{12,8},{16,20},{20,16},{24,28},{28,24},{1,5},{5... | collective-permute-start | bytes 776 | tf_op jit(solution)/shard_map/ppermute | solution.py:233
  119.6 2.3 %collective-permute-done.6 = f32[8,8]{1,0:T(8,128)S(1)} collective-permute-done((f32[8,8]{1,0:T(8,128)S(1)}, f32[8,8]{1,0:T(8,128)S(1)}, u32[]{:S(2)}, u32[]{:S(2)}) %collective-permute-start.6) | collective-permute-done | bytes 288 | tf_op jit(solution)/shard_map/ppermute | solution.py:233
  121.9 1.0 collective-permute-start.7
  122.9 2.6 %collective-permute-done.7 = f32[8,8]{1,0:T(8,128)S(1)} collective-permute-done((f32[8,8]{1,0:T(8,128)S(1)}, f32[8,8]{1,0:T(8,128)S(1)}, u32[]{:S(2)}, u32[]{:S(2)}) %collective-permute-start.7) | collective-permute-done | bytes 288 | tf_op jit(solution)/shard_map/ppermute | solution.py:233
  125.5 2.3 %collective-permute-start.8 = (f32[8,8]{1,0:T(8,128)S(1)}, f32[8,8]{1,0:T(8,128)S(1)}, u32[]{:S(2)}, u32[]{:S(2)}) collective-permute-start(f32[8,8]{1,0:T(8,128)S(1)} %add.66), channel_id=1, source_target_pairs={{0,16},{4,20},{8,24},{12,28},{16,0},{20,4},{24,8},{28,12},{1,17},{... | collective-permute-start | bytes 776 | tf_op jit(solution)/shard_map/ppermute | solution.py:233
  127.8 2.2 %collective-permute-done.8 = f32[8,8]{1,0:T(8,128)S(1)} collective-permute-done((f32[8,8]{1,0:T(8,128)S(1)}, f32[8,8]{1,0:T(8,128)S(1)}, u32[]{:S(2)}, u32[]{:S(2)}) %collective-permute-start.8) | collective-permute-done | bytes 288 | tf_op jit(solution)/shard_map/ppermute | solution.py:233
  (58 shorter events, 13.1 us)
Async XLA Ops:
  3.8 0.9 copy-start.6
  5.2 8.8 %copy-start.1 = (f32[4,512,128]{2,1,0:T(8,128)S(1)}, f32[4,512,128]{2,1,0:T(8,128)}, u32[]{:S(2)}) copy-start(f32[4,512,128]{2,1,0:T(8,128)} %d_ref.3) | copy-start | bytes 3145732
  5.2 8.8 %copy-start.2 = (f32[4,512,128]{2,1,0:T(8,128)S(1)}, f32[4,512,128]{2,1,0:T(8,128)}, u32[]{:S(2)}) copy-start(f32[4,512,128]{2,1,0:T(8,128)} %v_ref.3) | copy-start | bytes 3145732
  6.7 35.0 %all-to-all-start = ((f32[2,8,129,128]{3,0,2,1:T(2,128)}), f32[2,8,129,128]{3,0,2,1:T(2,128)}, u32[]{:S(2)}, u32[]{:S(2)}) async-start(f32[2,8,129,128]{3,0,2,1:T(2,128)} %pad_maximum_fusion), calls=%async_computation | async-start | bytes 2113536 | tf_op jit(solution)/shard_map/all_to_all | solution.py:259
  14.1 27.5 %collective-permute-start.2 = (bf16[2,2,512,128]{3,2,1,0:T(8,128)(2,1)S(1)}, bf16[2,2,512,128]{3,2,1,0:T(8,128)(2,1)S(1)}, u32[]{:S(2)}, u32[]{:S(2)}) collective-permute-start(bf16[2,2,512,128]{3,2,1,0:T(8,128)(2,1)S(1)} %fusion.8), channel_id=1, source_target_pairs={{0,4},{1,29},{2,6},{3,31},{4,8},{5,1},{6,10},{7,3},{8,12},{9,5},{1... | collective-permute-start | bytes 1572872 | tf_op jit(solution)/shard_map/ppermute | solution.py:40
  41.6 19.4 %collective-permute-start.3 = (bf16[2,2,512,128]{3,2,1,0:T(8,128)(2,1)S(1)}, bf16[2,2,512,128]{3,2,1,0:T(8,128)(2,1)S(1)}, u32[]{:S(2)}, u32[]{:S(2)}) collective-permute-start(bf16[2,2,512,128]{3,2,1,0:T(8,128)(2,1)S(1)} %collective-permute-done.2), channel_id=1, source_target_pairs={{0,1},{1,0},{2,3},{3,2},{4,5},{5,4},{6,7},{7,6},{8,9},{9,8},{10,11... | collective-permute-start | bytes 1572872 | tf_op jit(solution)/shard_map/ppermute | solution.py:41
  47.1 1.5 %copy-start = (f32[2,2048,128]{2,1,0:T(8,128)}, f32[2,2048,128]{2,1,0:T(8,128)S(1)}, u32[]{:S(2)}) copy-start(f32[2,2048,128]{2,1,0:T(8,128)S(1)} %slice_add_fusion) | copy-start | bytes 6291460
  48.6 27.4 %collective-permute-start = (bf16[2,2,512,128]{3,2,1,0:T(8,128)(2,1)}, bf16[2,2,512,128]{3,2,1,0:T(8,128)(2,1)S(1)}, u32[]{:S(2)}, u32[]{:S(2)}) collective-permute-start(bf16[2,2,512,128]{3,2,1,0:T(8,128)(2,1)} %get-tuple-element.11), channel_id=1, source_target_pairs={{0,4},{4,8},{8,12},{12,16},{16,20},{20,24},{24,28},{28,0},{1,5},{5... | collective-permute-start | bytes 1572872 | tf_op jit(solution)/shard_map/ppermute | solution.py:24
  54.0 23.1 %collective-permute-start.1 = (bf16[2,2,512,128]{3,2,1,0:T(8,128)(2,1)S(1)}, bf16[2,2,512,128]{3,2,1,0:T(8,128)(2,1)S(1)}, u32[]{:S(2)}, u32[]{:S(2)}) collective-permute-start(bf16[2,2,512,128]{3,2,1,0:T(8,128)(2,1)S(1)} %get-tuple-element.10), channel_id=1, source_target_pairs={{4,0},{8,4},{12,8},{16,12},{20,16},{24,20},{28,24},{0,28},{5,1},{9... | collective-permute-start | bytes 1572872 | tf_op jit(solution)/shard_map/ppermute | solution.py:24
  57.4 27.9 %all-to-all-start.2 = ((bf16[4,2,2,128,128]{4,3,2,1,0:T(8,128)(2,1)}), bf16[4,2,2,128,128]{4,3,2,1,0:T(8,128)(2,1)S(1)}, u32[]{:S(2)}, u32[]{:S(2)}) async-start(bf16[4,2,2,128,128]{4,3,2,1,0:T(8,128)(2,1)} %shard_map.69), calls=%async_computation.2 | async-start | bytes 1048576 | tf_op jit(solution)/shard_map/all_to_all | solution.py:276
  76.0 1.1 copy-start.3
  77.1 0.8 copy-start.4
  85.3 23.8 %all-to-all-start.1 = ((bf16[4,2,6,128,128]{4,3,2,1,0:T(8,128)(2,1)}), bf16[4,2,6,128,128]{4,3,2,1,0:T(8,128)(2,1)S(1)}, u32[]{:S(2)}, u32[]{:S(2)}) async-start(bf16[4,2,6,128,128]{4,3,2,1,0:T(8,128)(2,1)} %get-tuple-element.5), calls=%async_computation.1 | async-start | bytes 3145728 | tf_op jit(solution)/shard_map/all_to_all | solution.py:276
  111.6 1.0 copy-start.5
  113.5 1.2 collective-permute-start.4
  114.7 3.6 %collective-permute-start.5 = (f32[8,8]{1,0:T(8,128)S(1)}, f32[8,8]{1,0:T(8,128)S(1)}, u32[]{:S(2)}, u32[]{:S(2)}) collective-permute-start(f32[8,8]{1,0:T(8,128)S(1)} %add.63), channel_id=1, source_target_pairs={{0,2},{1,3},{2,0},{3,1},{4,6},{5,7},{6,4},{7,5},{8,10},{9,11},{10,... | collective-permute-start | bytes 776 | tf_op jit(solution)/shard_map/ppermute | solution.py:233
  118.3 3.6 %collective-permute-start.6 = (f32[8,8]{1,0:T(8,128)S(1)}, f32[8,8]{1,0:T(8,128)S(1)}, u32[]{:S(2)}, u32[]{:S(2)}) collective-permute-start(f32[8,8]{1,0:T(8,128)S(1)} %add.64), channel_id=1, source_target_pairs={{0,4},{4,0},{8,12},{12,8},{16,20},{20,16},{24,28},{28,24},{1,5},{5... | collective-permute-start | bytes 776 | tf_op jit(solution)/shard_map/ppermute | solution.py:233
  121.9 3.6 %collective-permute-start.7 = (f32[8,8]{1,0:T(8,128)S(1)}, f32[8,8]{1,0:T(8,128)S(1)}, u32[]{:S(2)}, u32[]{:S(2)}) collective-permute-start(f32[8,8]{1,0:T(8,128)S(1)} %add.65), channel_id=1, source_target_pairs={{0,8},{4,12},{8,0},{12,4},{16,24},{20,28},{24,16},{28,20},{1,9},{5... | collective-permute-start | bytes 776 | tf_op jit(solution)/shard_map/ppermute | solution.py:233
  125.5 4.5 %collective-permute-start.8 = (f32[8,8]{1,0:T(8,128)S(1)}, f32[8,8]{1,0:T(8,128)S(1)}, u32[]{:S(2)}, u32[]{:S(2)}) collective-permute-start(f32[8,8]{1,0:T(8,128)S(1)} %add.66), channel_id=1, source_target_pairs={{0,16},{4,20},{8,24},{12,28},{16,0},{20,4},{24,8},{28,12},{1,17},{... | collective-permute-start | bytes 776 | tf_op jit(solution)/shard_map/ppermute | solution.py:233
